TPU v7x, 256 devices: a whole 4x4x8 slice. The times are simulated.
256 devices in a mesh: gx: 32 (over z, y_hi, core), gy: 8 (over y_lo, x).
Axes of the slice: x: 4, y: 4 (y_hi: 2, y_lo: 2; y = y_hi * 2 + y_lo), z: 8, core: 2. Of those that a mesh axis runs over, the one named last changes fastest.
Arguments:
- noisy: float32 [32, 512, 4096], P(None, 'gx', 'gy'), may hold values from -6 to 6
- weight: float32 [32, 512, 4096], P(None, 'gx', 'gy'), may hold values from 0.05 to 1
Outputs:
- denoised: float32 [32, 512, 4096], P(None, 'gx', 'gy')
All inputs are finite; a program needn't handle non-finite values.
Results may differ from a plain program's by a relative error of at most 0.00002.
Values sent between devices are 32-bit elements; how exact they have to be, the bound alone decides.
No kernel may reach another device: no remote copies, remote signals or barrier semaphores. Data moves between devices by JAX's collectives and lax.ppermute only.
A program may use at most 192 MiB of HBM per device.

v0:
```python
import jax
import jax.numpy as jnp
from jax import lax
from jax.sharding import PartitionSpec as P

ITERS = 8


dual_step = 0.28
primal_step = 0.28
fidelity = 1.0


def from_behind(value, axis, steps):
    count = lax.axis_size(axis)
    leading, last = (max(0, -steps), min(count, count - steps))
    return lax.ppermute(value, axis, [(source, source + steps) for source in range(leading, last)])


def along_z(field):
    edge = jnp.zeros_like(field[:1])
    return jnp.concatenate([field[1:] - field[:-1], edge], 0)


def back_z(dual):
    edge = jnp.zeros_like(dual[:1])
    return dual - jnp.concatenate([edge, dual[:-1]], 0)


def project(dual_x, dual_y, dual_z, weight):
    length = jnp.sqrt(dual_x * dual_x + dual_y * dual_y + dual_z * dual_z)
    factor = jnp.maximum(1.0, length / weight)
    return (dual_x / factor, dual_y / factor, dual_z / factor)


def per_device(noisy, weight):
    planes, rows_x, rows_y = noisy.shape
    total_x = rows_x * lax.axis_size("gx")
    total_y = rows_y * lax.axis_size("gy")
    start_x = lax.axis_index("gx") * rows_x
    start_y = lax.axis_index("gy") * rows_y
    primal = noisy
    extrapolated = noisy
    last_x = (start_x + jnp.arange(rows_x, dtype=jnp.int32) == total_x - 1)[None, :, None]
    last_y = (start_y + jnp.arange(rows_y, dtype=jnp.int32) == total_y - 1)[None, None, :]
    dual_x = jnp.zeros_like(noisy)
    dual_y = jnp.zeros_like(noisy)
    dual_z = jnp.zeros_like(noisy)
    for iteration in range(ITERS):
        next_x = from_behind(extrapolated[:, :1, :], "gx", -1)
        next_y = from_behind(extrapolated[:, :, :1], "gy", -1)
        joined_x = jnp.concatenate([extrapolated, next_x], 1)
        joined_y = jnp.concatenate([extrapolated, next_y], 2)
        slope_x = jnp.where(last_x, 0.0, joined_x[:, 1:, :] - joined_x[:, :-1, :])
        slope_y = jnp.where(last_y, 0.0, joined_y[:, :, 1:] - joined_y[:, :, :-1])
        dual_x = dual_x + dual_step * slope_x
        dual_y = dual_y + dual_step * slope_y
        dual_z = dual_z + dual_step * along_z(extrapolated)
        dual_x, dual_y, dual_z = project(dual_x, dual_y, dual_z, weight)
        prior_x = from_behind(dual_x[:, -1:, :], "gx", 1)
        prior_y = from_behind(dual_y[:, :, -1:], "gy", 1)
        diverge_x = dual_x - jnp.concatenate([prior_x, dual_x[:, :-1, :]], 1)
        diverge_y = dual_y - jnp.concatenate([prior_y, dual_y[:, :, :-1]], 2)
        divergence = diverge_x + diverge_y + back_z(dual_z)
        updated = (primal + primal_step * divergence + primal_step * fidelity * noisy) / (
            1.0 + primal_step * fidelity
        )
        extrapolated = 2.0 * updated - primal
        primal = updated
    return primal


def solution(mesh):
    placed = (P(None, "gx", "gy"), P(None, "gx", "gy"))
    return jax.shard_map(
        per_device, mesh=mesh, in_specs=placed, out_specs=P(None, "gx", "gy"), check_vma=False
    )
```

profile of v0, /device:TPU:233, one launch (start us, length us, event | category | flops | bytes accessed | tf_op | source)
XLA Modules:
  0.0 255.3 jit_solution(6041596947101246742)
XLA Ops:
  1.1 2.6 %collective-permute-start = (f32[32,1,512]{2,1,0:T(1,128)S(1)}, f32[32,1,512]{2,1,0:T(1,128)S(1)}, u32[]{:S(2)}, u32[]{:S(2)}) collective-permute-start(f32[32,1,512]{2,1,0:T(1,128)S(1)} %slice.264), channel_id=1, source_target_pairs={{8,0},{16,8},{24,16},{32,24},{40,32},{48,40},{56,48},{64,56},{72,6... | collective-permute-start | bytes 196616 | tf_op jit(solution)/shard_map/ppermute | solution.py:17
  3.7 1.7 slice.266
  5.3 4.3 %collective-permute-start.1 = (f32[32,16,1]{2,1,0:T(8,128)}, f32[32,16,1]{2,1,0:T(8,128)S(1)}, u32[]{:S(2)}, u32[]{:S(2)}) collective-permute-start(f32[32,16,1]{2,1,0:T(8,128)} %slice.266), channel_id=1, source_target_pairs={{1,0},{2,1},{3,2},{4,3},{5,4},{6,5},{7,6},{9,8},{10,9},{11,10},{12... | collective-permute-start | bytes 6152 | tf_op jit(solution)/shard_map/ppermute | solution.py:17
  9.6 1.9 slice_subtract_fusion.7
  11.6 1.7 collective-permute-done.1
  15.0 7.3 %collective-permute-start.2 = (f32[32,1,512]{2,1,0:T(1,128)S(1)}, f32[32,1,512]{2,1,0:T(1,128)S(1)}, u32[]{:S(2)}, u32[]{:S(2)}) collective-permute-start(f32[32,1,512]{2,1,0:T(1,128)S(1)} %slice.352), channel_id=1, source_target_pairs={{0,8},{8,16},{16,24},{24,32},{32,40},{40,48},{48,56},{56,64},{64,7... | collective-permute-start | bytes 196616 | tf_op jit(solution)/shard_map/ppermute | solution.py:17
  22.4 2.6 %collective-permute-start.3 = (f32[32,16,1]{2,1,0:T(8,128)S(1)}, f32[32,16,1]{2,1,0:T(8,128)S(1)}, u32[]{:S(2)}, u32[]{:S(2)}) collective-permute-start(f32[32,16,1]{2,1,0:T(8,128)S(1)} %slice.354), channel_id=1, source_target_pairs={{0,1},{1,2},{2,3},{3,4},{4,5},{5,6},{6,7},{8,9},{9,10},{10,11},{11... | collective-permute-start | bytes 6152 | tf_op jit(solution)/shard_map/ppermute | solution.py:17
  25.1 8.7 %collective-permute-done.3 = f32[32,16,1]{2,1,0:T(8,128)S(1)} collective-permute-done((f32[32,16,1]{2,1,0:T(8,128)S(1)}, f32[32,16,1]{2,1,0:T(8,128)S(1)}, u32[]{:S(2)}, u32[]{:S(2)}) %collective-permute-start.3) | collective-permute-done | bytes 2080 | tf_op jit(solution)/shard_map/ppermute | solution.py:17
  35.1 1.9 collective-permute-start.4
  37.0 3.6 %collective-permute-start.5 = (f32[32,16,1]{2,1,0:T(8,128)S(1)}, f32[32,16,1]{2,1,0:T(8,128)S(1)}, u32[]{:S(2)}, u32[]{:S(2)}) collective-permute-start(f32[32,16,1]{2,1,0:T(8,128)S(1)} %slice.358), channel_id=1, source_target_pairs={{1,0},{2,1},{3,2},{4,3},{5,4},{6,5},{7,6},{9,8},{10,9},{11,10},{12... | collective-permute-start | bytes 6152 | tf_op jit(solution)/shard_map/ppermute | solution.py:17
  40.8 3.3 %collective-permute-done.5 = f32[32,16,1]{2,1,0:T(8,128)S(1)} collective-permute-done((f32[32,16,1]{2,1,0:T(8,128)S(1)}, f32[32,16,1]{2,1,0:T(8,128)S(1)}, u32[]{:S(2)}, u32[]{:S(2)}) %collective-permute-start.5) | collective-permute-done | bytes 2080 | tf_op jit(solution)/shard_map/ppermute | solution.py:17
  44.1 1.3 fusion.113
  46.3 6.3 %collective-permute-start.6 = (f32[32,1,512]{2,1,0:T(1,128)S(1)}, f32[32,1,512]{2,1,0:T(1,128)S(1)}, u32[]{:S(2)}, u32[]{:S(2)}) collective-permute-start(f32[32,1,512]{2,1,0:T(1,128)S(1)} %slice.361), channel_id=1, source_target_pairs={{0,8},{8,16},{16,24},{24,32},{32,40},{40,48},{48,56},{56,64},{64,7... | collective-permute-start | bytes 196616 | tf_op jit(solution)/shard_map/ppermute | solution.py:17
  52.7 1.9 collective-permute-start.7
  54.8 10.5 %collective-permute-done.7 = f32[32,16,1]{2,1,0:T(8,128)S(1)} collective-permute-done((f32[32,16,1]{2,1,0:T(8,128)S(1)}, f32[32,16,1]{2,1,0:T(8,128)S(1)}, u32[]{:S(2)}, u32[]{:S(2)}) %collective-permute-start.7) | collective-permute-done | bytes 2080 | tf_op jit(solution)/shard_map/ppermute | solution.py:17
  65.3 1.2 multiply_subtract_fusion.5
  66.6 2.3 collective-permute-start.8
  68.9 3.4 %collective-permute-start.9 = (f32[32,16,1]{2,1,0:T(8,128)S(1)}, f32[32,16,1]{2,1,0:T(8,128)S(1)}, u32[]{:S(2)}, u32[]{:S(2)}) collective-permute-start(f32[32,16,1]{2,1,0:T(8,128)S(1)} %slice.367), channel_id=1, source_target_pairs={{1,0},{2,1},{3,2},{4,3},{5,4},{6,5},{7,6},{9,8},{10,9},{11,10},{12... | collective-permute-start | bytes 6152 | tf_op jit(solution)/shard_map/ppermute | solution.py:17
  72.5 5.1 %collective-permute-done.9 = f32[32,16,1]{2,1,0:T(8,128)S(1)} collective-permute-done((f32[32,16,1]{2,1,0:T(8,128)S(1)}, f32[32,16,1]{2,1,0:T(8,128)S(1)}, u32[]{:S(2)}, u32[]{:S(2)}) %collective-permute-start.9) | collective-permute-done | bytes 2080 | tf_op jit(solution)/shard_map/ppermute | solution.py:17
  77.5 1.3 fusion.114
  79.8 4.4 %collective-permute-start.10 = (f32[32,1,512]{2,1,0:T(1,128)S(1)}, f32[32,1,512]{2,1,0:T(1,128)S(1)}, u32[]{:S(2)}, u32[]{:S(2)}) collective-permute-start(f32[32,1,512]{2,1,0:T(1,128)S(1)} %slice.370), channel_id=1, source_target_pairs={{0,8},{8,16},{16,24},{24,32},{32,40},{40,48},{48,56},{56,64},{64,7... | collective-permute-start | bytes 196616 | tf_op jit(solution)/shard_map/ppermute | solution.py:17
  84.3 2.1 collective-permute-start.11
  86.5 10.0 %collective-permute-done.11 = f32[32,16,1]{2,1,0:T(8,128)S(1)} collective-permute-done((f32[32,16,1]{2,1,0:T(8,128)S(1)}, f32[32,16,1]{2,1,0:T(8,128)S(1)}, u32[]{:S(2)}, u32[]{:S(2)}) %collective-permute-start.11) | collective-permute-done | bytes 2080 | tf_op jit(solution)/shard_map/ppermute | solution.py:17
  96.6 1.2 multiply_subtract_fusion.4
  97.9 2.3 collective-permute-start.12
  100.2 3.3 %collective-permute-start.13 = (f32[32,16,1]{2,1,0:T(8,128)S(1)}, f32[32,16,1]{2,1,0:T(8,128)S(1)}, u32[]{:S(2)}, u32[]{:S(2)}) collective-permute-start(f32[32,16,1]{2,1,0:T(8,128)S(1)} %slice.376), channel_id=1, source_target_pairs={{1,0},{2,1},{3,2},{4,3},{5,4},{6,5},{7,6},{9,8},{10,9},{11,10},{12... | collective-permute-start | bytes 6152 | tf_op jit(solution)/shard_map/ppermute | solution.py:17
  103.6 5.8 %collective-permute-done.13 = f32[32,16,1]{2,1,0:T(8,128)S(1)} collective-permute-done((f32[32,16,1]{2,1,0:T(8,128)S(1)}, f32[32,16,1]{2,1,0:T(8,128)S(1)}, u32[]{:S(2)}, u32[]{:S(2)}) %collective-permute-start.13) | collective-permute-done | bytes 2080 | tf_op jit(solution)/shard_map/ppermute | solution.py:17
  109.4 1.3 fusion.115
  111.6 3.8 %collective-permute-start.14 = (f32[32,1,512]{2,1,0:T(1,128)S(1)}, f32[32,1,512]{2,1,0:T(1,128)S(1)}, u32[]{:S(2)}, u32[]{:S(2)}) collective-permute-start(f32[32,1,512]{2,1,0:T(1,128)S(1)} %slice.379), channel_id=1, source_target_pairs={{0,8},{8,16},{16,24},{24,32},{32,40},{40,48},{48,56},{56,64},{64,7... | collective-permute-start | bytes 196616 | tf_op jit(solution)/shard_map/ppermute | solution.py:17
  115.6 1.9 collective-permute-start.15
  117.7 10.2 %collective-permute-done.15 = f32[32,16,1]{2,1,0:T(8,128)S(1)} collective-permute-done((f32[32,16,1]{2,1,0:T(8,128)S(1)}, f32[32,16,1]{2,1,0:T(8,128)S(1)}, u32[]{:S(2)}, u32[]{:S(2)}) %collective-permute-start.15) | collective-permute-done | bytes 2080 | tf_op jit(solution)/shard_map/ppermute | solution.py:17
  127.9 1.2 multiply_subtract_fusion.3
  129.2 2.3 collective-permute-start.16
  131.5 3.0 %collective-permute-start.17 = (f32[32,16,1]{2,1,0:T(8,128)S(1)}, f32[32,16,1]{2,1,0:T(8,128)S(1)}, u32[]{:S(2)}, u32[]{:S(2)}) collective-permute-start(f32[32,16,1]{2,1,0:T(8,128)S(1)} %slice.385), channel_id=1, source_target_pairs={{1,0},{2,1},{3,2},{4,3},{5,4},{6,5},{7,6},{9,8},{10,9},{11,10},{12... | collective-permute-start | bytes 6152 | tf_op jit(solution)/shard_map/ppermute | solution.py:17
  134.7 6.4 %collective-permute-done.17 = f32[32,16,1]{2,1,0:T(8,128)S(1)} collective-permute-done((f32[32,16,1]{2,1,0:T(8,128)S(1)}, f32[32,16,1]{2,1,0:T(8,128)S(1)}, u32[]{:S(2)}, u32[]{:S(2)}) %collective-permute-start.17) | collective-permute-done | bytes 2080 | tf_op jit(solution)/shard_map/ppermute | solution.py:17
  141.1 1.3 fusion.116
  143.3 3.5 %collective-permute-start.18 = (f32[32,1,512]{2,1,0:T(1,128)S(1)}, f32[32,1,512]{2,1,0:T(1,128)S(1)}, u32[]{:S(2)}, u32[]{:S(2)}) collective-permute-start(f32[32,1,512]{2,1,0:T(1,128)S(1)} %slice.388), channel_id=1, source_target_pairs={{0,8},{8,16},{16,24},{24,32},{32,40},{40,48},{48,56},{56,64},{64,7... | collective-permute-start | bytes 196616 | tf_op jit(solution)/shard_map/ppermute | solution.py:17
  146.9 1.9 collective-permute-start.19
  149.0 10.2 %collective-permute-done.19 = f32[32,16,1]{2,1,0:T(8,128)S(1)} collective-permute-done((f32[32,16,1]{2,1,0:T(8,128)S(1)}, f32[32,16,1]{2,1,0:T(8,128)S(1)}, u32[]{:S(2)}, u32[]{:S(2)}) %collective-permute-start.19) | collective-permute-done | bytes 2080 | tf_op jit(solution)/shard_map/ppermute | solution.py:17
  159.2 1.2 multiply_subtract_fusion.2
  160.5 2.3 collective-permute-start.20
  162.8 2.9 %collective-permute-start.21 = (f32[32,16,1]{2,1,0:T(8,128)S(1)}, f32[32,16,1]{2,1,0:T(8,128)S(1)}, u32[]{:S(2)}, u32[]{:S(2)}) collective-permute-start(f32[32,16,1]{2,1,0:T(8,128)S(1)} %slice.394), channel_id=1, source_target_pairs={{1,0},{2,1},{3,2},{4,3},{5,4},{6,5},{7,6},{9,8},{10,9},{11,10},{12... | collective-permute-start | bytes 6152 | tf_op jit(solution)/shard_map/ppermute | solution.py:17
  165.9 6.5 %collective-permute-done.21 = f32[32,16,1]{2,1,0:T(8,128)S(1)} collective-permute-done((f32[32,16,1]{2,1,0:T(8,128)S(1)}, f32[32,16,1]{2,1,0:T(8,128)S(1)}, u32[]{:S(2)}, u32[]{:S(2)}) %collective-permute-start.21) | collective-permute-done | bytes 2080 | tf_op jit(solution)/shard_map/ppermute | solution.py:17
  172.4 1.3 fusion.117
  174.6 3.5 %collective-permute-start.22 = (f32[32,1,512]{2,1,0:T(1,128)S(1)}, f32[32,1,512]{2,1,0:T(1,128)S(1)}, u32[]{:S(2)}, u32[]{:S(2)}) collective-permute-start(f32[32,1,512]{2,1,0:T(1,128)S(1)} %slice.397), channel_id=1, source_target_pairs={{0,8},{8,16},{16,24},{24,32},{32,40},{40,48},{48,56},{56,64},{64,7... | collective-permute-start | bytes 196616 | tf_op jit(solution)/shard_map/ppermute | solution.py:17
  178.2 1.9 collective-permute-start.23
  180.2 10.2 %collective-permute-done.23 = f32[32,16,1]{2,1,0:T(8,128)S(1)} collective-permute-done((f32[32,16,1]{2,1,0:T(8,128)S(1)}, f32[32,16,1]{2,1,0:T(8,128)S(1)}, u32[]{:S(2)}, u32[]{:S(2)}) %collective-permute-start.23) | collective-permute-done | bytes 2080 | tf_op jit(solution)/shard_map/ppermute | solution.py:17
  190.5 1.2 multiply_subtract_fusion.1
  191.8 2.3 collective-permute-start.24
  194.1 2.4 collective-permute-start.25
  196.6 7.0 %collective-permute-done.25 = f32[32,16,1]{2,1,0:T(8,128)S(1)} collective-permute-done((f32[32,16,1]{2,1,0:T(8,128)S(1)}, f32[32,16,1]{2,1,0:T(8,128)S(1)}, u32[]{:S(2)}, u32[]{:S(2)}) %collective-permute-start.25) | collective-permute-done | bytes 2080 | tf_op jit(solution)/shard_map/ppermute | solution.py:17
  203.7 1.3 fusion.118
  205.9 3.5 %collective-permute-start.26 = (f32[32,1,512]{2,1,0:T(1,128)S(1)}, f32[32,1,512]{2,1,0:T(1,128)S(1)}, u32[]{:S(2)}, u32[]{:S(2)}) collective-permute-start(f32[32,1,512]{2,1,0:T(1,128)S(1)} %slice.406), channel_id=1, source_target_pairs={{0,8},{8,16},{16,24},{24,32},{32,40},{40,48},{48,56},{56,64},{64,7... | collective-permute-start | bytes 196616 | tf_op jit(solution)/shard_map/ppermute | solution.py:17
  209.5 1.9 collective-permute-start.27
  211.6 10.2 %collective-permute-done.27 = f32[32,16,1]{2,1,0:T(8,128)S(1)} collective-permute-done((f32[32,16,1]{2,1,0:T(8,128)S(1)}, f32[32,16,1]{2,1,0:T(8,128)S(1)}, u32[]{:S(2)}, u32[]{:S(2)}) %collective-permute-start.27) | collective-permute-done | bytes 2080 | tf_op jit(solution)/shard_map/ppermute | solution.py:17
  221.8 1.2 multiply_subtract_fusion
  223.1 2.3 collective-permute-start.28
  225.4 2.3 collective-permute-start.29
  227.9 7.0 %collective-permute-done.29 = f32[32,16,1]{2,1,0:T(8,128)S(1)} collective-permute-done((f32[32,16,1]{2,1,0:T(8,128)S(1)}, f32[32,16,1]{2,1,0:T(8,128)S(1)}, u32[]{:S(2)}, u32[]{:S(2)}) %collective-permute-start.29) | collective-permute-done | bytes 2080 | tf_op jit(solution)/shard_map/ppermute | solution.py:17
  234.9 1.3 fusion.112
  237.2 3.5 %collective-permute-start.30 = (f32[32,1,512]{2,1,0:T(1,128)S(1)}, f32[32,1,512]{2,1,0:T(1,128)S(1)}, u32[]{:S(2)}, u32[]{:S(2)}) collective-permute-start(f32[32,1,512]{2,1,0:T(1,128)S(1)} %slice.415), channel_id=1, source_target_pairs={{0,8},{8,16},{16,24},{24,32},{32,40},{40,48},{48,56},{56,64},{64,7... | collective-permute-start | bytes 196616 | tf_op jit(solution)/shard_map/ppermute | solution.py:17
  240.8 1.9 collective-permute-start.31
  242.9 10.2 %collective-permute-done.31 = f32[32,16,1]{2,1,0:T(8,128)S(1)} collective-permute-done((f32[32,16,1]{2,1,0:T(8,128)S(1)}, f32[32,16,1]{2,1,0:T(8,128)S(1)}, u32[]{:S(2)}, u32[]{:S(2)}) %collective-permute-start.31) | collective-permute-done | bytes 2080 | tf_op jit(solution)/shard_map/ppermute | solution.py:17
  253.1 2.2 fusion.102
  (78 shorter events, 13.5 us)
Async XLA Ops:
  1.1 12.1 %collective-permute-start = (f32[32,1,512]{2,1,0:T(1,128)S(1)}, f32[32,1,512]{2,1,0:T(1,128)S(1)}, u32[]{:S(2)}, u32[]{:S(2)}) collective-permute-start(f32[32,1,512]{2,1,0:T(1,128)S(1)} %slice.264), channel_id=1, source_target_pairs={{8,0},{16,8},{24,16},{32,24},{40,32},{48,40},{56,48},{64,56},{72,6... | collective-permute-start | bytes 196616 | tf_op jit(solution)/shard_map/ppermute | solution.py:17
  5.3 7.9 %collective-permute-start.1 = (f32[32,16,1]{2,1,0:T(8,128)}, f32[32,16,1]{2,1,0:T(8,128)S(1)}, u32[]{:S(2)}, u32[]{:S(2)}) collective-permute-start(f32[32,16,1]{2,1,0:T(8,128)} %slice.266), channel_id=1, source_target_pairs={{1,0},{2,1},{3,2},{4,3},{5,4},{6,5},{7,6},{9,8},{10,9},{11,10},{12... | collective-permute-start | bytes 6152 | tf_op jit(solution)/shard_map/ppermute | solution.py:17
  9.6 3.6 %copy-start = (f32[32,16,512]{2,1,0:T(8,128)S(1)}, f32[32,16,512]{2,1,0:T(8,128)}, u32[]{:S(2)}) copy-start(f32[32,16,512]{2,1,0:T(8,128)} %param.2) | copy-start | bytes 3145732
  9.6 3.6 %copy-start.1 = (f32[32,16,512]{2,1,0:T(8,128)S(1)}, f32[32,16,512]{2,1,0:T(8,128)}, u32[]{:S(2)}) copy-start(f32[32,16,512]{2,1,0:T(8,128)} %param.3) | copy-start | bytes 3145732
  15.0 18.9 %collective-permute-start.2 = (f32[32,1,512]{2,1,0:T(1,128)S(1)}, f32[32,1,512]{2,1,0:T(1,128)S(1)}, u32[]{:S(2)}, u32[]{:S(2)}) collective-permute-start(f32[32,1,512]{2,1,0:T(1,128)S(1)} %slice.352), channel_id=1, source_target_pairs={{0,8},{8,16},{16,24},{24,32},{32,40},{40,48},{48,56},{56,64},{64,7... | collective-permute-start | bytes 196616 | tf_op jit(solution)/shard_map/ppermute | solution.py:17
  22.4 11.4 %collective-permute-start.3 = (f32[32,16,1]{2,1,0:T(8,128)S(1)}, f32[32,16,1]{2,1,0:T(8,128)S(1)}, u32[]{:S(2)}, u32[]{:S(2)}) collective-permute-start(f32[32,16,1]{2,1,0:T(8,128)S(1)} %slice.354), channel_id=1, source_target_pairs={{0,1},{1,2},{2,3},{3,4},{4,5},{5,6},{6,7},{8,9},{9,10},{10,11},{11... | collective-permute-start | bytes 6152 | tf_op jit(solution)/shard_map/ppermute | solution.py:17
  35.1 9.0 %collective-permute-start.4 = (f32[32,1,512]{2,1,0:T(1,128)S(1)}, f32[32,1,512]{2,1,0:T(1,128)S(1)}, u32[]{:S(2)}, u32[]{:S(2)}) collective-permute-start(f32[32,1,512]{2,1,0:T(1,128)S(1)} %slice.357), channel_id=1, source_target_pairs={{8,0},{16,8},{24,16},{32,24},{40,32},{48,40},{56,48},{64,56},{72,6... | collective-permute-start | bytes 196616 | tf_op jit(solution)/shard_map/ppermute | solution.py:17
  37.0 7.1 %collective-permute-start.5 = (f32[32,16,1]{2,1,0:T(8,128)S(1)}, f32[32,16,1]{2,1,0:T(8,128)S(1)}, u32[]{:S(2)}, u32[]{:S(2)}) collective-permute-start(f32[32,16,1]{2,1,0:T(8,128)S(1)} %slice.358), channel_id=1, source_target_pairs={{1,0},{2,1},{3,2},{4,3},{5,4},{6,5},{7,6},{9,8},{10,9},{11,10},{12... | collective-permute-start | bytes 6152 | tf_op jit(solution)/shard_map/ppermute | solution.py:17
  46.3 19.0 %collective-permute-start.6 = (f32[32,1,512]{2,1,0:T(1,128)S(1)}, f32[32,1,512]{2,1,0:T(1,128)S(1)}, u32[]{:S(2)}, u32[]{:S(2)}) collective-permute-start(f32[32,1,512]{2,1,0:T(1,128)S(1)} %slice.361), channel_id=1, source_target_pairs={{0,8},{8,16},{16,24},{24,32},{32,40},{40,48},{48,56},{56,64},{64,7... | collective-permute-start | bytes 196616 | tf_op jit(solution)/shard_map/ppermute | solution.py:17
  52.7 12.5 %collective-permute-start.7 = (f32[32,16,1]{2,1,0:T(8,128)S(1)}, f32[32,16,1]{2,1,0:T(8,128)S(1)}, u32[]{:S(2)}, u32[]{:S(2)}) collective-permute-start(f32[32,16,1]{2,1,0:T(8,128)S(1)} %slice.363), channel_id=1, source_target_pairs={{0,1},{1,2},{2,3},{3,4},{4,5},{5,6},{6,7},{8,9},{9,10},{10,11},{11... | collective-permute-start | bytes 6152 | tf_op jit(solution)/shard_map/ppermute | solution.py:17
  66.6 10.9 %collective-permute-start.8 = (f32[32,1,512]{2,1,0:T(1,128)S(1)}, f32[32,1,512]{2,1,0:T(1,128)S(1)}, u32[]{:S(2)}, u32[]{:S(2)}) collective-permute-start(f32[32,1,512]{2,1,0:T(1,128)S(1)} %slice.366), channel_id=1, source_target_pairs={{8,0},{16,8},{24,16},{32,24},{40,32},{48,40},{56,48},{64,56},{72,6... | collective-permute-start | bytes 196616 | tf_op jit(solution)/shard_map/ppermute | solution.py:17
  68.9 8.6 %collective-permute-start.9 = (f32[32,16,1]{2,1,0:T(8,128)S(1)}, f32[32,16,1]{2,1,0:T(8,128)S(1)}, u32[]{:S(2)}, u32[]{:S(2)}) collective-permute-start(f32[32,16,1]{2,1,0:T(8,128)S(1)} %slice.367), channel_id=1, source_target_pairs={{1,0},{2,1},{3,2},{4,3},{5,4},{6,5},{7,6},{9,8},{10,9},{11,10},{12... | collective-permute-start | bytes 6152 | tf_op jit(solution)/shard_map/ppermute | solution.py:17
  79.8 16.8 %collective-permute-start.10 = (f32[32,1,512]{2,1,0:T(1,128)S(1)}, f32[32,1,512]{2,1,0:T(1,128)S(1)}, u32[]{:S(2)}, u32[]{:S(2)}) collective-permute-start(f32[32,1,512]{2,1,0:T(1,128)S(1)} %slice.370), channel_id=1, source_target_pairs={{0,8},{8,16},{16,24},{24,32},{32,40},{40,48},{48,56},{56,64},{64,7... | collective-permute-start | bytes 196616 | tf_op jit(solution)/shard_map/ppermute | solution.py:17
  84.3 12.3 %collective-permute-start.11 = (f32[32,16,1]{2,1,0:T(8,128)S(1)}, f32[32,16,1]{2,1,0:T(8,128)S(1)}, u32[]{:S(2)}, u32[]{:S(2)}) collective-permute-start(f32[32,16,1]{2,1,0:T(8,128)S(1)} %slice.372), channel_id=1, source_target_pairs={{0,1},{1,2},{2,3},{3,4},{4,5},{5,6},{6,7},{8,9},{9,10},{10,11},{11... | collective-permute-start | bytes 6152 | tf_op jit(solution)/shard_map/ppermute | solution.py:17
  97.9 11.5 %collective-permute-start.12 = (f32[32,1,512]{2,1,0:T(1,128)S(1)}, f32[32,1,512]{2,1,0:T(1,128)S(1)}, u32[]{:S(2)}, u32[]{:S(2)}) collective-permute-start(f32[32,1,512]{2,1,0:T(1,128)S(1)} %slice.375), channel_id=1, source_target_pairs={{8,0},{16,8},{24,16},{32,24},{40,32},{48,40},{56,48},{64,56},{72,6... | collective-permute-start | bytes 196616 | tf_op jit(solution)/shard_map/ppermute | solution.py:17
  100.2 9.2 %collective-permute-start.13 = (f32[32,16,1]{2,1,0:T(8,128)S(1)}, f32[32,16,1]{2,1,0:T(8,128)S(1)}, u32[]{:S(2)}, u32[]{:S(2)}) collective-permute-start(f32[32,16,1]{2,1,0:T(8,128)S(1)} %slice.376), channel_id=1, source_target_pairs={{1,0},{2,1},{3,2},{4,3},{5,4},{6,5},{7,6},{9,8},{10,9},{11,10},{12... | collective-permute-start | bytes 6152 | tf_op jit(solution)/shard_map/ppermute | solution.py:17
  111.6 16.2 %collective-permute-start.14 = (f32[32,1,512]{2,1,0:T(1,128)S(1)}, f32[32,1,512]{2,1,0:T(1,128)S(1)}, u32[]{:S(2)}, u32[]{:S(2)}) collective-permute-start(f32[32,1,512]{2,1,0:T(1,128)S(1)} %slice.379), channel_id=1, source_target_pairs={{0,8},{8,16},{16,24},{24,32},{32,40},{40,48},{48,56},{56,64},{64,7... | collective-permute-start | bytes 196616 | tf_op jit(solution)/shard_map/ppermute | solution.py:17
  115.6 12.3 %collective-permute-start.15 = (f32[32,16,1]{2,1,0:T(8,128)S(1)}, f32[32,16,1]{2,1,0:T(8,128)S(1)}, u32[]{:S(2)}, u32[]{:S(2)}) collective-permute-start(f32[32,16,1]{2,1,0:T(8,128)S(1)} %slice.381), channel_id=1, source_target_pairs={{0,1},{1,2},{2,3},{3,4},{4,5},{5,6},{6,7},{8,9},{9,10},{10,11},{11... | collective-permute-start | bytes 6152 | tf_op jit(solution)/shard_map/ppermute | solution.py:17
  129.2 11.9 %collective-permute-start.16 = (f32[32,1,512]{2,1,0:T(1,128)S(1)}, f32[32,1,512]{2,1,0:T(1,128)S(1)}, u32[]{:S(2)}, u32[]{:S(2)}) collective-permute-start(f32[32,1,512]{2,1,0:T(1,128)S(1)} %slice.384), channel_id=1, source_target_pairs={{8,0},{16,8},{24,16},{32,24},{40,32},{48,40},{56,48},{64,56},{72,6... | collective-permute-start | bytes 196616 | tf_op jit(solution)/shard_map/ppermute | solution.py:17
  131.5 9.5 %collective-permute-start.17 = (f32[32,16,1]{2,1,0:T(8,128)S(1)}, f32[32,16,1]{2,1,0:T(8,128)S(1)}, u32[]{:S(2)}, u32[]{:S(2)}) collective-permute-start(f32[32,16,1]{2,1,0:T(8,128)S(1)} %slice.385), channel_id=1, source_target_pairs={{1,0},{2,1},{3,2},{4,3},{5,4},{6,5},{7,6},{9,8},{10,9},{11,10},{12... | collective-permute-start | bytes 6152 | tf_op jit(solution)/shard_map/ppermute | solution.py:17
  143.3 15.9 %collective-permute-start.18 = (f32[32,1,512]{2,1,0:T(1,128)S(1)}, f32[32,1,512]{2,1,0:T(1,128)S(1)}, u32[]{:S(2)}, u32[]{:S(2)}) collective-permute-start(f32[32,1,512]{2,1,0:T(1,128)S(1)} %slice.388), channel_id=1, source_target_pairs={{0,8},{8,16},{16,24},{24,32},{32,40},{40,48},{48,56},{56,64},{64,7... | collective-permute-start | bytes 196616 | tf_op jit(solution)/shard_map/ppermute | solution.py:17
  146.9 12.3 %collective-permute-start.19 = (f32[32,16,1]{2,1,0:T(8,128)S(1)}, f32[32,16,1]{2,1,0:T(8,128)S(1)}, u32[]{:S(2)}, u32[]{:S(2)}) collective-permute-start(f32[32,16,1]{2,1,0:T(8,128)S(1)} %slice.390), channel_id=1, source_target_pairs={{0,1},{1,2},{2,3},{3,4},{4,5},{5,6},{6,7},{8,9},{9,10},{10,11},{11... | collective-permute-start | bytes 6152 | tf_op jit(solution)/shard_map/ppermute | solution.py:17
  160.5 11.9 %collective-permute-start.20 = (f32[32,1,512]{2,1,0:T(1,128)S(1)}, f32[32,1,512]{2,1,0:T(1,128)S(1)}, u32[]{:S(2)}, u32[]{:S(2)}) collective-permute-start(f32[32,1,512]{2,1,0:T(1,128)S(1)} %slice.393), channel_id=1, source_target_pairs={{8,0},{16,8},{24,16},{32,24},{40,32},{48,40},{56,48},{64,56},{72,6... | collective-permute-start | bytes 196616 | tf_op jit(solution)/shard_map/ppermute | solution.py:17
  162.8 9.5 %collective-permute-start.21 = (f32[32,16,1]{2,1,0:T(8,128)S(1)}, f32[32,16,1]{2,1,0:T(8,128)S(1)}, u32[]{:S(2)}, u32[]{:S(2)}) collective-permute-start(f32[32,16,1]{2,1,0:T(8,128)S(1)} %slice.394), channel_id=1, source_target_pairs={{1,0},{2,1},{3,2},{4,3},{5,4},{6,5},{7,6},{9,8},{10,9},{11,10},{12... | collective-permute-start | bytes 6152 | tf_op jit(solution)/shard_map/ppermute | solution.py:17
  174.6 15.9 %collective-permute-start.22 = (f32[32,1,512]{2,1,0:T(1,128)S(1)}, f32[32,1,512]{2,1,0:T(1,128)S(1)}, u32[]{:S(2)}, u32[]{:S(2)}) collective-permute-start(f32[32,1,512]{2,1,0:T(1,128)S(1)} %slice.397), channel_id=1, source_target_pairs={{0,8},{8,16},{16,24},{24,32},{32,40},{40,48},{48,56},{56,64},{64,7... | collective-permute-start | bytes 196616 | tf_op jit(solution)/shard_map/ppermute | solution.py:17
  178.2 12.3 %collective-permute-start.23 = (f32[32,16,1]{2,1,0:T(8,128)S(1)}, f32[32,16,1]{2,1,0:T(8,128)S(1)}, u32[]{:S(2)}, u32[]{:S(2)}) collective-permute-start(f32[32,16,1]{2,1,0:T(8,128)S(1)} %slice.399), channel_id=1, source_target_pairs={{0,1},{1,2},{2,3},{3,4},{4,5},{5,6},{6,7},{8,9},{9,10},{10,11},{11... | collective-permute-start | bytes 6152 | tf_op jit(solution)/shard_map/ppermute | solution.py:17
  191.8 11.9 %collective-permute-start.24 = (f32[32,1,512]{2,1,0:T(1,128)S(1)}, f32[32,1,512]{2,1,0:T(1,128)S(1)}, u32[]{:S(2)}, u32[]{:S(2)}) collective-permute-start(f32[32,1,512]{2,1,0:T(1,128)S(1)} %slice.402), channel_id=1, source_target_pairs={{8,0},{16,8},{24,16},{32,24},{40,32},{48,40},{56,48},{64,56},{72,6... | collective-permute-start | bytes 196616 | tf_op jit(solution)/shard_map/ppermute | solution.py:17
  194.1 9.5 %collective-permute-start.25 = (f32[32,16,1]{2,1,0:T(8,128)S(1)}, f32[32,16,1]{2,1,0:T(8,128)S(1)}, u32[]{:S(2)}, u32[]{:S(2)}) collective-permute-start(f32[32,16,1]{2,1,0:T(8,128)S(1)} %slice.403), channel_id=1, source_target_pairs={{1,0},{2,1},{3,2},{4,3},{5,4},{6,5},{7,6},{9,8},{10,9},{11,10},{12... | collective-permute-start | bytes 6152 | tf_op jit(solution)/shard_map/ppermute | solution.py:17
  205.9 15.9 %collective-permute-start.26 = (f32[32,1,512]{2,1,0:T(1,128)S(1)}, f32[32,1,512]{2,1,0:T(1,128)S(1)}, u32[]{:S(2)}, u32[]{:S(2)}) collective-permute-start(f32[32,1,512]{2,1,0:T(1,128)S(1)} %slice.406), channel_id=1, source_target_pairs={{0,8},{8,16},{16,24},{24,32},{32,40},{40,48},{48,56},{56,64},{64,7... | collective-permute-start | bytes 196616 | tf_op jit(solution)/shard_map/ppermute | solution.py:17
  209.5 12.3 %collective-permute-start.27 = (f32[32,16,1]{2,1,0:T(8,128)S(1)}, f32[32,16,1]{2,1,0:T(8,128)S(1)}, u32[]{:S(2)}, u32[]{:S(2)}) collective-permute-start(f32[32,16,1]{2,1,0:T(8,128)S(1)} %slice.408), channel_id=1, source_target_pairs={{0,1},{1,2},{2,3},{3,4},{4,5},{5,6},{6,7},{8,9},{9,10},{10,11},{11... | collective-permute-start | bytes 6152 | tf_op jit(solution)/shard_map/ppermute | solution.py:17
  223.1 11.8 %collective-permute-start.28 = (f32[32,1,512]{2,1,0:T(1,128)S(1)}, f32[32,1,512]{2,1,0:T(1,128)S(1)}, u32[]{:S(2)}, u32[]{:S(2)}) collective-permute-start(f32[32,1,512]{2,1,0:T(1,128)S(1)} %slice.411), channel_id=1, source_target_pairs={{8,0},{16,8},{24,16},{32,24},{40,32},{48,40},{56,48},{64,56},{72,6... | collective-permute-start | bytes 196616 | tf_op jit(solution)/shard_map/ppermute | solution.py:17
  225.4 9.5 %collective-permute-start.29 = (f32[32,16,1]{2,1,0:T(8,128)S(1)}, f32[32,16,1]{2,1,0:T(8,128)S(1)}, u32[]{:S(2)}, u32[]{:S(2)}) collective-permute-start(f32[32,16,1]{2,1,0:T(8,128)S(1)} %slice.412), channel_id=1, source_target_pairs={{1,0},{2,1},{3,2},{4,3},{5,4},{6,5},{7,6},{9,8},{10,9},{11,10},{12... | collective-permute-start | bytes 6152 | tf_op jit(solution)/shard_map/ppermute | solution.py:17
  237.2 15.9 %collective-permute-start.30 = (f32[32,1,512]{2,1,0:T(1,128)S(1)}, f32[32,1,512]{2,1,0:T(1,128)S(1)}, u32[]{:S(2)}, u32[]{:S(2)}) collective-permute-start(f32[32,1,512]{2,1,0:T(1,128)S(1)} %slice.415), channel_id=1, source_target_pairs={{0,8},{8,16},{16,24},{24,32},{32,40},{40,48},{48,56},{56,64},{64,7... | collective-permute-start | bytes 196616 | tf_op jit(solution)/shard_map/ppermute | solution.py:17
  240.8 12.3 %collective-permute-start.31 = (f32[32,16,1]{2,1,0:T(8,128)S(1)}, f32[32,16,1]{2,1,0:T(8,128)S(1)}, u32[]{:S(2)}, u32[]{:S(2)}) collective-permute-start(f32[32,16,1]{2,1,0:T(8,128)S(1)} %slice.417), channel_id=1, source_target_pairs={{0,1},{1,2},{2,3},{3,4},{4,5},{5,6},{6,7},{8,9},{9,10},{10,11},{11... | collective-permute-start | bytes 6152 | tf_op jit(solution)/shard_map/ppermute | solution.py:17
where the time goes:
time: 257 us; the launch traced here: 255 us
  waiting for transfers between devices  123 us (48%)
  starting transfers between devices  95.6 us (37%)
  other arithmetic  30 us (12%)
  local copies, waits for them, and re-layouts  5.61 us (2%)
    ppermute x32, waiting for transfers between devices, from_behind(): lax.ppermute(value, axis, [(source, source + steps) for source in range(l...  123 us
    ppermute x32, starting transfers between devices, from_behind(): lax.ppermute(value, axis, [(source, source + steps) for source in range(l...  95.6 us
    div x16, other arithmetic, project(): return (dual_x / factor, dual_y / factor, dual_z / factor)  16.6 us
    sub x7, other arithmetic, per_device(): extrapolated = 2.0 * updated - primal  8.51 us
  transfers between devices with their start and end apart: 32, of which 16 were waited for; matrix products, arithmetic and copies ran while one was open for 2% of the time, Pallas kernels for 0%

commit v1 on v0

v1 whole, which is shorter than its diff:
```python
import jax
import jax.numpy as jnp
from jax import lax
from jax.sharding import PartitionSpec as P

ITERS = 8
HALO = ITERS


dual_step = 0.28
primal_step = 0.28
fidelity = 1.0


def from_offset(value, axis, offset):
    count = lax.axis_size(axis)
    return lax.ppermute(value, axis, [((dest + offset) % count, dest) for dest in range(count)])


def extend(noisy, weight):
    planes, rows, cols = noisy.shape
    width = -(-(cols + 2 * HALO) // 128) * 128
    both = jnp.stack([noisy, weight])
    right = from_offset(both[..., :HALO], "gy", 1)
    left = from_offset(both[..., cols - HALO:], "gy", -1)
    gap = width - cols - 2 * HALO
    filler = jnp.concatenate(
        [jnp.zeros((1, planes, rows, gap), noisy.dtype), jnp.ones((1, planes, rows, gap), noisy.dtype)], 0
    )
    wide = jnp.concatenate([both, right, filler, left], 3)
    below = from_offset(wide[:, :, :HALO, :], "gx", 1)
    above = from_offset(wide[:, :, rows - HALO:, :], "gx", -1)
    full = jnp.concatenate([wide, below, above], 2)
    return full[0], full[1], width


def along_z(field):
    edge = jnp.zeros_like(field[:1])
    return jnp.concatenate([field[1:] - field[:-1], edge], 0)


def back_z(dual):
    edge = jnp.zeros_like(dual[:1])
    return dual - jnp.concatenate([edge, dual[:-1]], 0)


def project(dual_x, dual_y, dual_z, weight):
    length = jnp.sqrt(dual_x * dual_x + dual_y * dual_y + dual_z * dual_z)
    factor = jnp.maximum(1.0, length / weight)
    return (dual_x / factor, dual_y / factor, dual_z / factor)


def per_device(noisy, weight):
    planes, rows_x, rows_y = noisy.shape
    total_x = rows_x * lax.axis_size("gx")
    total_y = rows_y * lax.axis_size("gy")
    start_x = lax.axis_index("gx") * rows_x
    start_y = lax.axis_index("gy") * rows_y
    noisy_e, weight_e, width = extend(noisy, weight)
    ext_x = rows_x + 2 * HALO

    local_x = jnp.arange(ext_x, dtype=jnp.int32)
    index_x = jnp.where(local_x >= rows_x + HALO, start_x + local_x - ext_x, start_x + local_x)
    keep_x = ((index_x >= 0) & (index_x < total_x - 1))[None, :, None]
    local_y = jnp.arange(width, dtype=jnp.int32)
    index_y = jnp.where(local_y >= width - HALO, start_y + local_y - width, start_y + local_y)
    inside_y = (local_y < rows_y + HALO) | (local_y >= width - HALO)
    keep_y = (inside_y & (index_y >= 0) & (index_y < total_y - 1))[None, None, :]

    primal = noisy_e
    extrapolated = noisy_e
    dual_x = jnp.zeros_like(noisy_e)
    dual_y = jnp.zeros_like(noisy_e)
    dual_z = jnp.zeros_like(noisy_e)
    for iteration in range(ITERS):
        slope_x = jnp.where(keep_x, jnp.roll(extrapolated, -1, 1) - extrapolated, 0.0)
        slope_y = jnp.where(keep_y, jnp.roll(extrapolated, -1, 2) - extrapolated, 0.0)
        dual_x = dual_x + dual_step * slope_x
        dual_y = dual_y + dual_step * slope_y
        dual_z = dual_z + dual_step * along_z(extrapolated)
        dual_x, dual_y, dual_z = project(dual_x, dual_y, dual_z, weight_e)
        diverge_x = dual_x - jnp.roll(dual_x, 1, 1)
        diverge_y = dual_y - jnp.roll(dual_y, 1, 2)
        divergence = diverge_x + diverge_y + back_z(dual_z)
        updated = (primal + primal_step * divergence + primal_step * fidelity * noisy_e) / (
            1.0 + primal_step * fidelity
        )
        extrapolated = 2.0 * updated - primal
        primal = updated
    return primal[:, :rows_x, :rows_y]


def solution(mesh):
    placed = (P(None, "gx", "gy"), P(None, "gx", "gy"))
    return jax.shard_map(
        per_device, mesh=mesh, in_specs=placed, out_specs=P(None, "gx", "gy"), check_vma=False
    )
```

time: 257 us -> 218 us (0.85)
  the two profiles are of different devices: /device:TPU:233 before, /device:TPU:1 now
where the time goes in v1:
time: 218 us; the launch traced here: 214 us
  other arithmetic  127 us (58%)
  waiting for transfers between devices  43.8 us (20%)
  local copies, waits for them, and re-layouts  33.4 us (15%)
  starting transfers between devices  9.15 us (4%)
    div x16, other arithmetic, project(): return (dual_x / factor, dual_y / factor, dual_z / factor)  73.1 us
    ppermute x4, waiting for transfers between devices, from_offset(): lax.ppermute(value, axis, [((dest + offset) % count, dest) for dest in ra...  43.8 us
    sub x7, other arithmetic, per_device(): extrapolated = 2.0 * updated - primal  33.7 us
    sub x8, other arithmetic, along_z(): return jnp.concatenate([field[1:] - field[:-1], edge], 0)  10.7 us
    unnamed x26, local copies, waits for them, and re-layouts  10.7 us
    ppermute x4, starting transfers between devices, from_offset(): lax.ppermute(value, axis, [((dest + offset) % count, dest) for dest in ra...  9.15 us
    slice x16, local copies, waits for them, and re-layouts, per_device(): jnp.roll(extrapolated, -1, 2) - extrapolated  8.59 us
    slice x16, local copies, waits for them, and re-layouts, per_device(): jnp.roll(extrapolated, -1, 1) - extrapolated  7.06 us
  transfers between devices with their start and end apart: 4, of which 3 were waited for; matrix products, arithmetic and copies ran while one was open for 0% of the time, Pallas kernels for 0%

profile of v1, /device:TPU:1, one launch (start us, length us, event | category | flops | bytes accessed | tf_op | source)
XLA Modules:
  0.0 213.9 jit_solution(8140218742398996590)
XLA Ops:
  0.0 1.6 pad_maximum_fusion.3
  1.6 4.4 %collective-permute-start = (f32[2,32,16,8]{3,2,1,0:T(8,128)S(1)}, f32[2,32,16,8]{3,2,1,0:T(8,128)S(1)}, u32[]{:S(2)}, u32[]{:S(2)}) collective-permute-start(f32[2,32,16,8]{3,2,1,0:T(8,128)S(1)} %get-tuple-element.67), channel_id=1, source_target_pairs={{1,0},{2,1},{3,2},{4,3},{5,4},{6,5},{7,6},{0,7},{9,8},{10,9},{11,1... | collective-permute-start | bytes 98312 | tf_op jit(solution)/shard_map/ppermute | solution.py:17
  5.9 10.6 %collective-permute-done = f32[2,32,16,8]{3,2,1,0:T(8,128)S(1)} collective-permute-done((f32[2,32,16,8]{3,2,1,0:T(8,128)S(1)}, f32[2,32,16,8]{3,2,1,0:T(8,128)S(1)}, u32[]{:S(2)}, u32[]{:S(2)}) %collective-permute-start) | collective-permute-done | bytes 32800 | tf_op jit(solution)/shard_map/ppermute | solution.py:17
  16.6 4.0 %collective-permute-done.1 = f32[2,32,16,8]{3,2,1,0:T(8,128)S(1)} collective-permute-done((f32[2,32,16,8]{3,2,1,0:T(8,128)S(1)}, f32[2,32,16,8]{3,2,1,0:T(8,128)S(1)}, u32[]{:S(2)}, u32[]{:S(2)}) %collective-permute-start.1) | collective-permute-done | bytes 32800 | tf_op jit(solution)/shard_map/ppermute | solution.py:17
  21.4 1.6 fusion.129
  23.0 1.8 collective-permute-start.2
  24.8 3.0 %collective-permute-start.3 = (f32[2,32,8,640]{3,2,1,0:T(8,128)}, f32[2,32,8,640]{3,2,1,0:T(8,128)}, u32[]{:S(2)}, u32[]{:S(2)}) collective-permute-start(f32[2,32,8,640]{3,2,1,0:T(8,128)} %get-tuple-element.66), channel_id=1, source_target_pairs={{248,0},{0,8},{8,16},{16,24},{24,32},{32,40},{40,48},{48,56},{56,6... | collective-permute-start | bytes 3932168 | tf_op jit(solution)/shard_map/ppermute | solution.py:17
  27.8 29.2 %collective-permute-done.2 = f32[2,32,8,640]{3,2,1,0:T(8,128)} collective-permute-done((f32[2,32,8,640]{3,2,1,0:T(8,128)}, f32[2,32,8,640]{3,2,1,0:T(8,128)}, u32[]{:S(2)}, u32[]{:S(2)}) %collective-permute-start.2) | collective-permute-done | bytes 1310752 | tf_op jit(solution)/shard_map/ppermute | solution.py:17
  57.0 2.4 %pad_maximum_fusion = f32[2,32,32,640]{3,2,1,0:T(8,128)S(1)} fusion(f32[2,32,8,640]{3,2,1,0:T(8,128)} %collective-permute-done.3, f32[2,32,8,640]{3,2,1,0:T(8,128)} %collective-permute-done.2, f32[2,32,16,8]{3,2,1,0:T(8,128)} %copy-done.10, f32[2,32,16,112]{3,2,1,0:T(8,128)S(1)} %concatenate.157, f32[2,32,16,8]{3,2,1,0:T(8,128)S(1)} %collective-permute-done, ...), kind=kLoop, calls=%fused_computation | loop fusion | flops 7864320 | bytes 10485760 | tf_op jit(solution)/shard_map/concatenate | solution.py:33
  59.9 0.7 slice.397
  60.9 3.1 %fusion.82 = (f32[32,32,640]{2,1,0:T(8,128)S(1)}, f32[32,32,640]{2,1,0:T(8,128)S(1)}) fusion(f32[31,32,640]{2,1,0:T(8,128)S(1)} %fusion.81, f32[2,32,32,640]{3,2,1,0:T(8,128)S(1)} %pad_maximum_fusion, f32[32,32,1]{2,1,0:T(8,128)S(1)} %slice.398, f32[32,32,639]{2,1,0:T(8,128)S(1)} %slice.397, pred[640]{0:T(1024)(128)(4,1)S(1)} %fusion.99, ...), kind=kLoop, calls=%fused_computation.149 | loop fusion | flops 11141120 | bytes 18268832 | tf_op jit(solution)/shard_map/div | solution.py:50
  64.0 1.8 fusion.100
  66.3 3.4 %multiply_subtract_fusion.6 = (f32[32,32,640]{2,1,0:T(8,128)S(1)}, f32[32,32,640]{2,1,0:T(8,128)}) fusion(f32[2,32,32,640]{3,2,1,0:T(8,128)S(1)} %pad_maximum_fusion, f32[32,32,640]{2,1,0:T(8,128)S(1)} %get-tuple-element.46, f32[31,32,640]{2,1,0:T(8,128)S(1)} %slice.406, f32[32,32,640]{2,1,0:T(8,128)S(1)} %get-tuple-element.49, ...), kind=kLoop, calls=%fused_computation.137 | loop fusion | flops 8519680 | bytes 23511040 | tf_op jit(solution)/shard_map/sub | solution.py:88
  69.7 0.7 slice.408
  70.4 1.7 slice_subtract_fusion.6
  72.1 0.7 slice.409
  73.1 6.2 %fusion.87 = (f32[32,32,640]{2,1,0:T(8,128)S(1)}, f32[32,32,640]{2,1,0:T(8,128)S(1)}, f32[32,32,640]{2,1,0:T(8,128)S(1)}, f32[32,32,640]{2,1,0:T(8,128)}) fusion(f32[32,32,640]{2,1,0:T(8,128)S(1)} %get-tuple-element.46, f32[31,32,640]{2,1,0:T(8,128)} %slice_subtract_fusion.6, f32[2,32,32,640]{3,2,1,0:T(8,128)} %copy-done, ...), kind=kLoop, calls=%fused_computation.159 | loop fusion | flops 13107200 | bytes 31376032 | tf_op jit(solution)/shard_map/div | solution.py:50
  79.3 2.6 %fusion.128 = (f32[32,32,640]{2,1,0:T(8,128)S(1)}, f32[32,32,640]{2,1,0:T(8,128)S(1)}) fusion(f32[32,32,640]{2,1,0:T(8,128)} %get-tuple-element.43, f32[32,32,640]{2,1,0:T(8,128)S(1)} %get-tuple-element.41, f32[32,32,640]{2,1,0:T(8,128)S(1)} %get-tuple-element.42), kind=kLoop, calls=%fused_computation.187 | loop fusion | flops 1310720 | bytes 13107200 | tf_op jit(solution)/shard_map/div | solution.py:50
  82.4 1.6 copy-done.7
  84.0 5.2 %multiply_subtract_fusion.5 = (f32[32,32,640]{2,1,0:T(8,128)S(1)}, f32[32,32,640]{2,1,0:T(8,128)}) fusion(f32[32,32,640]{2,1,0:T(8,128)S(1)} %copy-done.7, f32[2,32,32,640]{3,2,1,0:T(8,128)} %copy-done, f32[32,32,640]{2,1,0:T(8,128)S(1)} %get-tuple-element.40, f32[31,32,640]{2,1,0:T(8,128)S(1)} %slice.417, f32[32,32,640]{2,1,0:T(8,128)S(1)} %get-tuple-element.64, ...), kind=kLoop, calls=%fused_computation.134 | loop fusion | flops 9175040 | bytes 26132480 | tf_op jit(solution)/shard_map/sub | solution.py:88
  89.2 0.7 slice.419
  90.0 1.7 slice_subtract_fusion.5
  91.7 0.7 slice.420
  92.7 6.2 %fusion.88 = (f32[32,32,640]{2,1,0:T(8,128)S(1)}, f32[32,32,640]{2,1,0:T(8,128)S(1)}, f32[32,32,640]{2,1,0:T(8,128)S(1)}, f32[32,32,640]{2,1,0:T(8,128)}) fusion(f32[32,32,640]{2,1,0:T(8,128)S(1)} %get-tuple-element.40, f32[31,32,640]{2,1,0:T(8,128)} %slice_subtract_fusion.5, f32[2,32,32,640]{3,2,1,0:T(8,128)} %copy-done, ...), kind=kLoop, calls=%fused_computation.160 | loop fusion | flops 13107200 | bytes 31376032 | tf_op jit(solution)/shard_map/div | solution.py:50
  98.9 2.6 %fusion.127 = (f32[32,32,640]{2,1,0:T(8,128)S(1)}, f32[32,32,640]{2,1,0:T(8,128)S(1)}) fusion(f32[32,32,640]{2,1,0:T(8,128)} %get-tuple-element.37, f32[32,32,640]{2,1,0:T(8,128)S(1)} %get-tuple-element.35, f32[32,32,640]{2,1,0:T(8,128)S(1)} %get-tuple-element.36), kind=kLoop, calls=%fused_computation.186 | loop fusion | flops 1310720 | bytes 13107200 | tf_op jit(solution)/shard_map/div | solution.py:50
  102.0 1.6 copy-done.2
  103.5 5.0 %multiply_subtract_fusion.4 = (f32[32,32,640]{2,1,0:T(8,128)S(1)}, f32[32,32,640]{2,1,0:T(8,128)}) fusion(f32[32,32,640]{2,1,0:T(8,128)S(1)} %copy-done.2, f32[2,32,32,640]{3,2,1,0:T(8,128)} %copy-done, f32[32,32,640]{2,1,0:T(8,128)S(1)} %get-tuple-element.34, f32[31,32,640]{2,1,0:T(8,128)S(1)} %slice.428, f32[32,32,640]{2,1,0:T(8,128)S(1)} %get-tuple-element.62, ...), kind=kLoop, calls=%fused_computation.131 | loop fusion | flops 9175040 | bytes 26132480 | tf_op jit(solution)/shard_map/sub | solution.py:88
  108.5 0.7 slice.430
  109.3 1.7 slice_subtract_fusion.4
  111.0 0.7 slice.431
  112.0 6.2 %fusion.89 = (f32[32,32,640]{2,1,0:T(8,128)S(1)}, f32[32,32,640]{2,1,0:T(8,128)S(1)}, f32[32,32,640]{2,1,0:T(8,128)S(1)}, f32[32,32,640]{2,1,0:T(8,128)}) fusion(f32[32,32,640]{2,1,0:T(8,128)S(1)} %get-tuple-element.34, f32[31,32,640]{2,1,0:T(8,128)} %slice_subtract_fusion.4, f32[2,32,32,640]{3,2,1,0:T(8,128)} %copy-done, ...), kind=kLoop, calls=%fused_computation.161 | loop fusion | flops 13107200 | bytes 31376032 | tf_op jit(solution)/shard_map/div | solution.py:50
  118.2 2.6 %fusion.126 = (f32[32,32,640]{2,1,0:T(8,128)S(1)}, f32[32,32,640]{2,1,0:T(8,128)S(1)}) fusion(f32[32,32,640]{2,1,0:T(8,128)} %get-tuple-element.31, f32[32,32,640]{2,1,0:T(8,128)S(1)} %get-tuple-element.29, f32[32,32,640]{2,1,0:T(8,128)S(1)} %get-tuple-element.30), kind=kLoop, calls=%fused_computation.185 | loop fusion | flops 1310720 | bytes 13107200 | tf_op jit(solution)/shard_map/div | solution.py:50
  121.3 1.6 copy-done.3
  122.8 5.1 %multiply_subtract_fusion.3 = (f32[32,32,640]{2,1,0:T(8,128)S(1)}, f32[32,32,640]{2,1,0:T(8,128)}) fusion(f32[32,32,640]{2,1,0:T(8,128)S(1)} %copy-done.3, f32[2,32,32,640]{3,2,1,0:T(8,128)} %copy-done, f32[32,32,640]{2,1,0:T(8,128)S(1)} %get-tuple-element.28, f32[31,32,640]{2,1,0:T(8,128)S(1)} %slice.439, f32[32,32,640]{2,1,0:T(8,128)S(1)} %get-tuple-element.60, ...), kind=kLoop, calls=%fused_computation.128 | loop fusion | flops 9175040 | bytes 26132480 | tf_op jit(solution)/shard_map/sub | solution.py:88
  127.9 0.7 slice.441
  128.7 1.7 slice_subtract_fusion.3
  130.4 0.7 slice.442
  131.4 6.4 %fusion.90 = (f32[32,32,640]{2,1,0:T(8,128)S(1)}, f32[32,32,640]{2,1,0:T(8,128)S(1)}, f32[32,32,640]{2,1,0:T(8,128)S(1)}, f32[32,32,640]{2,1,0:T(8,128)}) fusion(f32[32,32,640]{2,1,0:T(8,128)S(1)} %get-tuple-element.28, f32[31,32,640]{2,1,0:T(8,128)} %slice_subtract_fusion.3, f32[2,32,32,640]{3,2,1,0:T(8,128)} %copy-done, ...), kind=kLoop, calls=%fused_computation.162 | loop fusion | flops 13107200 | bytes 31376032 | tf_op jit(solution)/shard_map/div | solution.py:50
  137.8 2.6 %fusion.125 = (f32[32,32,640]{2,1,0:T(8,128)S(1)}, f32[32,32,640]{2,1,0:T(8,128)S(1)}) fusion(f32[32,32,640]{2,1,0:T(8,128)} %get-tuple-element.25, f32[32,32,640]{2,1,0:T(8,128)S(1)} %get-tuple-element.23, f32[32,32,640]{2,1,0:T(8,128)S(1)} %get-tuple-element.24), kind=kLoop, calls=%fused_computation.184 | loop fusion | flops 1310720 | bytes 13107200 | tf_op jit(solution)/shard_map/div | solution.py:50
  140.9 1.6 copy-done.4
  142.5 5.0 %multiply_subtract_fusion.2 = (f32[32,32,640]{2,1,0:T(8,128)S(1)}, f32[32,32,640]{2,1,0:T(8,128)}) fusion(f32[32,32,640]{2,1,0:T(8,128)S(1)} %copy-done.4, f32[2,32,32,640]{3,2,1,0:T(8,128)} %copy-done, f32[32,32,640]{2,1,0:T(8,128)S(1)} %get-tuple-element.22, f32[31,32,640]{2,1,0:T(8,128)S(1)} %slice.450, f32[32,32,640]{2,1,0:T(8,128)S(1)} %get-tuple-element.58, ...), kind=kLoop, calls=%fused_computation.125 | loop fusion | flops 9175040 | bytes 26132480 | tf_op jit(solution)/shard_map/sub | solution.py:88
  147.5 0.7 slice.452
  148.2 1.7 slice_subtract_fusion.2
  149.9 0.7 slice.453
  150.9 6.2 %fusion.91 = (f32[32,32,640]{2,1,0:T(8,128)S(1)}, f32[32,32,640]{2,1,0:T(8,128)S(1)}, f32[32,32,640]{2,1,0:T(8,128)S(1)}, f32[32,32,640]{2,1,0:T(8,128)}) fusion(f32[32,32,640]{2,1,0:T(8,128)S(1)} %get-tuple-element.22, f32[31,32,640]{2,1,0:T(8,128)} %slice_subtract_fusion.2, f32[2,32,32,640]{3,2,1,0:T(8,128)} %copy-done, ...), kind=kLoop, calls=%fused_computation.163 | loop fusion | flops 13107200 | bytes 31376032 | tf_op jit(solution)/shard_map/div | solution.py:50
  157.1 2.6 %fusion.124 = (f32[32,32,640]{2,1,0:T(8,128)S(1)}, f32[32,32,640]{2,1,0:T(8,128)S(1)}) fusion(f32[32,32,640]{2,1,0:T(8,128)} %get-tuple-element.19, f32[32,32,640]{2,1,0:T(8,128)S(1)} %get-tuple-element.17, f32[32,32,640]{2,1,0:T(8,128)S(1)} %get-tuple-element.18), kind=kLoop, calls=%fused_computation.183 | loop fusion | flops 1310720 | bytes 13107200 | tf_op jit(solution)/shard_map/div | solution.py:50
  160.2 1.6 copy-done.5
  161.8 5.1 %multiply_subtract_fusion.1 = (f32[32,32,640]{2,1,0:T(8,128)S(1)}, f32[32,32,640]{2,1,0:T(8,128)}) fusion(f32[32,32,640]{2,1,0:T(8,128)S(1)} %copy-done.5, f32[2,32,32,640]{3,2,1,0:T(8,128)} %copy-done, f32[32,32,640]{2,1,0:T(8,128)S(1)} %get-tuple-element.16, f32[31,32,640]{2,1,0:T(8,128)S(1)} %slice.461, f32[32,32,640]{2,1,0:T(8,128)S(1)} %get-tuple-element.56, ...), kind=kLoop, calls=%fused_computation.122 | loop fusion | flops 9175040 | bytes 26132480 | tf_op jit(solution)/shard_map/sub | solution.py:88
  166.9 0.8 slice.465
  167.7 1.7 slice_subtract_fusion.1
  169.4 0.7 slice.464
  170.4 6.5 %fusion.92 = (f32[32,32,640]{2,1,0:T(8,128)S(1)}, f32[32,32,640]{2,1,0:T(8,128)S(1)}, f32[32,32,640]{2,1,0:T(8,128)S(1)}, f32[32,32,640]{2,1,0:T(8,128)}) fusion(f32[32,32,640]{2,1,0:T(8,128)S(1)} %get-tuple-element.16, f32[31,32,640]{2,1,0:T(8,128)} %slice_subtract_fusion.1, f32[2,32,32,640]{3,2,1,0:T(8,128)} %copy-done, ...), kind=kLoop, calls=%fused_computation.164 | loop fusion | flops 13107200 | bytes 31376032 | tf_op jit(solution)/shard_map/div | solution.py:50
  177.0 2.5 %fusion.123 = (f32[32,32,640]{2,1,0:T(8,128)S(1)}, f32[32,32,640]{2,1,0:T(8,128)S(1)}) fusion(f32[32,32,640]{2,1,0:T(8,128)} %get-tuple-element.13, f32[32,32,640]{2,1,0:T(8,128)S(1)} %get-tuple-element.11, f32[32,32,640]{2,1,0:T(8,128)S(1)} %get-tuple-element.12), kind=kLoop, calls=%fused_computation.182 | loop fusion | flops 1310720 | bytes 13107200 | tf_op jit(solution)/shard_map/div | solution.py:50
  180.0 1.6 copy-done.6
  181.6 4.9 %multiply_subtract_fusion = (f32[32,32,640]{2,1,0:T(8,128)S(1)}, f32[32,32,640]{2,1,0:T(8,128)}) fusion(f32[32,32,640]{2,1,0:T(8,128)S(1)} %copy-done.6, f32[2,32,32,640]{3,2,1,0:T(8,128)} %copy-done, f32[32,32,640]{2,1,0:T(8,128)S(1)} %get-tuple-element.10, f32[31,32,640]{2,1,0:T(8,128)S(1)} %slice.472, f32[32,32,640]{2,1,0:T(8,128)S(1)} %get-tuple-element.54, ...), kind=kLoop, calls=%fused_computation.119 | loop fusion | flops 9175040 | bytes 26132480 | tf_op jit(solution)/shard_map/sub | solution.py:88
  186.8 2.3 %slice.475 = f32[32,32,639]{2,1,0:T(8,128)} slice(f32[32,32,640]{2,1,0:T(8,128)S(1)} %get-tuple-element.8), slice={[0:32], [0:32], [1:640]} | slice | bytes 5234688 | tf_op jit(solution)/shard_map/jit(_roll_static)/slice | solution.py:77
  189.1 1.7 slice.473
  190.9 0.5 slice-done
  191.4 0.5 slice-done.1
  191.9 7.3 %fusion.101 = (f32[32,32,640]{2,1,0:T(8,128)S(1)}, f32[32,32,640]{2,1,0:T(8,128)}, f32[32,32,640]{2,1,0:T(8,128)}, f32[32,32,640]{2,1,0:T(8,128)}) fusion(f32[2,32,32,640]{3,2,1,0:T(8,128)S(1)} %bitcast.81, f32[32,32,640]{2,1,0:T(8,128)S(1)} %get-tuple-element.10, f32[31,32,640]{2,1,0:T(8,128)S(1)} %slice_subtract_fusion, ...), kind=kLoop, calls=%fused_computation.180 | loop fusion | flops 13762560 | bytes 33997472 | tf_op jit(solution)/shard_map/div | solution.py:50
  199.2 7.5 %fusion.122 = (f32[32,32,640]{2,1,0:T(8,128)S(1)}, f32[32,32,640]{2,1,0:T(8,128)}, f32[32,32,640]{2,1,0:T(8,128)}) fusion(f32[32,32,640]{2,1,0:T(8,128)} %get-tuple-element.7, f32[32,32,640]{2,1,0:T(8,128)} %get-tuple-element.6, f32[32,32,640]{2,1,0:T(8,128)S(1)} %get-tuple-element.10, f32[31,32,640]{2,1,0:T(8,128)} %copy-done.1, ...), kind=kLoop, calls=%fused_computation.181 | loop fusion | flops 3932160 | bytes 23511040 | tf_op jit(solution)/shard_map/div | solution.py:50
  206.9 1.9 slice.483
  208.8 0.8 maximum_subtract_fusion.31
  209.6 3.9 %fusion.83 = f32[32,16,512]{2,1,0:T(8,128)} fusion(f32[32,32,640]{2,1,0:T(8,128)} %get-tuple-element.50, f32[32,32,640]{2,1,0:T(8,128)} %get-tuple-element.9, f32[31,32,640]{2,1,0:T(8,128)S(1)} %slice.483, f32[32,32,640]{2,1,0:T(8,128)} %get-tuple-element.52, f32[32,32,640]{2,1,0:T(8,128)S(1)} %maximum_subtract_fusion.31, f32[32,32,640]{2,1,0:T(8,128)} %get-tuple-element.69), kind=kLoop, calls=%fused_computation.152 | loop fusion | flops 2097152 | bytes 8830976 | tf_op jit(solution)/shard_map/div | solution.py:85
  (68 shorter events, 6.8 us)
Async XLA Ops:
  0.0 20.6 %copy-start.8 = (f32[32,16,512]{2,1,0:T(8,128)S(1)}, f32[32,16,512]{2,1,0:T(8,128)}, u32[]{:S(2)}) copy-start(f32[32,16,512]{2,1,0:T(8,128)} %param.3) | copy-start | bytes 3145732
  0.0 20.6 %copy-start.9 = (f32[32,16,512]{2,1,0:T(8,128)S(1)}, f32[32,16,512]{2,1,0:T(8,128)}, u32[]{:S(2)}) copy-start(f32[32,16,512]{2,1,0:T(8,128)} %param.2) | copy-start | bytes 3145732
  1.6 15.0 %collective-permute-start = (f32[2,32,16,8]{3,2,1,0:T(8,128)S(1)}, f32[2,32,16,8]{3,2,1,0:T(8,128)S(1)}, u32[]{:S(2)}, u32[]{:S(2)}) collective-permute-start(f32[2,32,16,8]{3,2,1,0:T(8,128)S(1)} %get-tuple-element.67), channel_id=1, source_target_pairs={{1,0},{2,1},{3,2},{4,3},{5,4},{6,5},{7,6},{0,7},{9,8},{10,9},{11,1... | collective-permute-start | bytes 98312 | tf_op jit(solution)/shard_map/ppermute | solution.py:17
  5.9 14.6 %collective-permute-start.1 = (f32[2,32,16,8]{3,2,1,0:T(8,128)S(1)}, f32[2,32,16,8]{3,2,1,0:T(8,128)S(1)}, u32[]{:S(2)}, u32[]{:S(2)}) collective-permute-start(f32[2,32,16,8]{3,2,1,0:T(8,128)S(1)} %get-tuple-element.68), channel_id=1, source_target_pairs={{7,0},{0,1},{1,2},{2,3},{3,4},{4,5},{5,6},{6,7},{15,8},{8,9},{9,10... | collective-permute-start | bytes 98312 | tf_op jit(solution)/shard_map/ppermute | solution.py:17
  20.6 0.8 copy-start.10
  23.0 34.0 %collective-permute-start.2 = (f32[2,32,8,640]{3,2,1,0:T(8,128)}, f32[2,32,8,640]{3,2,1,0:T(8,128)}, u32[]{:S(2)}, u32[]{:S(2)}) collective-permute-start(f32[2,32,8,640]{3,2,1,0:T(8,128)} %get-tuple-element.65), channel_id=1, source_target_pairs={{8,0},{16,8},{24,16},{32,24},{40,32},{48,40},{56,48},{64,56},{72,6... | collective-permute-start | bytes 3932168 | tf_op jit(solution)/shard_map/ppermute | solution.py:17
  24.8 32.2 %collective-permute-start.3 = (f32[2,32,8,640]{3,2,1,0:T(8,128)}, f32[2,32,8,640]{3,2,1,0:T(8,128)}, u32[]{:S(2)}, u32[]{:S(2)}) collective-permute-start(f32[2,32,8,640]{3,2,1,0:T(8,128)} %get-tuple-element.66), channel_id=1, source_target_pairs={{248,0},{0,8},{8,16},{16,24},{24,32},{32,40},{40,48},{48,56},{56,6... | collective-permute-start | bytes 3932168 | tf_op jit(solution)/shard_map/ppermute | solution.py:17
  59.4 6.9 %copy-start = (f32[2,32,32,640]{3,2,1,0:T(8,128)}, f32[2,32,32,640]{3,2,1,0:T(8,128)S(1)}, u32[]{:S(2)}) copy-start(f32[2,32,32,640]{3,2,1,0:T(8,128)S(1)} %pad_maximum_fusion) | copy-start | bytes 15728644
  82.2 1.7 copy-start.7
  101.8 1.7 copy-start.2
  121.1 1.7 copy-start.3
  140.7 1.7 copy-start.4
  160.0 1.7 copy-start.5
  179.8 1.7 copy-start.6
  186.6 4.8 %slice-start = ((s8[5242880]{0:T(1024)(128)(4,1)}), s8[4194304]{0:T(1024)(128)(4,1)S(1)}, s32[]{:S(2)}) async-start(s8[5242880]{0:T(1024)(128)(4,1)} %bitcast.80), calls=%async_computation | async-start | bytes 8388608
  186.8 4.1 %copy-start.1 = (f32[31,32,640]{2,1,0:T(8,128)}, f32[31,32,640]{2,1,0:T(8,128)S(1)}, u32[]{:S(2)}) copy-start(f32[31,32,640]{2,1,0:T(8,128)S(1)} %slice_subtract_fusion) | copy-start | bytes 7618564
  186.8 5.1 %slice-start.1 = ((s8[5242880]{0:T(1024)(128)(4,1)}), s8[1048576]{0:T(1024)(128)(4,1)S(1)}, s32[]{:S(2)}) async-start(s8[5242880]{0:T(1024)(128)(4,1)} %bitcast.80), calls=%async_computation.1 | async-start | bytes 2097152

commit v2 on v1

--- a/solution.py
+++ b/solution.py
@@ -1,6 +1,10 @@
+import functools
+
 import jax
 import jax.numpy as jnp
 from jax import lax
+from jax.experimental import pallas as pl
+from jax.experimental.pallas import tpu as pltpu
 from jax.sharding import PartitionSpec as P
 
 ITERS = 8
@@ -34,14 +38,46 @@
     return full[0], full[1], width
 
 
-def along_z(field):
-    edge = jnp.zeros_like(field[:1])
-    return jnp.concatenate([field[1:] - field[:-1], edge], 0)
+def iterate_kernel(noisy_ref, weight_ref, keep_x_ref, keep_y_ref, out_ref, primal, extrapolated, dual_x, dual_y, dual_z):
+    planes, rows, width = noisy_ref.shape
+    primal[...] = noisy_ref[...]
+    extrapolated[...] = noisy_ref[...]
+    dual_x[...] = jnp.zeros_like(noisy_ref)
+    dual_y[...] = jnp.zeros_like(noisy_ref)
+    dual_z[...] = jnp.zeros_like(noisy_ref)
+    keep_x = keep_x_ref[...] > 0.5
+    keep_y = keep_y_ref[...] > 0.5
 
+    def plane(z, dual_z_before):
+        here = extrapolated[z]
+        after = extrapolated[jnp.minimum(z + 1, planes - 1)]
+        slope_x = jnp.where(keep_x, pltpu.roll(here, rows - 1, 0) - here, 0.0)
+        slope_y = jnp.where(keep_y, pltpu.roll(here, width - 1, 1) - here, 0.0)
+        slope_z = jnp.where(z < planes - 1, after - here, 0.0)
+        new_x, new_y, new_z = project(
+            dual_x[z] + dual_step * slope_x,
+            dual_y[z] + dual_step * slope_y,
+            dual_z[z] + dual_step * slope_z,
+            weight_ref[z],
+        )
+        dual_x[z] = new_x
+        dual_y[z] = new_y
+        dual_z[z] = new_z
+        divergence = (
+            (new_x - pltpu.roll(new_x, 1, 0)) + (new_y - pltpu.roll(new_y, 1, 1)) + (new_z - dual_z_before)
+        )
+        old = primal[z]
+        updated = (old + primal_step * divergence + primal_step * fidelity * noisy_ref[z]) / (
+            1.0 + primal_step * fidelity
+        )
+        extrapolated[z] = 2.0 * updated - old
+        primal[z] = updated
+        return new_z
 
-def back_z(dual):
-    edge = jnp.zeros_like(dual[:1])
-    return dual - jnp.concatenate([edge, dual[:-1]], 0)
+    for iteration in range(ITERS):
+        lax.fori_loop(0, planes, plane, jnp.zeros((rows, width), jnp.float32))
+    own_rows, own_cols = out_ref.shape[1:]
+    out_ref[...] = primal[:, :own_rows, :own_cols]
 
 
 def project(dual_x, dual_y, dual_z, weight):
@@ -61,33 +97,24 @@
 
     local_x = jnp.arange(ext_x, dtype=jnp.int32)
     index_x = jnp.where(local_x >= rows_x + HALO, start_x + local_x - ext_x, start_x + local_x)
-    keep_x = ((index_x >= 0) & (index_x < total_x - 1))[None, :, None]
+    keep_x = (index_x >= 0) & (index_x < total_x - 1)
     local_y = jnp.arange(width, dtype=jnp.int32)
     index_y = jnp.where(local_y >= width - HALO, start_y + local_y - width, start_y + local_y)
     inside_y = (local_y < rows_y + HALO) | (local_y >= width - HALO)
-    keep_y = (inside_y & (index_y >= 0) & (index_y < total_y - 1))[None, None, :]
+    keep_y = inside_y & (index_y >= 0) & (index_y < total_y - 1)
+    keep_x = jnp.broadcast_to(keep_x[:, None], (ext_x, width)).astype(jnp.float32)
+    keep_y = jnp.broadcast_to(keep_y[None, :], (ext_x, width)).astype(jnp.float32)
 
-    primal = noisy_e
-    extrapolated = noisy_e
-    dual_x = jnp.zeros_like(noisy_e)
-    dual_y = jnp.zeros_like(noisy_e)
-    dual_z = jnp.zeros_like(noisy_e)
-    for iteration in range(ITERS):
-        slope_x = jnp.where(keep_x, jnp.roll(extrapolated, -1, 1) - extrapolated, 0.0)
-        slope_y = jnp.where(keep_y, jnp.roll(extrapolated, -1, 2) - extrapolated, 0.0)
-        dual_x = dual_x + dual_step * slope_x
-        dual_y = dual_y + dual_step * slope_y
-        dual_z = dual_z + dual_step * along_z(extrapolated)
-        dual_x, dual_y, dual_z = project(dual_x, dual_y, dual_z, weight_e)
-        diverge_x = dual_x - jnp.roll(dual_x, 1, 1)
-        diverge_y = dual_y - jnp.roll(dual_y, 1, 2)
-        divergence = diverge_x + diverge_y + back_z(dual_z)
-        updated = (primal + primal_step * divergence + primal_step * fidelity * noisy_e) / (
-            1.0 + primal_step * fidelity
-        )
-        extrapolated = 2.0 * updated - primal
-        primal = updated
-    return primal[:, :rows_x, :rows_y]
+    field = jax.ShapeDtypeStruct((planes, ext_x, width), jnp.float32)
+    vmem = pl.BlockSpec(memory_space=pltpu.VMEM)
+    return pl.pallas_call(
+        iterate_kernel,
+        out_shape=jax.ShapeDtypeStruct(noisy.shape, jnp.float32),
+        in_specs=[vmem] * 4,
+        out_specs=vmem,
+        scratch_shapes=[pltpu.VMEM(field.shape, jnp.float32)] * 5,
+        compiler_params=pltpu.CompilerParams(vmem_limit_bytes=48 * 1024 * 1024),
+    )(noisy_e, weight_e, keep_x, keep_y)
 
 
 def solution(mesh):

time: 218 us -> 123 us (0.56); the launches traced: 214 us -> 123 us
  other arithmetic: 127 us -> 4.45 us
  Pallas kernels: 0 us -> 63 us
  local copies, waits for them, and re-layouts: 33.4 us -> 2.39 us
    div x17 -> x0, other arithmetic: 76.9 us -> none  [the longest x16 73.1 us: project(): return (dual_x / factor, dual_y / factor, dual_z / factor)]
    pallas_call x0 -> x1, Pallas kernels: none -> 63 us  [per_device(): pl.pallas_call(iterate_kernel, out_shape=jax.ShapeDtypeStruct(noisy.shape...]
    sub x16 -> x0, other arithmetic: 45.2 us -> none  [the longest x7 33.7 us: per_device(): extrapolated = 2.0 * updated - primal]
    slice x56 -> x0, local copies, waits for them, and re-layouts: 20.9 us -> none  [the longest x16 8.59 us: per_device(): jnp.roll(extrapolated, -1, 2) - extrapolated]
    unnamed x26 -> x6, local copies, waits for them, and re-layouts: 10.7 us -> 0.25 us
where the time goes in v2:
time: 123 us
  Pallas kernels  63 us (51%)
  waiting for transfers between devices  44.3 us (36%)
  starting transfers between devices  8.71 us (7%)
  other arithmetic  4.45 us (4%)
  local copies, waits for them, and re-layouts  2.39 us (2%)
    pallas_call x1, Pallas kernels, per_device(): pl.pallas_call(iterate_kernel, out_shape=jax.ShapeDtypeStruct(noisy.shape...  63 us
    ppermute x4, waiting for transfers between devices, from_offset(): lax.ppermute(value, axis, [((dest + offset) % count, dest) for dest in ra...  44.3 us
    ppermute x4, starting transfers between devices, from_offset(): lax.ppermute(value, axis, [((dest + offset) % count, dest) for dest in ra...  8.71 us
  transfers between devices with their start and end apart: 4, of which 3 were waited for; matrix products, arithmetic and copies ran while one was open for 0% of the time, Pallas kernels for 0%

profile of v2, /device:TPU:1, one launch (start us, length us, event | category | flops | bytes accessed | tf_op | source)
XLA Modules:
  0.0 122.9 jit_solution(2278153024013633401)
XLA Ops:
  0.0 0.0 copy-start.1
  0.0 0.0 copy-start
  0.0 1.6 %pad_maximum_fusion.3 = (f32[2,32,16,8]{3,2,1,0:T(8,128)S(1)}, f32[2,32,16,8]{3,2,1,0:T(8,128)S(1)}) fusion(f32[1,32,16,512]{3,2,1,0:T(8,128)} %bitcast.6, f32[1,32,16,512]{3,2,1,0:T(8,128)} %bitcast.9), kind=kLoop, calls=%fused_computation.5 | loop fusion | flops 16384 | bytes 2162688 | tf_op jit(solution)/shard_map/slice | solution.py:28
  1.6 4.4 %collective-permute-start = (f32[2,32,16,8]{3,2,1,0:T(8,128)S(1)}, f32[2,32,16,8]{3,2,1,0:T(8,128)S(1)}, u32[]{:S(2)}, u32[]{:S(2)}) collective-permute-start(f32[2,32,16,8]{3,2,1,0:T(8,128)S(1)} %get-tuple-element.9), channel_id=1, source_target_pairs={{1,0},{2,1},{3,2},{4,3},{5,4},{6,5},{7,6},{0,7},{9,8},{10,9},{11,1... | collective-permute-start | bytes 98312 | tf_op jit(solution)/shard_map/ppermute | solution.py:21
  5.9 0.0 collective-permute-start.1
  5.9 10.6 %collective-permute-done = f32[2,32,16,8]{3,2,1,0:T(8,128)S(1)} collective-permute-done((f32[2,32,16,8]{3,2,1,0:T(8,128)S(1)}, f32[2,32,16,8]{3,2,1,0:T(8,128)S(1)}, u32[]{:S(2)}, u32[]{:S(2)}) %collective-permute-start) | collective-permute-done | bytes 32800 | tf_op jit(solution)/shard_map/ppermute | solution.py:21
  16.6 4.0 %collective-permute-done.1 = f32[2,32,16,8]{3,2,1,0:T(8,128)S(1)} collective-permute-done((f32[2,32,16,8]{3,2,1,0:T(8,128)S(1)}, f32[2,32,16,8]{3,2,1,0:T(8,128)S(1)}, u32[]{:S(2)}, u32[]{:S(2)}) %collective-permute-start.1) | collective-permute-done | bytes 32800 | tf_op jit(solution)/shard_map/ppermute | solution.py:21
  20.6 0.0 copy-start.2
  20.6 0.0 copy-done.1
  20.6 0.0 copy-done
  20.6 0.5 pad_maximum_fusion.1
  21.1 0.2 copy-done.2
  21.4 1.7 %fusion.6 = (f32[2,32,8,640]{3,2,1,0:T(8,128)}, f32[2,32,8,640]{3,2,1,0:T(8,128)}) fusion(f32[2,32,16,640]{3,2,1,0:T(8,128)S(1)} %pad_maximum_fusion.1), kind=kLoop, calls=%fused_computation.17 | loop fusion | bytes 5242880 | tf_op jit(solution)/shard_map/slice | solution.py:35
  23.1 1.8 %collective-permute-start.2 = (f32[2,32,8,640]{3,2,1,0:T(8,128)}, f32[2,32,8,640]{3,2,1,0:T(8,128)}, u32[]{:S(2)}, u32[]{:S(2)}) collective-permute-start(f32[2,32,8,640]{3,2,1,0:T(8,128)} %get-tuple-element.7), channel_id=1, source_target_pairs={{8,0},{16,8},{24,16},{32,24},{40,32},{48,40},{56,48},{64,56},{72,6... | collective-permute-start | bytes 3932168 | tf_op jit(solution)/shard_map/ppermute | solution.py:21
  24.9 2.5 %collective-permute-start.3 = (f32[2,32,8,640]{3,2,1,0:T(8,128)}, f32[2,32,8,640]{3,2,1,0:T(8,128)}, u32[]{:S(2)}, u32[]{:S(2)}) collective-permute-start(f32[2,32,8,640]{3,2,1,0:T(8,128)} %get-tuple-element.8), channel_id=1, source_target_pairs={{248,0},{0,8},{8,16},{16,24},{24,32},{32,40},{40,48},{48,56},{56,6... | collective-permute-start | bytes 3932168 | tf_op jit(solution)/shard_map/ppermute | solution.py:21
  27.4 29.6 %collective-permute-done.2 = f32[2,32,8,640]{3,2,1,0:T(8,128)} collective-permute-done((f32[2,32,8,640]{3,2,1,0:T(8,128)}, f32[2,32,8,640]{3,2,1,0:T(8,128)}, u32[]{:S(2)}, u32[]{:S(2)}) %collective-permute-start.2) | collective-permute-done | bytes 1310752 | tf_op jit(solution)/shard_map/ppermute | solution.py:21
  57.0 0.0 collective-permute-done.3
  57.0 2.4 %pad_maximum_fusion = f32[2,32,32,640]{3,2,1,0:T(8,128)S(1)} fusion(f32[2,32,8,640]{3,2,1,0:T(8,128)} %collective-permute-done.3, f32[2,32,8,640]{3,2,1,0:T(8,128)} %collective-permute-done.2, f32[2,32,16,8]{3,2,1,0:T(8,128)} %copy-done.2, f32[2,32,16,112]{3,2,1,0:T(8,128)S(1)} %concatenate.9, f32[2,32,16,8]{3,2,1,0:T(8,128)S(1)} %collective-permute-done, ...), kind=kLoop, calls=%fused_computation | loop fusion | flops 7864320 | bytes 10485760 | tf_op jit(solution)/shard_map/concatenate | solution.py:37
  59.4 0.3 slice_bitcast_fusion
  59.8 0.1 broadcast_in_dim.4.keep_x_ref
  59.9 63.0 %shard_map.28 = f32[32,16,512]{2,1,0:T(8,128)} custom-call(f32[32,32,640]{2,1,0:T(8,128)S(1)} %get-tuple-element.6.noisy_ref, f32[32,32,640]{2,1,0:T(8,128)S(1)} %get-tuple-element.5.weight_ref, f32[32,640]{1,0:T(8,128)S(1)} %broadcast_in_dim.4.keep_x_ref, f32[32,640]{1,0:T(8,128)S(1)} %broadcast_in_dim.5.keep_y_ref), custom_call_target="tpu_custom_call" | custom-call | tf_op jit(solution)/shard_map/pallas_call | solution.py:110
  (4 shorter events, 0.1 us)
Async XLA Ops:
  0.0 20.6 %copy-start.1 = (f32[32,16,512]{2,1,0:T(8,128)S(1)}, f32[32,16,512]{2,1,0:T(8,128)}, u32[]{:S(2)}) copy-start(f32[32,16,512]{2,1,0:T(8,128)} %param.2) | copy-start | bytes 3145732
  0.0 20.6 %copy-start = (f32[32,16,512]{2,1,0:T(8,128)S(1)}, f32[32,16,512]{2,1,0:T(8,128)}, u32[]{:S(2)}) copy-start(f32[32,16,512]{2,1,0:T(8,128)} %param.3) | copy-start | bytes 3145732
  1.6 15.0 %collective-permute-start = (f32[2,32,16,8]{3,2,1,0:T(8,128)S(1)}, f32[2,32,16,8]{3,2,1,0:T(8,128)S(1)}, u32[]{:S(2)}, u32[]{:S(2)}) collective-permute-start(f32[2,32,16,8]{3,2,1,0:T(8,128)S(1)} %get-tuple-element.9), channel_id=1, source_target_pairs={{1,0},{2,1},{3,2},{4,3},{5,4},{6,5},{7,6},{0,7},{9,8},{10,9},{11,1... | collective-permute-start | bytes 98312 | tf_op jit(solution)/shard_map/ppermute | solution.py:21
  5.9 14.6 %collective-permute-start.1 = (f32[2,32,16,8]{3,2,1,0:T(8,128)S(1)}, f32[2,32,16,8]{3,2,1,0:T(8,128)S(1)}, u32[]{:S(2)}, u32[]{:S(2)}) collective-permute-start(f32[2,32,16,8]{3,2,1,0:T(8,128)S(1)} %get-tuple-element.10), channel_id=1, source_target_pairs={{7,0},{0,1},{1,2},{2,3},{3,4},{4,5},{5,6},{6,7},{15,8},{8,9},{9,10... | collective-permute-start | bytes 98312 | tf_op jit(solution)/shard_map/ppermute | solution.py:21
  20.6 0.8 copy-start.2
  23.1 34.0 %collective-permute-start.2 = (f32[2,32,8,640]{3,2,1,0:T(8,128)}, f32[2,32,8,640]{3,2,1,0:T(8,128)}, u32[]{:S(2)}, u32[]{:S(2)}) collective-permute-start(f32[2,32,8,640]{3,2,1,0:T(8,128)} %get-tuple-element.7), channel_id=1, source_target_pairs={{8,0},{16,8},{24,16},{32,24},{40,32},{48,40},{56,48},{64,56},{72,6... | collective-permute-start | bytes 3932168 | tf_op jit(solution)/shard_map/ppermute | solution.py:21
  24.9 32.2 %collective-permute-start.3 = (f32[2,32,8,640]{3,2,1,0:T(8,128)}, f32[2,32,8,640]{3,2,1,0:T(8,128)}, u32[]{:S(2)}, u32[]{:S(2)}) collective-permute-start(f32[2,32,8,640]{3,2,1,0:T(8,128)} %get-tuple-element.8), channel_id=1, source_target_pairs={{248,0},{0,8},{8,16},{16,24},{24,32},{32,40},{40,48},{48,56},{56,6... | collective-permute-start | bytes 3932168 | tf_op jit(solution)/shard_map/ppermute | solution.py:21

commit v3 on v2

--- a/solution.py
+++ b/solution.py
@@ -38,7 +38,9 @@
     return full[0], full[1], width
 
 
-def iterate_kernel(noisy_ref, weight_ref, keep_x_ref, keep_y_ref, out_ref, primal, extrapolated, dual_x, dual_y, dual_z):
+def iterate_kernel(
+    noisy_ref, weight_ref, keep_x_ref, keep_y_ref, out_ref, primal, extrapolated, dual_x, dual_y, dual_z, inverse_weight
+):
     planes, rows, width = noisy_ref.shape
     primal[...] = noisy_ref[...]
     extrapolated[...] = noisy_ref[...]
@@ -47,6 +49,8 @@
     dual_z[...] = jnp.zeros_like(noisy_ref)
     keep_x = keep_x_ref[...] > 0.5
     keep_y = keep_y_ref[...] > 0.5
+    inverse_weight[...] = 1.0 / weight_ref[...]
+    shrink = 1.0 / (1.0 + primal_step * fidelity)
 
     def plane(z, dual_z_before):
         here = extrapolated[z]
@@ -58,7 +62,7 @@
             dual_x[z] + dual_step * slope_x,
             dual_y[z] + dual_step * slope_y,
             dual_z[z] + dual_step * slope_z,
-            weight_ref[z],
+            inverse_weight[z],
         )
         dual_x[z] = new_x
         dual_y[z] = new_y
@@ -67,9 +71,7 @@
             (new_x - pltpu.roll(new_x, 1, 0)) + (new_y - pltpu.roll(new_y, 1, 1)) + (new_z - dual_z_before)
         )
         old = primal[z]
-        updated = (old + primal_step * divergence + primal_step * fidelity * noisy_ref[z]) / (
-            1.0 + primal_step * fidelity
-        )
+        updated = (old + primal_step * divergence + primal_step * fidelity * noisy_ref[z]) * shrink
         extrapolated[z] = 2.0 * updated - old
         primal[z] = updated
         return new_z
@@ -80,10 +82,10 @@
     out_ref[...] = primal[:, :own_rows, :own_cols]
 
 
-def project(dual_x, dual_y, dual_z, weight):
+def project(dual_x, dual_y, dual_z, inverse_weight):
     length = jnp.sqrt(dual_x * dual_x + dual_y * dual_y + dual_z * dual_z)
-    factor = jnp.maximum(1.0, length / weight)
-    return (dual_x / factor, dual_y / factor, dual_z / factor)
+    scale = 1.0 / jnp.maximum(1.0, length * inverse_weight)
+    return (dual_x * scale, dual_y * scale, dual_z * scale)
 
 
 def per_device(noisy, weight):
@@ -112,7 +114,7 @@
         out_shape=jax.ShapeDtypeStruct(noisy.shape, jnp.float32),
         in_specs=[vmem] * 4,
         out_specs=vmem,
-        scratch_shapes=[pltpu.VMEM(field.shape, jnp.float32)] * 5,
+        scratch_shapes=[pltpu.VMEM(field.shape, jnp.float32)] * 6,
         compiler_params=pltpu.CompilerParams(vmem_limit_bytes=48 * 1024 * 1024),
     )(noisy_e, weight_e, keep_x, keep_y)
 

time: 123 us -> 123 us (level)
  no operation moved by 1% of the time
where the time goes in v3:
time: 123 us
  Pallas kernels  63.4 us (52%)
  waiting for transfers between devices  44.3 us (36%)
  starting transfers between devices  8.71 us (7%)
  other arithmetic  4.45 us (4%)
  local copies, waits for them, and re-layouts  2.39 us (2%)
    pallas_call x1, Pallas kernels, per_device(): pl.pallas_call(iterate_kernel, out_shape=jax.ShapeDtypeStruct(noisy.shape...  63.4 us
    ppermute x4, waiting for transfers between devices, from_offset(): lax.ppermute(value, axis, [((dest + offset) % count, dest) for dest in ra...  44.3 us
    ppermute x4, starting transfers between devices, from_offset(): lax.ppermute(value, axis, [((dest + offset) % count, dest) for dest in ra...  8.71 us
  transfers between devices with their start and end apart: 4, of which 3 were waited for; matrix products, arithmetic and copies ran while one was open for 0% of the time, Pallas kernels for 0%

profile of v3, /device:TPU:1, one launch (start us, length us, event | category | flops | bytes accessed | tf_op | source)
XLA Modules:
  0.0 123.3 jit_solution(16164261239345430277)
XLA Ops:
  0.0 0.0 copy-start.1
  0.0 0.0 copy-start
  0.0 1.6 %pad_maximum_fusion.3 = (f32[2,32,16,8]{3,2,1,0:T(8,128)S(1)}, f32[2,32,16,8]{3,2,1,0:T(8,128)S(1)}) fusion(f32[1,32,16,512]{3,2,1,0:T(8,128)} %bitcast.6, f32[1,32,16,512]{3,2,1,0:T(8,128)} %bitcast.9), kind=kLoop, calls=%fused_computation.5 | loop fusion | flops 16384 | bytes 2162688 | tf_op jit(solution)/shard_map/slice | solution.py:28
  1.6 4.4 %collective-permute-start = (f32[2,32,16,8]{3,2,1,0:T(8,128)S(1)}, f32[2,32,16,8]{3,2,1,0:T(8,128)S(1)}, u32[]{:S(2)}, u32[]{:S(2)}) collective-permute-start(f32[2,32,16,8]{3,2,1,0:T(8,128)S(1)} %get-tuple-element.9), channel_id=1, source_target_pairs={{1,0},{2,1},{3,2},{4,3},{5,4},{6,5},{7,6},{0,7},{9,8},{10,9},{11,1... | collective-permute-start | bytes 98312 | tf_op jit(solution)/shard_map/ppermute | solution.py:21
  5.9 0.0 collective-permute-start.1
  5.9 10.6 %collective-permute-done = f32[2,32,16,8]{3,2,1,0:T(8,128)S(1)} collective-permute-done((f32[2,32,16,8]{3,2,1,0:T(8,128)S(1)}, f32[2,32,16,8]{3,2,1,0:T(8,128)S(1)}, u32[]{:S(2)}, u32[]{:S(2)}) %collective-permute-start) | collective-permute-done | bytes 32800 | tf_op jit(solution)/shard_map/ppermute | solution.py:21
  16.6 4.0 %collective-permute-done.1 = f32[2,32,16,8]{3,2,1,0:T(8,128)S(1)} collective-permute-done((f32[2,32,16,8]{3,2,1,0:T(8,128)S(1)}, f32[2,32,16,8]{3,2,1,0:T(8,128)S(1)}, u32[]{:S(2)}, u32[]{:S(2)}) %collective-permute-start.1) | collective-permute-done | bytes 32800 | tf_op jit(solution)/shard_map/ppermute | solution.py:21
  20.6 0.0 copy-start.2
  20.6 0.0 copy-done.1
  20.6 0.0 copy-done
  20.6 0.5 pad_maximum_fusion.1
  21.1 0.2 copy-done.2
  21.4 1.7 %fusion.6 = (f32[2,32,8,640]{3,2,1,0:T(8,128)}, f32[2,32,8,640]{3,2,1,0:T(8,128)}) fusion(f32[2,32,16,640]{3,2,1,0:T(8,128)S(1)} %pad_maximum_fusion.1), kind=kLoop, calls=%fused_computation.17 | loop fusion | bytes 5242880 | tf_op jit(solution)/shard_map/slice | solution.py:35
  23.1 1.8 %collective-permute-start.2 = (f32[2,32,8,640]{3,2,1,0:T(8,128)}, f32[2,32,8,640]{3,2,1,0:T(8,128)}, u32[]{:S(2)}, u32[]{:S(2)}) collective-permute-start(f32[2,32,8,640]{3,2,1,0:T(8,128)} %get-tuple-element.7), channel_id=1, source_target_pairs={{8,0},{16,8},{24,16},{32,24},{40,32},{48,40},{56,48},{64,56},{72,6... | collective-permute-start | bytes 3932168 | tf_op jit(solution)/shard_map/ppermute | solution.py:21
  24.9 2.5 %collective-permute-start.3 = (f32[2,32,8,640]{3,2,1,0:T(8,128)}, f32[2,32,8,640]{3,2,1,0:T(8,128)}, u32[]{:S(2)}, u32[]{:S(2)}) collective-permute-start(f32[2,32,8,640]{3,2,1,0:T(8,128)} %get-tuple-element.8), channel_id=1, source_target_pairs={{248,0},{0,8},{8,16},{16,24},{24,32},{32,40},{40,48},{48,56},{56,6... | collective-permute-start | bytes 3932168 | tf_op jit(solution)/shard_map/ppermute | solution.py:21
  27.4 29.6 %collective-permute-done.2 = f32[2,32,8,640]{3,2,1,0:T(8,128)} collective-permute-done((f32[2,32,8,640]{3,2,1,0:T(8,128)}, f32[2,32,8,640]{3,2,1,0:T(8,128)}, u32[]{:S(2)}, u32[]{:S(2)}) %collective-permute-start.2) | collective-permute-done | bytes 1310752 | tf_op jit(solution)/shard_map/ppermute | solution.py:21
  57.0 0.0 collective-permute-done.3
  57.0 2.4 %pad_maximum_fusion = f32[2,32,32,640]{3,2,1,0:T(8,128)S(1)} fusion(f32[2,32,8,640]{3,2,1,0:T(8,128)} %collective-permute-done.3, f32[2,32,8,640]{3,2,1,0:T(8,128)} %collective-permute-done.2, f32[2,32,16,8]{3,2,1,0:T(8,128)} %copy-done.2, f32[2,32,16,112]{3,2,1,0:T(8,128)S(1)} %concatenate.9, f32[2,32,16,8]{3,2,1,0:T(8,128)S(1)} %collective-permute-done, ...), kind=kLoop, calls=%fused_computation | loop fusion | flops 7864320 | bytes 10485760 | tf_op jit(solution)/shard_map/concatenate | solution.py:37
  59.4 0.3 slice_bitcast_fusion
  59.8 0.1 broadcast_in_dim.4.keep_x_ref
  59.9 63.4 %shard_map.28 = f32[32,16,512]{2,1,0:T(8,128)} custom-call(f32[32,32,640]{2,1,0:T(8,128)S(1)} %get-tuple-element.6.noisy_ref, f32[32,32,640]{2,1,0:T(8,128)S(1)} %get-tuple-element.5.weight_ref, f32[32,640]{1,0:T(8,128)S(1)} %broadcast_in_dim.4.keep_x_ref, f32[32,640]{1,0:T(8,128)S(1)} %broadcast_in_dim.5.keep_y_ref), custom_call_target="tpu_custom_call" | custom-call | tf_op jit(solution)/shard_map/pallas_call | solution.py:112
  (4 shorter events, 0.1 us)
Async XLA Ops:
  0.0 20.6 %copy-start.1 = (f32[32,16,512]{2,1,0:T(8,128)S(1)}, f32[32,16,512]{2,1,0:T(8,128)}, u32[]{:S(2)}) copy-start(f32[32,16,512]{2,1,0:T(8,128)} %param.2) | copy-start | bytes 3145732
  0.0 20.6 %copy-start = (f32[32,16,512]{2,1,0:T(8,128)S(1)}, f32[32,16,512]{2,1,0:T(8,128)}, u32[]{:S(2)}) copy-start(f32[32,16,512]{2,1,0:T(8,128)} %param.3) | copy-start | bytes 3145732
  1.6 15.0 %collective-permute-start = (f32[2,32,16,8]{3,2,1,0:T(8,128)S(1)}, f32[2,32,16,8]{3,2,1,0:T(8,128)S(1)}, u32[]{:S(2)}, u32[]{:S(2)}) collective-permute-start(f32[2,32,16,8]{3,2,1,0:T(8,128)S(1)} %get-tuple-element.9), channel_id=1, source_target_pairs={{1,0},{2,1},{3,2},{4,3},{5,4},{6,5},{7,6},{0,7},{9,8},{10,9},{11,1... | collective-permute-start | bytes 98312 | tf_op jit(solution)/shard_map/ppermute | solution.py:21
  5.9 14.6 %collective-permute-start.1 = (f32[2,32,16,8]{3,2,1,0:T(8,128)S(1)}, f32[2,32,16,8]{3,2,1,0:T(8,128)S(1)}, u32[]{:S(2)}, u32[]{:S(2)}) collective-permute-start(f32[2,32,16,8]{3,2,1,0:T(8,128)S(1)} %get-tuple-element.10), channel_id=1, source_target_pairs={{7,0},{0,1},{1,2},{2,3},{3,4},{4,5},{5,6},{6,7},{15,8},{8,9},{9,10... | collective-permute-start | bytes 98312 | tf_op jit(solution)/shard_map/ppermute | solution.py:21
  20.6 0.8 copy-start.2
  23.1 34.0 %collective-permute-start.2 = (f32[2,32,8,640]{3,2,1,0:T(8,128)}, f32[2,32,8,640]{3,2,1,0:T(8,128)}, u32[]{:S(2)}, u32[]{:S(2)}) collective-permute-start(f32[2,32,8,640]{3,2,1,0:T(8,128)} %get-tuple-element.7), channel_id=1, source_target_pairs={{8,0},{16,8},{24,16},{32,24},{40,32},{48,40},{56,48},{64,56},{72,6... | collective-permute-start | bytes 3932168 | tf_op jit(solution)/shard_map/ppermute | solution.py:21
  24.9 32.2 %collective-permute-start.3 = (f32[2,32,8,640]{3,2,1,0:T(8,128)}, f32[2,32,8,640]{3,2,1,0:T(8,128)}, u32[]{:S(2)}, u32[]{:S(2)}) collective-permute-start(f32[2,32,8,640]{3,2,1,0:T(8,128)} %get-tuple-element.8), channel_id=1, source_target_pairs={{248,0},{0,8},{8,16},{16,24},{24,32},{32,40},{40,48},{48,56},{56,6... | collective-permute-start | bytes 3932168 | tf_op jit(solution)/shard_map/ppermute | solution.py:21

commit v4 on v3

--- a/solution.py
+++ b/solution.py
@@ -16,25 +16,47 @@
 fidelity = 1.0
 
 
-def from_offset(value, axis, offset):
-    count = lax.axis_size(axis)
-    return lax.ppermute(value, axis, [((dest + offset) % count, dest) for dest in range(count)])
+def from_offset(value, step_x, step_y):
+    count_x, count_y = lax.axis_size("gx"), lax.axis_size("gy")
+    pairs = []
+    for dest_x in range(count_x):
+        for dest_y in range(count_y):
+            source = ((dest_x + step_x) % count_x) * count_y + (dest_y + step_y) % count_y
+            pairs.append((source, dest_x * count_y + dest_y))
+    axes = tuple(name for name, step in (("gx", step_x), ("gy", step_y)) if step)
+    if len(axes) == 1:
+        pairs = [(source % count_y, dest % count_y) if axes == ("gy",) else (source // count_y, dest // count_y)
+                 for source, dest in pairs]
+        pairs = sorted(set(pairs))
+        return lax.ppermute(value, axes[0], pairs)
+    return lax.ppermute(value, axes, pairs)
 
 
 def extend(noisy, weight):
     planes, rows, cols = noisy.shape
     width = -(-(cols + 2 * HALO) // 128) * 128
     both = jnp.stack([noisy, weight])
-    right = from_offset(both[..., :HALO], "gy", 1)
-    left = from_offset(both[..., cols - HALO:], "gy", -1)
+    first_rows, last_rows = both[:, :, :HALO, :], both[:, :, rows - HALO:, :]
+    below = from_offset(first_rows, 1, 0)
+    above = from_offset(last_rows, -1, 0)
+    right = from_offset(both[..., :HALO], 0, 1)
+    left = from_offset(both[..., cols - HALO:], 0, -1)
+    below_right = from_offset(first_rows[..., :HALO], 1, 1)
+    below_left = from_offset(first_rows[..., cols - HALO:], 1, -1)
+    above_right = from_offset(last_rows[..., :HALO], -1, 1)
+    above_left = from_offset(last_rows[..., cols - HALO:], -1, -1)
     gap = width - cols - 2 * HALO
-    filler = jnp.concatenate(
-        [jnp.zeros((1, planes, rows, gap), noisy.dtype), jnp.ones((1, planes, rows, gap), noisy.dtype)], 0
+
+    def band(middle, after, before):
+        count = middle.shape[2]
+        filler = jnp.concatenate(
+            [jnp.zeros((1, planes, count, gap), noisy.dtype), jnp.ones((1, planes, count, gap), noisy.dtype)], 0
+        )
+        return jnp.concatenate([middle, after, filler, before], 3)
+
+    full = jnp.concatenate(
+        [band(both, right, left), band(below, below_right, below_left), band(above, above_right, above_left)], 2
     )
-    wide = jnp.concatenate([both, right, filler, left], 3)
-    below = from_offset(wide[:, :, :HALO, :], "gx", 1)
-    above = from_offset(wide[:, :, rows - HALO:, :], "gx", -1)
-    full = jnp.concatenate([wide, below, above], 2)
     return full[0], full[1], width
 
 

time: 123 us -> 126 us (1.024); the launches traced: 123 us -> 125 us
  waiting for transfers between devices: 44.3 us -> 27.4 us
  starting transfers between devices: 8.71 us -> 21.6 us
  other arithmetic: 4.45 us -> 11.8 us
  local copies, waits for them, and re-layouts: 2.39 us -> 0.47 us
    ppermute x4 -> x8, waiting for transfers between devices: 44.3 us -> 27.4 us  [the longest x4 15.3 us: from_offset(): return lax.ppermute(value, axes[0], pairs)]
    ppermute x4 -> x8, starting transfers between devices: 8.71 us -> 21.6 us  [the longest x4 12.7 us: from_offset(): return lax.ppermute(value, axes, pairs)]
    another operation x0 -> x3, other arithmetic: none -> 6.74 us  [extend(): both = jnp.stack([noisy, weight])]
    concatenate x2 -> x1, other arithmetic: 2.89 us -> 5.04 us  [extend(): jnp.concatenate([band(both, right, left), band(below, below_right, below_...]
    slice x1 -> x0, local copies, waits for them, and re-layouts: 1.68 us -> none  [extend(): below = from_offset(wide[:, :, :HALO, :], 'gx', 1)]
    slice x1 -> x0, other arithmetic: 1.55 us -> none  [extend(): right = from_offset(both[..., :HALO], 'gy', 1)]
  transfers between devices with their start and end apart: 4 -> 8, of which waited for: 3 -> 6; matrix products, arithmetic and copies ran while one was open for 0% -> 3% of each run, Pallas kernels for 0% -> 0%
where the time goes in v4:
time: 126 us; the launch traced here: 125 us
  Pallas kernels  63.4 us (50%)
  waiting for transfers between devices  27.4 us (22%)
  starting transfers between devices  21.6 us (17%)
  other arithmetic  11.8 us (9%)
    pallas_call x1, Pallas kernels, per_device(): pl.pallas_call(iterate_kernel, out_shape=jax.ShapeDtypeStruct(noisy.shape...  63.4 us
    ppermute x4, waiting for transfers between devices, from_offset(): return lax.ppermute(value, axes[0], pairs)  15.3 us
    ppermute x4, starting transfers between devices, from_offset(): return lax.ppermute(value, axes, pairs)  12.7 us
    ppermute x4, waiting for transfers between devices, from_offset(): return lax.ppermute(value, axes, pairs)  12.1 us
    ppermute x4, starting transfers between devices, from_offset(): return lax.ppermute(value, axes[0], pairs)  8.93 us
    another operation x3, other arithmetic, extend(): both = jnp.stack([noisy, weight])  6.74 us
    concatenate x1, other arithmetic, extend(): jnp.concatenate([band(both, right, left), band(below, below_right, below_...  5.04 us
  transfers between devices with their start and end apart: 8, of which 6 were waited for; matrix products, arithmetic and copies ran while one was open for 3% of the time, Pallas kernels for 0%

profile of v4, /device:TPU:1, one launch (start us, length us, event | category | flops | bytes accessed | tf_op | source)
XLA Modules:
  0.0 124.7 jit_solution(7881106522961443699)
XLA Ops:
  0.0 0.0 copy-start
  0.0 0.0 copy-start.1
  0.0 0.0 copy-start.2
  0.0 3.2 %fusion = (f32[2,32,8,512]{3,2,1,0:T(8,128)}, f32[2,32,8,512]{3,2,1,0:T(8,128)}) fusion(f32[1,32,16,512]{3,2,1,0:T(8,128)} %bitcast.6, f32[1,32,16,512]{3,2,1,0:T(8,128)} %bitcast.10), kind=kLoop, calls=%fused_computation.17 | loop fusion | flops 524288 | bytes 4194304 | tf_op jit(solution)/shard_map/stack | solution.py:38
  3.2 3.2 %collective-permute-start.2 = (f32[2,32,8,512]{3,2,1,0:T(8,128)}, f32[2,32,8,512]{3,2,1,0:T(8,128)S(1)}, u32[]{:S(2)}, u32[]{:S(2)}) collective-permute-start(f32[2,32,8,512]{3,2,1,0:T(8,128)} %get-tuple-element.9), channel_id=1, source_target_pairs={{0,248},{8,0},{16,8},{24,16},{32,24},{40,32},{48,40},{56,48},{64,5... | collective-permute-start | bytes 3145736 | tf_op jit(solution)/shard_map/ppermute | solution.py:31
  6.4 1.1 collective-permute-start.5
  7.5 2.4 %fusion.5 = (f32[2,32,8,8]{3,2,1,0:T(8,128)}, f32[2,32,8,8]{3,2,1,0:T(8,128)}, f32[2,32,8,8]{3,2,1,0:T(8,128)}, f32[2,32,8,8]{3,2,1,0:T(8,128)}) fusion(f32[1,32,16,512]{3,2,1,0:T(8,128)} %bitcast.7, f32[1,32,16,512]{3,2,1,0:T(8,128)} %bitcast.11), kind=kLoop, calls=%fused_computation.22 | loop fusion | flops 16384 | bytes 2162688 | tf_op jit(solution)/shard_map/stack | solution.py:38
  9.9 7.6 %collective-permute-start.3 = (f32[2,32,8,8]{3,2,1,0:T(8,128)}, f32[2,32,8,8]{3,2,1,0:T(8,128)}, u32[]{:S(2)}, u32[]{:S(2)}) collective-permute-start(f32[2,32,8,8]{3,2,1,0:T(8,128)} %get-tuple-element.11), channel_id=1, source_target_pairs={{9,0},{10,1},{11,2},{12,3},{13,4},{14,5},{15,6},{8,7},{17,8},{18,9... | collective-permute-start | bytes 49160 | tf_op jit(solution)/shard_map/ppermute | solution.py:32
  17.5 3.9 %collective-permute-start.4 = (f32[2,32,8,8]{3,2,1,0:T(8,128)}, f32[2,32,8,8]{3,2,1,0:T(8,128)}, u32[]{:S(2)}, u32[]{:S(2)}) collective-permute-start(f32[2,32,8,8]{3,2,1,0:T(8,128)} %get-tuple-element.12), channel_id=1, source_target_pairs={{15,0},{8,1},{9,2},{10,3},{11,4},{12,5},{13,6},{14,7},{23,8},{16,9... | collective-permute-start | bytes 49160 | tf_op jit(solution)/shard_map/ppermute | solution.py:32
  21.5 1.1 collective-permute-start.6
  22.6 0.0 copy-done
  22.6 0.0 copy-done.1
  22.6 1.1 fusion.2
  23.7 0.3 collective-permute-done.3
  24.0 0.0 collective-permute-start.7
  24.0 5.5 %collective-permute-done.4 = f32[2,32,8,8]{3,2,1,0:T(8,128)} collective-permute-done((f32[2,32,8,8]{3,2,1,0:T(8,128)}, f32[2,32,8,8]{3,2,1,0:T(8,128)}, u32[]{:S(2)}, u32[]{:S(2)}) %collective-permute-start.4) | collective-permute-done | bytes 16416 | tf_op jit(solution)/shard_map/ppermute | solution.py:32
  29.4 4.6 %collective-permute-start = (f32[2,32,16,8]{3,2,1,0:T(8,128)}, f32[2,32,16,8]{3,2,1,0:T(8,128)S(1)}, u32[]{:S(2)}, u32[]{:S(2)}) collective-permute-start(f32[2,32,16,8]{3,2,1,0:T(8,128)} %get-tuple-element.7), channel_id=1, source_target_pairs={{0,7},{1,0},{2,1},{3,2},{4,3},{5,4},{6,5},{7,6},{8,15},{9,8},{10,9... | collective-permute-start | bytes 98312 | tf_op jit(solution)/shard_map/ppermute | solution.py:31
  34.1 0.0 collective-permute-done.6
  34.1 0.0 collective-permute-start.1
  34.1 6.4 %collective-permute-done.7 = f32[2,32,8,8]{3,2,1,0:T(8,128)S(1)} collective-permute-done((f32[2,32,8,8]{3,2,1,0:T(8,128)}, f32[2,32,8,8]{3,2,1,0:T(8,128)S(1)}, u32[]{:S(2)}, u32[]{:S(2)}) %collective-permute-start.7) | collective-permute-done | bytes 16416 | tf_op jit(solution)/shard_map/ppermute | solution.py:32
  40.4 1.1 collective-permute-done
  41.5 3.8 %collective-permute-done.1 = f32[2,32,16,8]{3,2,1,0:T(8,128)S(1)} collective-permute-done((f32[2,32,16,8]{3,2,1,0:T(8,128)}, f32[2,32,16,8]{3,2,1,0:T(8,128)S(1)}, u32[]{:S(2)}, u32[]{:S(2)}) %collective-permute-start.1) | collective-permute-done | bytes 32800 | tf_op jit(solution)/shard_map/ppermute | solution.py:31
  45.3 10.4 %collective-permute-done.2 = f32[2,32,8,512]{3,2,1,0:T(8,128)S(1)} collective-permute-done((f32[2,32,8,512]{3,2,1,0:T(8,128)}, f32[2,32,8,512]{3,2,1,0:T(8,128)S(1)}, u32[]{:S(2)}, u32[]{:S(2)}) %collective-permute-start.2) | collective-permute-done | bytes 1048608 | tf_op jit(solution)/shard_map/ppermute | solution.py:31
  55.8 0.0 collective-permute-done.5
  55.8 0.0 copy-done.2
  55.8 5.0 %maximum_maximum_fusion = f32[2,32,32,640]{3,2,1,0:T(8,128)S(1)} fusion(f32[2,32,8,8]{3,2,1,0:T(8,128)S(1)} %collective-permute-done.7, f32[2,32,8,112]{3,2,1,0:T(8,128)S(1)} %copy-done.2, f32[2,32,8,8]{3,2,1,0:T(8,128)} %collective-permute-done.6, f32[2,32,8,512]{3,2,1,0:T(8,128)} %collective-permute-done.5, f32[2,32,8,8]{3,2,1,0:T(8,128)} %collective-permute-done.4, ...), kind=kLoop, calls=%fused_computation | loop fusion | flops 15728640 | bytes 10256384 | tf_op jit(solution)/shard_map/concatenate | solution.py:57
  60.9 0.3 slice_bitcast_fusion
  61.2 0.1 broadcast_in_dim.4.keep_x_ref
  61.3 63.4 %shard_map.28 = f32[32,16,512]{2,1,0:T(8,128)} custom-call(f32[32,32,640]{2,1,0:T(8,128)S(1)} %get-tuple-element.6.noisy_ref, f32[32,32,640]{2,1,0:T(8,128)S(1)} %get-tuple-element.5.weight_ref, f32[32,640]{1,0:T(8,128)S(1)} %broadcast_in_dim.4.keep_x_ref, f32[32,640]{1,0:T(8,128)S(1)} %broadcast_in_dim.5.keep_y_ref), custom_call_target="tpu_custom_call" | custom-call | tf_op jit(solution)/shard_map/pallas_call | solution.py:134
  (4 shorter events, 0.1 us)
Async XLA Ops:
  0.0 22.6 %copy-start = (f32[32,16,512]{2,1,0:T(8,128)S(1)}, f32[32,16,512]{2,1,0:T(8,128)}, u32[]{:S(2)}) copy-start(f32[32,16,512]{2,1,0:T(8,128)} %param.2) | copy-start | bytes 3145732
  0.0 22.6 %copy-start.1 = (f32[32,16,512]{2,1,0:T(8,128)S(1)}, f32[32,16,512]{2,1,0:T(8,128)}, u32[]{:S(2)}) copy-start(f32[32,16,512]{2,1,0:T(8,128)} %param.3) | copy-start | bytes 3145732
  0.0 55.8 %copy-start.2 = (f32[2,32,8,112]{3,2,1,0:T(8,128)S(1)}, f32[2,32,8,112]{3,2,1,0:T(8,128)}, u32[]{:S(2)}) copy-start(f32[2,32,8,112]{3,2,1,0:T(8,128)} %constant.14.clone.1) | copy-start | bytes 688132
  3.2 52.6 %collective-permute-start.2 = (f32[2,32,8,512]{3,2,1,0:T(8,128)}, f32[2,32,8,512]{3,2,1,0:T(8,128)S(1)}, u32[]{:S(2)}, u32[]{:S(2)}) collective-permute-start(f32[2,32,8,512]{3,2,1,0:T(8,128)} %get-tuple-element.9), channel_id=1, source_target_pairs={{0,248},{8,0},{16,8},{24,16},{32,24},{40,32},{48,40},{56,48},{64,5... | collective-permute-start | bytes 3145736 | tf_op jit(solution)/shard_map/ppermute | solution.py:31
  6.4 49.4 %collective-permute-start.5 = (f32[2,32,8,512]{3,2,1,0:T(8,128)}, f32[2,32,8,512]{3,2,1,0:T(8,128)}, u32[]{:S(2)}, u32[]{:S(2)}) collective-permute-start(f32[2,32,8,512]{3,2,1,0:T(8,128)} %get-tuple-element.10), channel_id=1, source_target_pairs={{0,8},{8,16},{16,24},{24,32},{32,40},{40,48},{48,56},{56,64},{64,7... | collective-permute-start | bytes 3145736 | tf_op jit(solution)/shard_map/ppermute | solution.py:31
  9.9 14.1 %collective-permute-start.3 = (f32[2,32,8,8]{3,2,1,0:T(8,128)}, f32[2,32,8,8]{3,2,1,0:T(8,128)}, u32[]{:S(2)}, u32[]{:S(2)}) collective-permute-start(f32[2,32,8,8]{3,2,1,0:T(8,128)} %get-tuple-element.11), channel_id=1, source_target_pairs={{9,0},{10,1},{11,2},{12,3},{13,4},{14,5},{15,6},{8,7},{17,8},{18,9... | collective-permute-start | bytes 49160 | tf_op jit(solution)/shard_map/ppermute | solution.py:32
  17.5 11.9 %collective-permute-start.4 = (f32[2,32,8,8]{3,2,1,0:T(8,128)}, f32[2,32,8,8]{3,2,1,0:T(8,128)}, u32[]{:S(2)}, u32[]{:S(2)}) collective-permute-start(f32[2,32,8,8]{3,2,1,0:T(8,128)} %get-tuple-element.12), channel_id=1, source_target_pairs={{15,0},{8,1},{9,2},{10,3},{11,4},{12,5},{13,6},{14,7},{23,8},{16,9... | collective-permute-start | bytes 49160 | tf_op jit(solution)/shard_map/ppermute | solution.py:32
  21.5 12.6 %collective-permute-start.6 = (f32[2,32,8,8]{3,2,1,0:T(8,128)}, f32[2,32,8,8]{3,2,1,0:T(8,128)}, u32[]{:S(2)}, u32[]{:S(2)}) collective-permute-start(f32[2,32,8,8]{3,2,1,0:T(8,128)} %get-tuple-element.14), channel_id=1, source_target_pairs={{249,0},{250,1},{251,2},{252,3},{253,4},{254,5},{255,6},{248,7},{1... | collective-permute-start | bytes 49160 | tf_op jit(solution)/shard_map/ppermute | solution.py:32
  24.0 16.5 %collective-permute-start.7 = (f32[2,32,8,8]{3,2,1,0:T(8,128)}, f32[2,32,8,8]{3,2,1,0:T(8,128)S(1)}, u32[]{:S(2)}, u32[]{:S(2)}) collective-permute-start(f32[2,32,8,8]{3,2,1,0:T(8,128)} %get-tuple-element.13), channel_id=1, source_target_pairs={{255,0},{248,1},{249,2},{250,3},{251,4},{252,5},{253,6},{254,7},{7... | collective-permute-start | bytes 49160 | tf_op jit(solution)/shard_map/ppermute | solution.py:32
  29.4 12.1 %collective-permute-start = (f32[2,32,16,8]{3,2,1,0:T(8,128)}, f32[2,32,16,8]{3,2,1,0:T(8,128)S(1)}, u32[]{:S(2)}, u32[]{:S(2)}) collective-permute-start(f32[2,32,16,8]{3,2,1,0:T(8,128)} %get-tuple-element.7), channel_id=1, source_target_pairs={{0,7},{1,0},{2,1},{3,2},{4,3},{5,4},{6,5},{7,6},{8,15},{9,8},{10,9... | collective-permute-start | bytes 98312 | tf_op jit(solution)/shard_map/ppermute | solution.py:31
  34.1 11.3 %collective-permute-start.1 = (f32[2,32,16,8]{3,2,1,0:T(8,128)}, f32[2,32,16,8]{3,2,1,0:T(8,128)S(1)}, u32[]{:S(2)}, u32[]{:S(2)}) collective-permute-start(f32[2,32,16,8]{3,2,1,0:T(8,128)} %get-tuple-element.8), channel_id=1, source_target_pairs={{0,1},{1,2},{2,3},{3,4},{4,5},{5,6},{6,7},{7,0},{8,9},{9,10},{10,1... | collective-permute-start | bytes 98312 | tf_op jit(solution)/shard_map/ppermute | solution.py:31

commit v5 on v3

v5 whole, which is shorter than its diff:
```python
import functools

import jax
import jax.numpy as jnp
from jax import lax
from jax.experimental import pallas as pl
from jax.experimental.pallas import tpu as pltpu
from jax.sharding import PartitionSpec as P

ITERS = 8
HALO = ITERS


dual_step = 0.28
primal_step = 0.28
fidelity = 1.0


def from_offset(value, axis, offset):
    count = lax.axis_size(axis)
    return lax.ppermute(value, axis, [((dest + offset) % count, dest) for dest in range(count)])


def extend(noisy, weight):
    planes, rows, cols = noisy.shape
    width = -(-(cols + 2 * HALO) // 128) * 128
    both = jnp.stack([noisy, weight])
    right = from_offset(both[..., :HALO], "gy", 1)
    left = from_offset(both[..., cols - HALO:], "gy", -1)
    gap = width - cols - 2 * HALO
    filler = jnp.concatenate(
        [jnp.zeros((1, planes, rows, gap), noisy.dtype), jnp.ones((1, planes, rows, gap), noisy.dtype)], 0
    )
    wide = jnp.concatenate([both, right, filler, left], 3)
    below = from_offset(wide[:, :, :HALO, :], "gx", 1)
    above = from_offset(wide[:, :, rows - HALO:, :], "gx", -1)
    full = jnp.concatenate([wide, below, above], 2)
    return full[0], full[1], width


LANES = 128


def iterate_kernel(
    noisy_ref, weight_ref, step_x_ref, step_y_ref, out_ref,
    primal, extrapolated, dual_x, dual_y, dual_z, pulled,
):
    planes, rows, width = noisy_ref.shape
    blocks = width // LANES
    shrink = 1.0 / (1.0 + primal_step * fidelity)

    def setup(z, carry):
        noisy = noisy_ref[z]
        primal[z] = noisy
        extrapolated[z] = noisy
        pulled[z] = primal_step * fidelity * noisy
        dual_x[z] = jnp.zeros_like(noisy)
        dual_y[z] = jnp.zeros_like(noisy)
        dual_z[z] = jnp.zeros_like(noisy)
        return carry

    lax.fori_loop(0, planes, setup, 0)
    lane = lax.broadcasted_iota(jnp.int32, (rows, LANES), 1)
    last_lane = lane == LANES - 1
    first_lane = lane == 0

    def plane(z, carry):
        after = jnp.minimum(z + 1, planes - 1)
        before = jnp.maximum(z - 1, 0)
        step_z = jnp.where(z < planes - 1, dual_step, 0.0)
        turned = [pltpu.roll(extrapolated[z, :, pl.ds(block * LANES, LANES)], LANES - 1, 1) for block in range(blocks)]
        for block in range(blocks):
            cols = pl.ds(block * LANES, LANES)
            here = extrapolated[z, :, cols]
            next_y = jnp.where(last_lane, turned[(block + 1) % blocks], turned[block])
            next_x = pltpu.roll(here, rows - 1, 0)
            new_x, new_y, new_z = project(
                dual_x[z, :, cols] + step_x_ref[:, cols] * (next_x - here),
                dual_y[z, :, cols] + step_y_ref[:, cols] * (next_y - here),
                dual_z[z, :, cols] + step_z * (extrapolated[after, :, cols] - here),
                weight_ref[z, :, cols],
            )
            dual_x[z, :, cols] = new_x
            dual_y[z, :, cols] = new_y
            dual_z[z, :, cols] = new_z
        turned = [pltpu.roll(dual_y[z, :, pl.ds(block * LANES, LANES)], 1, 1) for block in range(blocks)]
        for block in range(blocks):
            cols = pl.ds(block * LANES, LANES)
            new_x = dual_x[z, :, cols]
            new_y = dual_y[z, :, cols]
            prev_y = jnp.where(first_lane, turned[(block - 1) % blocks], turned[block])
            prev_z = jnp.where(z > 0, dual_z[before, :, cols], 0.0)
            divergence = (new_x - pltpu.roll(new_x, 1, 0)) + (new_y - prev_y) + (dual_z[z, :, cols] - prev_z)
            old = primal[z, :, cols]
            updated = (old + primal_step * divergence + pulled[z, :, cols]) * shrink
            extrapolated[z, :, cols] = 2.0 * updated - old
            primal[z, :, cols] = updated
        return carry

    for iteration in range(ITERS):
        lax.fori_loop(0, planes, plane, 0)
    own_rows, own_cols = out_ref.shape[1:]
    out_ref[...] = primal[:, :own_rows, :own_cols]


def project(dual_x, dual_y, dual_z, weight):
    scale = jnp.minimum(1.0, weight * lax.rsqrt(dual_x * dual_x + dual_y * dual_y + dual_z * dual_z))
    return (dual_x * scale, dual_y * scale, dual_z * scale)


def per_device(noisy, weight):
    planes, rows_x, rows_y = noisy.shape
    total_x = rows_x * lax.axis_size("gx")
    total_y = rows_y * lax.axis_size("gy")
    start_x = lax.axis_index("gx") * rows_x
    start_y = lax.axis_index("gy") * rows_y
    noisy_e, weight_e, width = extend(noisy, weight)
    ext_x = rows_x + 2 * HALO

    local_x = jnp.arange(ext_x, dtype=jnp.int32)
    index_x = jnp.where(local_x >= rows_x + HALO, start_x + local_x - ext_x, start_x + local_x)
    keep_x = (index_x >= 0) & (index_x < total_x - 1)
    local_y = jnp.arange(width, dtype=jnp.int32)
    index_y = jnp.where(local_y >= width - HALO, start_y + local_y - width, start_y + local_y)
    inside_y = (local_y < rows_y + HALO) | (local_y >= width - HALO)
    keep_y = inside_y & (index_y >= 0) & (index_y < total_y - 1)
    step_x = jnp.broadcast_to(jnp.where(keep_x, dual_step, 0.0)[:, None], (ext_x, width)).astype(jnp.float32)
    step_y = jnp.broadcast_to(jnp.where(keep_y, dual_step, 0.0)[None, :], (ext_x, width)).astype(jnp.float32)

    field = jax.ShapeDtypeStruct((planes, ext_x, width), jnp.float32)
    vmem = pl.BlockSpec(memory_space=pltpu.VMEM)
    return pl.pallas_call(
        iterate_kernel,
        out_shape=jax.ShapeDtypeStruct(noisy.shape, jnp.float32),
        in_specs=[vmem] * 4,
        out_specs=vmem,
        scratch_shapes=[pltpu.VMEM(field.shape, jnp.float32)] * 6,
        compiler_params=pltpu.CompilerParams(vmem_limit_bytes=48 * 1024 * 1024),
    )(noisy_e, weight_e, step_x, step_y)


def solution(mesh):
    placed = (P(None, "gx", "gy"), P(None, "gx", "gy"))
    return jax.shard_map(
        per_device, mesh=mesh, in_specs=placed, out_specs=P(None, "gx", "gy"), check_vma=False
    )
```

time: 123 us -> 115 us (0.935)
  Pallas kernels: 63.4 us -> 55.5 us
    pallas_call x1, Pallas kernels: 63.4 us -> 55.5 us  [per_device(): pl.pallas_call(iterate_kernel, out_shape=jax.ShapeDtypeStruct(noisy.shape...]
where the time goes in v5:
time: 115 us
  Pallas kernels  55.5 us (48%)
  waiting for transfers between devices  44.3 us (39%)
  starting transfers between devices  8.71 us (8%)
  other arithmetic  4.45 us (4%)
  local copies, waits for them, and re-layouts  2.39 us (2%)
    pallas_call x1, Pallas kernels, per_device(): pl.pallas_call(iterate_kernel, out_shape=jax.ShapeDtypeStruct(noisy.shape...  55.5 us
    ppermute x4, waiting for transfers between devices, from_offset(): lax.ppermute(value, axis, [((dest + offset) % count, dest) for dest in ra...  44.3 us
    ppermute x4, starting transfers between devices, from_offset(): lax.ppermute(value, axis, [((dest + offset) % count, dest) for dest in ra...  8.71 us
    concatenate x1, other arithmetic, extend(): full = jnp.concatenate([wide, below, above], 2)  2.41 us
  transfers between devices with their start and end apart: 4, of which 3 were waited for; matrix products, arithmetic and copies ran while one was open for 0% of the time, Pallas kernels for 0%

profile of v5, /device:TPU:1, one launch (start us, length us, event | category | flops | bytes accessed | tf_op | source)
XLA Modules:
  0.0 115.3 jit_solution(10271601218442131874)
XLA Ops:
  0.0 0.0 copy-start.1
  0.0 0.0 copy-start
  0.0 1.6 %pad_maximum_fusion.3 = (f32[2,32,16,8]{3,2,1,0:T(8,128)S(1)}, f32[2,32,16,8]{3,2,1,0:T(8,128)S(1)}) fusion(f32[1,32,16,512]{3,2,1,0:T(8,128)} %bitcast.6, f32[1,32,16,512]{3,2,1,0:T(8,128)} %bitcast.9), kind=kLoop, calls=%fused_computation.5 | loop fusion | flops 16384 | bytes 2162688 | tf_op jit(solution)/shard_map/slice | solution.py:28
  1.6 4.4 %collective-permute-start = (f32[2,32,16,8]{3,2,1,0:T(8,128)S(1)}, f32[2,32,16,8]{3,2,1,0:T(8,128)S(1)}, u32[]{:S(2)}, u32[]{:S(2)}) collective-permute-start(f32[2,32,16,8]{3,2,1,0:T(8,128)S(1)} %get-tuple-element.9), channel_id=1, source_target_pairs={{1,0},{2,1},{3,2},{4,3},{5,4},{6,5},{7,6},{0,7},{9,8},{10,9},{11,1... | collective-permute-start | bytes 98312 | tf_op jit(solution)/shard_map/ppermute | solution.py:21
  5.9 0.0 collective-permute-start.1
  5.9 10.6 %collective-permute-done = f32[2,32,16,8]{3,2,1,0:T(8,128)S(1)} collective-permute-done((f32[2,32,16,8]{3,2,1,0:T(8,128)S(1)}, f32[2,32,16,8]{3,2,1,0:T(8,128)S(1)}, u32[]{:S(2)}, u32[]{:S(2)}) %collective-permute-start) | collective-permute-done | bytes 32800 | tf_op jit(solution)/shard_map/ppermute | solution.py:21
  16.6 4.0 %collective-permute-done.1 = f32[2,32,16,8]{3,2,1,0:T(8,128)S(1)} collective-permute-done((f32[2,32,16,8]{3,2,1,0:T(8,128)S(1)}, f32[2,32,16,8]{3,2,1,0:T(8,128)S(1)}, u32[]{:S(2)}, u32[]{:S(2)}) %collective-permute-start.1) | collective-permute-done | bytes 32800 | tf_op jit(solution)/shard_map/ppermute | solution.py:21
  20.6 0.0 copy-start.2
  20.6 0.0 copy-done.1
  20.6 0.0 copy-done
  20.6 0.5 pad_maximum_fusion.1
  21.1 0.2 copy-done.2
  21.4 1.7 %fusion.6 = (f32[2,32,8,640]{3,2,1,0:T(8,128)}, f32[2,32,8,640]{3,2,1,0:T(8,128)}) fusion(f32[2,32,16,640]{3,2,1,0:T(8,128)S(1)} %pad_maximum_fusion.1), kind=kLoop, calls=%fused_computation.17 | loop fusion | bytes 5242880 | tf_op jit(solution)/shard_map/slice | solution.py:35
  23.1 1.8 %collective-permute-start.2 = (f32[2,32,8,640]{3,2,1,0:T(8,128)}, f32[2,32,8,640]{3,2,1,0:T(8,128)}, u32[]{:S(2)}, u32[]{:S(2)}) collective-permute-start(f32[2,32,8,640]{3,2,1,0:T(8,128)} %get-tuple-element.7), channel_id=1, source_target_pairs={{8,0},{16,8},{24,16},{32,24},{40,32},{48,40},{56,48},{64,56},{72,6... | collective-permute-start | bytes 3932168 | tf_op jit(solution)/shard_map/ppermute | solution.py:21
  24.9 2.5 %collective-permute-start.3 = (f32[2,32,8,640]{3,2,1,0:T(8,128)}, f32[2,32,8,640]{3,2,1,0:T(8,128)}, u32[]{:S(2)}, u32[]{:S(2)}) collective-permute-start(f32[2,32,8,640]{3,2,1,0:T(8,128)} %get-tuple-element.8), channel_id=1, source_target_pairs={{248,0},{0,8},{8,16},{16,24},{24,32},{32,40},{40,48},{48,56},{56,6... | collective-permute-start | bytes 3932168 | tf_op jit(solution)/shard_map/ppermute | solution.py:21
  27.4 29.6 %collective-permute-done.2 = f32[2,32,8,640]{3,2,1,0:T(8,128)} collective-permute-done((f32[2,32,8,640]{3,2,1,0:T(8,128)}, f32[2,32,8,640]{3,2,1,0:T(8,128)}, u32[]{:S(2)}, u32[]{:S(2)}) %collective-permute-start.2) | collective-permute-done | bytes 1310752 | tf_op jit(solution)/shard_map/ppermute | solution.py:21
  57.0 0.0 collective-permute-done.3
  57.0 2.4 %pad_maximum_fusion = f32[2,32,32,640]{3,2,1,0:T(8,128)S(1)} fusion(f32[2,32,8,640]{3,2,1,0:T(8,128)} %collective-permute-done.3, f32[2,32,8,640]{3,2,1,0:T(8,128)} %collective-permute-done.2, f32[2,32,16,8]{3,2,1,0:T(8,128)} %copy-done.2, f32[2,32,16,112]{3,2,1,0:T(8,128)S(1)} %concatenate.9, f32[2,32,16,8]{3,2,1,0:T(8,128)S(1)} %collective-permute-done, ...), kind=kLoop, calls=%fused_computation | loop fusion | flops 7864320 | bytes 10485760 | tf_op jit(solution)/shard_map/concatenate | solution.py:37
  59.4 0.3 slice_bitcast_fusion
  59.8 0.1 broadcast_in_dim.32.step_x_ref
  59.9 55.5 %shard_map.28 = f32[32,16,512]{2,1,0:T(8,128)} custom-call(f32[32,32,640]{2,1,0:T(8,128)S(1)} %get-tuple-element.6.noisy_ref, f32[32,32,640]{2,1,0:T(8,128)S(1)} %get-tuple-element.5.weight_ref, f32[32,640]{1,0:T(8,128)S(1)} %broadcast_in_dim.32.step_x_ref, f32[32,640]{1,0:T(8,128)S(1)} %broadcast_in_dim.35.step_y_ref), custom_call_target="tpu_custom_call" | custom-call | tf_op jit(solution)/shard_map/pallas_call | solution.py:132
  (4 shorter events, 0.1 us)
Async XLA Ops:
  0.0 20.6 %copy-start.1 = (f32[32,16,512]{2,1,0:T(8,128)S(1)}, f32[32,16,512]{2,1,0:T(8,128)}, u32[]{:S(2)}) copy-start(f32[32,16,512]{2,1,0:T(8,128)} %param.2) | copy-start | bytes 3145732
  0.0 20.6 %copy-start = (f32[32,16,512]{2,1,0:T(8,128)S(1)}, f32[32,16,512]{2,1,0:T(8,128)}, u32[]{:S(2)}) copy-start(f32[32,16,512]{2,1,0:T(8,128)} %param.3) | copy-start | bytes 3145732
  1.6 15.0 %collective-permute-start = (f32[2,32,16,8]{3,2,1,0:T(8,128)S(1)}, f32[2,32,16,8]{3,2,1,0:T(8,128)S(1)}, u32[]{:S(2)}, u32[]{:S(2)}) collective-permute-start(f32[2,32,16,8]{3,2,1,0:T(8,128)S(1)} %get-tuple-element.9), channel_id=1, source_target_pairs={{1,0},{2,1},{3,2},{4,3},{5,4},{6,5},{7,6},{0,7},{9,8},{10,9},{11,1... | collective-permute-start | bytes 98312 | tf_op jit(solution)/shard_map/ppermute | solution.py:21
  5.9 14.6 %collective-permute-start.1 = (f32[2,32,16,8]{3,2,1,0:T(8,128)S(1)}, f32[2,32,16,8]{3,2,1,0:T(8,128)S(1)}, u32[]{:S(2)}, u32[]{:S(2)}) collective-permute-start(f32[2,32,16,8]{3,2,1,0:T(8,128)S(1)} %get-tuple-element.10), channel_id=1, source_target_pairs={{7,0},{0,1},{1,2},{2,3},{3,4},{4,5},{5,6},{6,7},{15,8},{8,9},{9,10... | collective-permute-start | bytes 98312 | tf_op jit(solution)/shard_map/ppermute | solution.py:21
  20.6 0.8 copy-start.2
  23.1 34.0 %collective-permute-start.2 = (f32[2,32,8,640]{3,2,1,0:T(8,128)}, f32[2,32,8,640]{3,2,1,0:T(8,128)}, u32[]{:S(2)}, u32[]{:S(2)}) collective-permute-start(f32[2,32,8,640]{3,2,1,0:T(8,128)} %get-tuple-element.7), channel_id=1, source_target_pairs={{8,0},{16,8},{24,16},{32,24},{40,32},{48,40},{56,48},{64,56},{72,6... | collective-permute-start | bytes 3932168 | tf_op jit(solution)/shard_map/ppermute | solution.py:21
  24.9 32.2 %collective-permute-start.3 = (f32[2,32,8,640]{3,2,1,0:T(8,128)}, f32[2,32,8,640]{3,2,1,0:T(8,128)}, u32[]{:S(2)}, u32[]{:S(2)}) collective-permute-start(f32[2,32,8,640]{3,2,1,0:T(8,128)} %get-tuple-element.8), channel_id=1, source_target_pairs={{248,0},{0,8},{8,16},{16,24},{24,32},{32,40},{40,48},{48,56},{56,6... | collective-permute-start | bytes 3932168 | tf_op jit(solution)/shard_map/ppermute | solution.py:21

commit v6 on v5

--- a/solution.py
+++ b/solution.py
@@ -31,25 +31,33 @@
     filler = jnp.concatenate(
         [jnp.zeros((1, planes, rows, gap), noisy.dtype), jnp.ones((1, planes, rows, gap), noisy.dtype)], 0
     )
-    wide = jnp.concatenate([both, right, filler, left], 3)
-    below = from_offset(wide[:, :, :HALO, :], "gx", 1)
-    above = from_offset(wide[:, :, rows - HALO:, :], "gx", -1)
-    full = jnp.concatenate([wide, below, above], 2)
-    return full[0], full[1], width
+    tail = jnp.concatenate([right, filler, left], 3)
+    first = jnp.concatenate([both[:, :, :HALO, :], tail[:, :, :HALO, :]], 3)
+    last = jnp.concatenate([both[:, :, rows - HALO:, :], tail[:, :, rows - HALO:, :]], 3)
+    below = from_offset(first, "gx", 1)
+    above = from_offset(last, "gx", -1)
+    return tail, below, above, width
 
 
 LANES = 128
 
 
 def iterate_kernel(
-    noisy_ref, weight_ref, step_x_ref, step_y_ref, out_ref,
-    primal, extrapolated, dual_x, dual_y, dual_z, pulled,
+    own_noisy_ref, own_weight_ref, tail_ref, below_ref, above_ref, step_x_ref, step_y_ref, out_ref,
+    noisy_ref, weight_ref, primal, extrapolated, dual_x, dual_y, dual_z, pulled,
 ):
     planes, rows, width = noisy_ref.shape
+    own_rows, own_cols = out_ref.shape[1:]
+    halo = below_ref.shape[2]
     blocks = width // LANES
     shrink = 1.0 / (1.0 + primal_step * fidelity)
 
     def setup(z, carry):
+        for field, own_ref, part in ((noisy_ref, own_noisy_ref, 0), (weight_ref, own_weight_ref, 1)):
+            field[z, pl.ds(0, own_rows), pl.ds(0, own_cols)] = own_ref[z]
+            field[z, pl.ds(0, own_rows), pl.ds(own_cols, width - own_cols)] = tail_ref[part, z]
+            field[z, pl.ds(own_rows, halo)] = below_ref[part, z]
+            field[z, pl.ds(own_rows + halo, halo)] = above_ref[part, z]
         noisy = noisy_ref[z]
         primal[z] = noisy
         extrapolated[z] = noisy
@@ -99,7 +107,6 @@
 
     for iteration in range(ITERS):
         lax.fori_loop(0, planes, plane, 0)
-    own_rows, own_cols = out_ref.shape[1:]
     out_ref[...] = primal[:, :own_rows, :own_cols]
 
 
@@ -114,7 +121,7 @@
     total_y = rows_y * lax.axis_size("gy")
     start_x = lax.axis_index("gx") * rows_x
     start_y = lax.axis_index("gy") * rows_y
-    noisy_e, weight_e, width = extend(noisy, weight)
+    tail, below, above, width = extend(noisy, weight)
     ext_x = rows_x + 2 * HALO
 
     local_x = jnp.arange(ext_x, dtype=jnp.int32)
@@ -132,11 +139,11 @@
     return pl.pallas_call(
         iterate_kernel,
         out_shape=jax.ShapeDtypeStruct(noisy.shape, jnp.float32),
-        in_specs=[vmem] * 4,
+        in_specs=[vmem] * 7,
         out_specs=vmem,
-        scratch_shapes=[pltpu.VMEM(field.shape, jnp.float32)] * 6,
+        scratch_shapes=[pltpu.VMEM(field.shape, jnp.float32)] * 8,
         compiler_params=pltpu.CompilerParams(vmem_limit_bytes=48 * 1024 * 1024),
-    )(noisy_e, weight_e, step_x, step_y)
+    )(noisy, weight, tail, below, above, step_x, step_y)
 
 
 def solution(mesh):

time: 115 us -> 114 us (level)
  local copies, waits for them, and re-layouts: 2.39 us -> 0.16 us
  Pallas kernels: 55.5 us -> 57.4 us
  waiting for transfers between devices: 44.3 us -> 43 us
    pallas_call x1, Pallas kernels: 55.5 us -> 57.4 us  [per_device(): pl.pallas_call(iterate_kernel, out_shape=jax.ShapeDtypeStruct(noisy.shape...]
    slice x1, local copies, waits for them, and re-layouts: 1.68 us -> 0.04 us  [extend(): tail[:, :, rows - HALO:, :]]
    another operation x0 -> x2, other arithmetic: none -> 1.64 us  [extend(): both = jnp.stack([noisy, weight])]
    slice x1 -> x0, other arithmetic: 1.55 us -> none  [extend(): right = from_offset(both[..., :HALO], 'gy', 1)]
    ppermute x4, waiting for transfers between devices: 44.3 us -> 43 us  [from_offset(): lax.ppermute(value, axis, [((dest + offset) % count, dest) for dest in ra...]
    concatenate x2 -> x3, other arithmetic: 2.89 us -> 2.66 us  [the longest x1 1.17 us: extend(): first = jnp.concatenate([both[:, :, :HALO, :], tail[:, :, :HALO, :]], 3)]
  transfers between devices with their start and end apart: 4 -> 4, of which waited for: 3 -> 3; matrix products, arithmetic and copies ran while one was open for 0% -> 1% of each run, Pallas kernels for 0% -> 0%
where the time goes in v6:
time: 114 us
  Pallas kernels  57.4 us (50%)
  waiting for transfers between devices  43 us (38%)
  starting transfers between devices  8.71 us (8%)
  other arithmetic  4.32 us (4%)
    pallas_call x1, Pallas kernels, per_device(): pl.pallas_call(iterate_kernel, out_shape=jax.ShapeDtypeStruct(noisy.shape...  57.4 us
    ppermute x4, waiting for transfers between devices, from_offset(): lax.ppermute(value, axis, [((dest + offset) % count, dest) for dest in ra...  43 us
    ppermute x4, starting transfers between devices, from_offset(): lax.ppermute(value, axis, [((dest + offset) % count, dest) for dest in ra...  8.71 us
  transfers between devices with their start and end apart: 4, of which 3 were waited for; matrix products, arithmetic and copies ran while one was open for 1% of the time, Pallas kernels for 0%

profile of v6, /device:TPU:1, one launch (start us, length us, event | category | flops | bytes accessed | tf_op | source)
XLA Modules:
  0.0 113.6 jit_solution(1480212493959658317)
XLA Ops:
  0.0 0.0 copy-start
  0.0 0.0 copy-start.1
  0.0 1.6 %fusion.2 = (f32[2,32,16,8]{3,2,1,0:T(8,128)S(1)}, f32[2,32,16,8]{3,2,1,0:T(8,128)S(1)}) fusion(f32[1,32,16,512]{3,2,1,0:T(8,128)} %bitcast.2, f32[1,32,16,512]{3,2,1,0:T(8,128)} %bitcast.5), kind=kLoop, calls=%fused_computation.10 | loop fusion | flops 16384 | bytes 2162688 | tf_op jit(solution)/shard_map/stack | solution.py:27
  1.6 4.4 %collective-permute-start = (f32[2,32,16,8]{3,2,1,0:T(8,128)S(1)}, f32[2,32,16,8]{3,2,1,0:T(8,128)S(1)}, u32[]{:S(2)}, u32[]{:S(2)}) collective-permute-start(f32[2,32,16,8]{3,2,1,0:T(8,128)S(1)} %get-tuple-element.5), channel_id=1, source_target_pairs={{1,0},{2,1},{3,2},{4,3},{5,4},{6,5},{7,6},{0,7},{9,8},{10,9},{11,1... | collective-permute-start | bytes 98312 | tf_op jit(solution)/shard_map/ppermute | solution.py:21
  5.9 0.0 collective-permute-start.1
  5.9 0.0 copy-done
  6.0 0.0 copy-done.1
  6.0 0.1 fusion.1
  6.1 10.5 %collective-permute-done = f32[2,32,16,8]{3,2,1,0:T(8,128)S(1)} collective-permute-done((f32[2,32,16,8]{3,2,1,0:T(8,128)S(1)}, f32[2,32,16,8]{3,2,1,0:T(8,128)S(1)}, u32[]{:S(2)}, u32[]{:S(2)}) %collective-permute-start) | collective-permute-done | bytes 32800 | tf_op jit(solution)/shard_map/ppermute | solution.py:21
  16.6 4.0 %collective-permute-done.1 = f32[2,32,16,8]{3,2,1,0:T(8,128)S(1)} collective-permute-done((f32[2,32,16,8]{3,2,1,0:T(8,128)S(1)}, f32[2,32,16,8]{3,2,1,0:T(8,128)S(1)}, u32[]{:S(2)}, u32[]{:S(2)}) %collective-permute-start.1) | collective-permute-done | bytes 32800 | tf_op jit(solution)/shard_map/ppermute | solution.py:21
  20.6 0.3 pad_maximum_fusion.2.tail_ref
  21.0 1.2 %pad_maximum_fusion.1 = f32[2,32,8,640]{3,2,1,0:T(8,128)} fusion(f32[2,32,8,128]{3,2,1,0:T(8,128)S(1)} %get-tuple-element.8, f32[2,32,8,512]{3,2,1,0:T(8,128)S(1)} %fusion.1), kind=kLoop, calls=%fused_computation.8 | loop fusion | flops 327680 | bytes 2621440 | tf_op jit(solution)/shard_map/concatenate | solution.py:35
  22.2 1.8 %collective-permute-start.2 = (f32[2,32,8,640]{3,2,1,0:T(8,128)}, f32[2,32,8,640]{3,2,1,0:T(8,128)}, u32[]{:S(2)}, u32[]{:S(2)}) collective-permute-start(f32[2,32,8,640]{3,2,1,0:T(8,128)} %pad_maximum_fusion.1), channel_id=1, source_target_pairs={{8,0},{16,8},{24,16},{32,24},{40,32},{48,40},{56,48},{64,56},{72,6... | collective-permute-start | bytes 3932168 | tf_op jit(solution)/shard_map/ppermute | solution.py:21
  24.0 1.2 %fusion = f32[2,32,8,640]{3,2,1,0:T(8,128)} fusion(f32[1,32,16,512]{3,2,1,0:T(8,128)S(1)} %bitcast.7, f32[1,32,16,512]{3,2,1,0:T(8,128)S(1)} %bitcast.4, f32[2,32,8,128]{3,2,1,0:T(8,128)S(1)} %get-tuple-element.7), kind=kLoop, calls=%fused_computation.7 | loop fusion | flops 655360 | bytes 3670016 | tf_op jit(solution)/shard_map/concatenate | solution.py:36
  25.1 2.5 %collective-permute-start.3 = (f32[2,32,8,640]{3,2,1,0:T(8,128)}, f32[2,32,8,640]{3,2,1,0:T(8,128)}, u32[]{:S(2)}, u32[]{:S(2)}) collective-permute-start(f32[2,32,8,640]{3,2,1,0:T(8,128)} %fusion), channel_id=1, source_target_pairs={{248,0},{0,8},{8,16},{16,24},{24,32},{32,40},{40,48},{48,56},{56,6... | collective-permute-start | bytes 3932168 | tf_op jit(solution)/shard_map/ppermute | solution.py:21
  27.7 28.5 %collective-permute-done.2.below_ref = f32[2,32,8,640]{3,2,1,0:T(8,128)} collective-permute-done((f32[2,32,8,640]{3,2,1,0:T(8,128)}, f32[2,32,8,640]{3,2,1,0:T(8,128)}, u32[]{:S(2)}, u32[]{:S(2)}) %collective-permute-start.2) | collective-permute-done | bytes 1310752 | tf_op jit(solution)/shard_map/ppermute | solution.py:21
  56.1 0.0 collective-permute-done.3.above_ref
  56.2 0.1 broadcast_in_dim.32.step_x_ref
  56.2 57.4 %shard_map.28 = f32[32,16,512]{2,1,0:T(8,128)} custom-call(f32[32,16,512]{2,1,0:T(8,128)S(1)} %copy-done, f32[32,16,512]{2,1,0:T(8,128)S(1)} %copy-done.1, f32[2,32,16,128]{3,2,1,0:T(8,128)S(1)} %pad_maximum_fusion.2.tail_ref, f32[2,32,8,640]{3,2,1,0:T(8,128)} %collective-permute-done.2.below_ref, f32[2,32,8,640]{3,2,1,0:T(8,128)} %collective-permute-done.3.above_ref, ...), custom_call_target="tpu_custom_call" | custom-call | tf_op jit(solution)/shard_map/pallas_call | solution.py:139
  (5 shorter events, 0.1 us)
Async XLA Ops:
  0.0 6.0 %copy-start = (f32[32,16,512]{2,1,0:T(8,128)S(1)}, f32[32,16,512]{2,1,0:T(8,128)}, u32[]{:S(2)}) copy-start(f32[32,16,512]{2,1,0:T(8,128)} %own_noisy_ref.1) | copy-start | bytes 3145732
  0.0 6.0 %copy-start.1 = (f32[32,16,512]{2,1,0:T(8,128)S(1)}, f32[32,16,512]{2,1,0:T(8,128)}, u32[]{:S(2)}) copy-start(f32[32,16,512]{2,1,0:T(8,128)} %own_weight_ref.1) | copy-start | bytes 3145732
  1.6 15.0 %collective-permute-start = (f32[2,32,16,8]{3,2,1,0:T(8,128)S(1)}, f32[2,32,16,8]{3,2,1,0:T(8,128)S(1)}, u32[]{:S(2)}, u32[]{:S(2)}) collective-permute-start(f32[2,32,16,8]{3,2,1,0:T(8,128)S(1)} %get-tuple-element.5), channel_id=1, source_target_pairs={{1,0},{2,1},{3,2},{4,3},{5,4},{6,5},{7,6},{0,7},{9,8},{10,9},{11,1... | collective-permute-start | bytes 98312 | tf_op jit(solution)/shard_map/ppermute | solution.py:21
  5.9 14.6 %collective-permute-start.1 = (f32[2,32,16,8]{3,2,1,0:T(8,128)S(1)}, f32[2,32,16,8]{3,2,1,0:T(8,128)S(1)}, u32[]{:S(2)}, u32[]{:S(2)}) collective-permute-start(f32[2,32,16,8]{3,2,1,0:T(8,128)S(1)} %get-tuple-element.6), channel_id=1, source_target_pairs={{7,0},{0,1},{1,2},{2,3},{3,4},{4,5},{5,6},{6,7},{15,8},{8,9},{9,10... | collective-permute-start | bytes 98312 | tf_op jit(solution)/shard_map/ppermute | solution.py:21
  22.2 34.0 %collective-permute-start.2 = (f32[2,32,8,640]{3,2,1,0:T(8,128)}, f32[2,32,8,640]{3,2,1,0:T(8,128)}, u32[]{:S(2)}, u32[]{:S(2)}) collective-permute-start(f32[2,32,8,640]{3,2,1,0:T(8,128)} %pad_maximum_fusion.1), channel_id=1, source_target_pairs={{8,0},{16,8},{24,16},{32,24},{40,32},{48,40},{56,48},{64,56},{72,6... | collective-permute-start | bytes 3932168 | tf_op jit(solution)/shard_map/ppermute | solution.py:21
  25.1 31.0 %collective-permute-start.3 = (f32[2,32,8,640]{3,2,1,0:T(8,128)}, f32[2,32,8,640]{3,2,1,0:T(8,128)}, u32[]{:S(2)}, u32[]{:S(2)}) collective-permute-start(f32[2,32,8,640]{3,2,1,0:T(8,128)} %fusion), channel_id=1, source_target_pairs={{248,0},{0,8},{8,16},{16,24},{24,32},{32,40},{40,48},{48,56},{56,6... | collective-permute-start | bytes 3932168 | tf_op jit(solution)/shard_map/ppermute | solution.py:21

commit v7 on v6

--- a/solution.py
+++ b/solution.py
@@ -32,10 +32,21 @@
         [jnp.zeros((1, planes, rows, gap), noisy.dtype), jnp.ones((1, planes, rows, gap), noisy.dtype)], 0
     )
     tail = jnp.concatenate([right, filler, left], 3)
-    first = jnp.concatenate([both[:, :, :HALO, :], tail[:, :, :HALO, :]], 3)
-    last = jnp.concatenate([both[:, :, rows - HALO:, :], tail[:, :, rows - HALO:, :]], 3)
-    below = from_offset(first, "gx", 1)
-    above = from_offset(last, "gx", -1)
+    sides = jnp.concatenate([right, left], 3)
+
+    def pack(band):
+        edge, corner = both[:, :, band, :], sides[:, :, band, :]
+        return jnp.concatenate([edge.reshape(2, planes * HALO, cols), corner.reshape(2, -1, cols)], 1)
+
+    def unpack(slab):
+        edge = slab[:, : planes * HALO].reshape(2, planes, HALO, cols)
+        corner = slab[:, planes * HALO :].reshape(2, planes, HALO, 2 * HALO)
+        after, before = corner[..., :HALO], corner[..., HALO:]
+        band_filler = filler[:, :, :HALO, :]
+        return edge, jnp.concatenate([after, band_filler, before], 3)
+
+    below = unpack(from_offset(pack(slice(0, HALO)), "gx", 1))
+    above = unpack(from_offset(pack(slice(rows - HALO, rows)), "gx", -1))
     return tail, below, above, width
 
 
@@ -43,7 +54,8 @@
 
 
 def iterate_kernel(
-    own_noisy_ref, own_weight_ref, tail_ref, below_ref, above_ref, step_x_ref, step_y_ref, out_ref,
+    own_noisy_ref, own_weight_ref, tail_ref, below_ref, below_tail_ref, above_ref, above_tail_ref,
+    step_x_ref, step_y_ref, out_ref,
     noisy_ref, weight_ref, primal, extrapolated, dual_x, dual_y, dual_z, pulled,
 ):
     planes, rows, width = noisy_ref.shape
@@ -56,8 +68,10 @@
         for field, own_ref, part in ((noisy_ref, own_noisy_ref, 0), (weight_ref, own_weight_ref, 1)):
             field[z, pl.ds(0, own_rows), pl.ds(0, own_cols)] = own_ref[z]
             field[z, pl.ds(0, own_rows), pl.ds(own_cols, width - own_cols)] = tail_ref[part, z]
-            field[z, pl.ds(own_rows, halo)] = below_ref[part, z]
-            field[z, pl.ds(own_rows + halo, halo)] = above_ref[part, z]
+            for offset, (edge_ref, corner_ref) in ((own_rows, (below_ref, below_tail_ref)),
+                                                   (own_rows + halo, (above_ref, above_tail_ref))):
+                field[z, pl.ds(offset, halo), pl.ds(0, own_cols)] = edge_ref[part, z]
+                field[z, pl.ds(offset, halo), pl.ds(own_cols, width - own_cols)] = corner_ref[part, z]
         noisy = noisy_ref[z]
         primal[z] = noisy
         extrapolated[z] = noisy
@@ -139,11 +153,11 @@
     return pl.pallas_call(
         iterate_kernel,
         out_shape=jax.ShapeDtypeStruct(noisy.shape, jnp.float32),
-        in_specs=[vmem] * 7,
+        in_specs=[vmem] * 9,
         out_specs=vmem,
         scratch_shapes=[pltpu.VMEM(field.shape, jnp.float32)] * 8,
         compiler_params=pltpu.CompilerParams(vmem_limit_bytes=48 * 1024 * 1024),
-    )(noisy, weight, tail, below, above, step_x, step_y)
+    )(noisy, weight, tail, *below, *above, step_x, step_y)
 
 
 def solution(mesh):

time: 114 us -> 115 us (level)
  waiting for transfers between devices: 43 us -> 35.5 us
  local copies, waits for them, and re-layouts: 0.16 us -> 5.97 us
  other arithmetic: 4.32 us -> 8.89 us
  Pallas kernels: 57.4 us -> 55.7 us
    ppermute x4, waiting for transfers between devices: 43 us -> 35.5 us  [from_offset(): lax.ppermute(value, axis, [((dest + offset) % count, dest) for dest in ra...]
    reshape x0 -> x6, local copies, waits for them, and re-layouts: none -> 4.1 us  [the longest x2 2.6 us: unpack(): edge = slab[:, :planes * HALO].reshape(2, planes, HALO, cols)]
    concatenate x2 -> x4, other arithmetic: 2.32 us -> 4.59 us  [the longest x2 3.39 us: pack(): jnp.concatenate([edge.reshape(2, planes * HALO, cols), corner.reshape(2,...]
    slice x1 -> x4, local copies, waits for them, and re-layouts: 0.04 us -> 1.74 us  [the longest x2 1.52 us: unpack(): corner = slab[:, planes * HALO:].reshape(2, planes, HALO, 2 * HALO)]
    pallas_call x1, Pallas kernels: 57.4 us -> 55.7 us  [per_device(): pl.pallas_call(iterate_kernel, out_shape=jax.ShapeDtypeStruct(noisy.shape...]
    concatenate x1, other arithmetic: 0.34 us -> 1.54 us  [extend(): tail = jnp.concatenate([right, filler, left], 3)]
    reshape x0 -> x1, other arithmetic: none -> 1.2 us  [pack(): edge.reshape(2, planes * HALO, cols)]
  transfers between devices with their start and end apart: 4 -> 4, of which waited for: 3 -> 3; matrix products, arithmetic and copies ran while one was open for 1% -> 4% of each run, Pallas kernels for 0% -> 0%
where the time goes in v7:
time: 115 us
  Pallas kernels  55.7 us (48%)
  waiting for transfers between devices  35.5 us (31%)
  other arithmetic  8.89 us (8%)
  starting transfers between devices  8.71 us (8%)
  local copies, waits for them, and re-layouts  5.97 us (5%)
    pallas_call x1, Pallas kernels, per_device(): pl.pallas_call(iterate_kernel, out_shape=jax.ShapeDtypeStruct(noisy.shape...  55.7 us
    ppermute x4, waiting for transfers between devices, from_offset(): lax.ppermute(value, axis, [((dest + offset) % count, dest) for dest in ra...  35.5 us
    ppermute x4, starting transfers between devices, from_offset(): lax.ppermute(value, axis, [((dest + offset) % count, dest) for dest in ra...  8.71 us
    concatenate x2, other arithmetic, pack(): jnp.concatenate([edge.reshape(2, planes * HALO, cols), corner.reshape(2,...  3.39 us
    reshape x2, local copies, waits for them, and re-layouts, unpack(): edge = slab[:, :planes * HALO].reshape(2, planes, HALO, cols)  2.6 us
  transfers between devices with their start and end apart: 4, of which 3 were waited for; matrix products, arithmetic and copies ran while one was open for 4% of the time, Pallas kernels for 0%

profile of v7, /device:TPU:1, one launch (start us, length us, event | category | flops | bytes accessed | tf_op | source)
XLA Modules:
  0.0 114.8 jit_solution(551289563965141922)
XLA Ops:
  0.0 0.0 copy-start
  0.0 0.0 copy-start.1
  0.0 1.6 %fusion.3 = (f32[2,32,16,8]{3,2,1,0:T(8,128)S(1)}, f32[2,32,16,8]{3,2,1,0:T(8,128)S(1)}) fusion(f32[1,32,16,512]{3,2,1,0:T(8,128)} %bitcast.14, f32[1,32,16,512]{3,2,1,0:T(8,128)} %bitcast.16), kind=kLoop, calls=%fused_computation.14 | loop fusion | flops 16384 | bytes 2162688 | tf_op jit(solution)/shard_map/stack | solution.py:27
  1.6 4.4 %collective-permute-start = (f32[2,32,16,8]{3,2,1,0:T(8,128)S(1)}, f32[2,32,16,8]{3,2,1,0:T(8,128)S(1)}, u32[]{:S(2)}, u32[]{:S(2)}) collective-permute-start(f32[2,32,16,8]{3,2,1,0:T(8,128)S(1)} %get-tuple-element.7), channel_id=1, source_target_pairs={{1,0},{2,1},{3,2},{4,3},{5,4},{6,5},{7,6},{0,7},{9,8},{10,9},{11,1... | collective-permute-start | bytes 98312 | tf_op jit(solution)/shard_map/ppermute | solution.py:21
  5.9 0.0 collective-permute-start.1
  5.9 0.0 copy-done
  6.0 0.0 copy-done.1
  6.0 1.2 %fusion.2 = (f32[2,256,512]{2,1,0:T(8,128)S(1)}, f32[2,256,512]{2,1,0:T(8,128)}) fusion(f32[1,32,16,512]{3,2,1,0:T(8,128)S(1)} %bitcast.17, f32[1,32,16,512]{3,2,1,0:T(8,128)S(1)} %bitcast.15), kind=kLoop, calls=%fused_computation.12 | loop fusion | flops 524288 | bytes 4194304 | tf_op jit(solution)/shard_map/reshape | solution.py:39
  7.2 9.4 %collective-permute-done = f32[2,32,16,8]{3,2,1,0:T(8,128)S(1)} collective-permute-done((f32[2,32,16,8]{3,2,1,0:T(8,128)S(1)}, f32[2,32,16,8]{3,2,1,0:T(8,128)S(1)}, u32[]{:S(2)}, u32[]{:S(2)}) %collective-permute-start) | collective-permute-done | bytes 32800 | tf_op jit(solution)/shard_map/ppermute | solution.py:21
  16.6 0.0 copy-start.2
  16.6 4.0 %collective-permute-done.1 = f32[2,32,16,8]{3,2,1,0:T(8,128)S(1)} collective-permute-done((f32[2,32,16,8]{3,2,1,0:T(8,128)S(1)}, f32[2,32,16,8]{3,2,1,0:T(8,128)S(1)}, u32[]{:S(2)}, u32[]{:S(2)}) %collective-permute-start.1) | collective-permute-done | bytes 32800 | tf_op jit(solution)/shard_map/ppermute | solution.py:21
  20.6 0.0 copy-done.2
  20.6 0.0 copy-start.3
  20.6 0.9 pad_maximum_fusion.4
  21.5 0.0 copy-done.3
  21.5 1.1 reshape.58
  22.6 0.2 reshape.54
  22.8 2.3 %pad_maximum_fusion = f32[2,264,512]{2,1,0:T(8,128)} fusion(f32[2,8,512]{2,1,0:T(8,128)S(1)} %reshape.54, f32[2,256,512]{2,1,0:T(8,128)} %get-tuple-element.6), kind=kLoop, calls=%fused_computation.6 | loop fusion | flops 270336 | bytes 2162688 | tf_op jit(solution)/shard_map/concatenate | solution.py:39
  25.1 1.8 %collective-permute-start.2 = (f32[2,264,512]{2,1,0:T(8,128)}, f32[2,264,512]{2,1,0:T(8,128)}, u32[]{:S(2)}, u32[]{:S(2)}) collective-permute-start(f32[2,264,512]{2,1,0:T(8,128)} %pad_maximum_fusion), channel_id=1, source_target_pairs={{8,0},{16,8},{24,16},{32,24},{40,32},{48,40},{56,48},{64,56},{72,6... | collective-permute-start | bytes 3244040 | tf_op jit(solution)/shard_map/ppermute | solution.py:21
  26.9 1.1 pad_maximum_fusion.1
  28.0 2.5 %collective-permute-start.3 = (f32[2,264,512]{2,1,0:T(8,128)}, f32[2,264,512]{2,1,0:T(8,128)}, u32[]{:S(2)}, u32[]{:S(2)}) collective-permute-start(f32[2,264,512]{2,1,0:T(8,128)} %pad_maximum_fusion.1), channel_id=1, source_target_pairs={{248,0},{0,8},{8,16},{16,24},{24,32},{32,40},{40,48},{48,56},{56,6... | collective-permute-start | bytes 3244040 | tf_op jit(solution)/shard_map/ppermute | solution.py:21
  30.5 1.5 %pad_maximum_fusion.3.tail_ref = f32[2,32,16,128]{3,2,1,0:T(8,128)S(1)} fusion(f32[2,32,16,8]{3,2,1,0:T(8,128)} %copy-done.3, f32[2,32,16,112]{3,2,1,0:T(8,128)S(1)} %concatenate.21, f32[2,32,16,8]{3,2,1,0:T(8,128)} %copy-done.2), kind=kLoop, calls=%fused_computation.16 | loop fusion | flops 262144 | bytes 1048576 | tf_op jit(solution)/shard_map/concatenate | solution.py:34
  32.1 22.0 %collective-permute-done.2 = f32[2,264,512]{2,1,0:T(8,128)} collective-permute-done((f32[2,264,512]{2,1,0:T(8,128)}, f32[2,264,512]{2,1,0:T(8,128)}, u32[]{:S(2)}, u32[]{:S(2)}) %collective-permute-start.2) | collective-permute-done | bytes 1081376 | tf_op jit(solution)/shard_map/ppermute | solution.py:21
  54.1 0.8 slice.73
  54.9 0.1 reshape.56
  55.0 0.0 collective-permute-done.3
  55.0 0.8 slice.77
  55.8 0.1 reshape.60
  55.9 0.2 fusion.12
  56.1 0.3 pad_maximum_fusion.6
  56.4 1.3 %slice_bitcast_fusion.1.below_ref = f32[2,32,8,512]{3,2,1,0:T(8,128)S(1)} fusion(f32[2,264,512]{2,1,0:T(8,128)} %collective-permute-done.2), kind=kLoop, calls=%fused_computation.13 | loop fusion | bytes 2097152 | tf_op jit(solution)/shard_map/reshape | solution.py:42
  57.7 1.3 %slice_bitcast_fusion.above_ref = f32[2,32,8,512]{3,2,1,0:T(8,128)S(1)} fusion(f32[2,264,512]{2,1,0:T(8,128)} %collective-permute-done.3), kind=kLoop, calls=%fused_computation.10 | loop fusion | bytes 2097152 | tf_op jit(solution)/shard_map/reshape | solution.py:42
  59.0 0.1 broadcast_in_dim.32.step_x_ref
  59.1 55.7 %shard_map.28 = f32[32,16,512]{2,1,0:T(8,128)} custom-call(f32[32,16,512]{2,1,0:T(8,128)S(1)} %copy-done, f32[32,16,512]{2,1,0:T(8,128)S(1)} %copy-done.1, f32[2,32,16,128]{3,2,1,0:T(8,128)S(1)} %pad_maximum_fusion.3.tail_ref, f32[2,32,8,512]{3,2,1,0:T(8,128)S(1)} %slice_bitcast_fusion.1.below_ref, f32[2,32,8,128]{3,2,1,0:T(8,128)S(1)} %get-tuple-element.12.below_tail_ref, ...), custom_call_target="tpu_custom_call" | custom-call | tf_op jit(solution)/shard_map/pallas_call | solution.py:153
  (5 shorter events, 0.1 us)
Async XLA Ops:
  0.0 5.9 %copy-start = (f32[32,16,512]{2,1,0:T(8,128)S(1)}, f32[32,16,512]{2,1,0:T(8,128)}, u32[]{:S(2)}) copy-start(f32[32,16,512]{2,1,0:T(8,128)} %own_noisy_ref.1) | copy-start | bytes 3145732
  0.0 6.0 %copy-start.1 = (f32[32,16,512]{2,1,0:T(8,128)S(1)}, f32[32,16,512]{2,1,0:T(8,128)}, u32[]{:S(2)}) copy-start(f32[32,16,512]{2,1,0:T(8,128)} %own_weight_ref.1) | copy-start | bytes 3145732
  1.6 15.0 %collective-permute-start = (f32[2,32,16,8]{3,2,1,0:T(8,128)S(1)}, f32[2,32,16,8]{3,2,1,0:T(8,128)S(1)}, u32[]{:S(2)}, u32[]{:S(2)}) collective-permute-start(f32[2,32,16,8]{3,2,1,0:T(8,128)S(1)} %get-tuple-element.7), channel_id=1, source_target_pairs={{1,0},{2,1},{3,2},{4,3},{5,4},{6,5},{7,6},{0,7},{9,8},{10,9},{11,1... | collective-permute-start | bytes 98312 | tf_op jit(solution)/shard_map/ppermute | solution.py:21
  5.9 14.6 %collective-permute-start.1 = (f32[2,32,16,8]{3,2,1,0:T(8,128)S(1)}, f32[2,32,16,8]{3,2,1,0:T(8,128)S(1)}, u32[]{:S(2)}, u32[]{:S(2)}) collective-permute-start(f32[2,32,16,8]{3,2,1,0:T(8,128)S(1)} %get-tuple-element.8), channel_id=1, source_target_pairs={{7,0},{0,1},{1,2},{2,3},{3,4},{4,5},{5,6},{6,7},{15,8},{8,9},{9,10... | collective-permute-start | bytes 98312 | tf_op jit(solution)/shard_map/ppermute | solution.py:21
  16.6 4.0 %copy-start.2 = (f32[2,32,16,8]{3,2,1,0:T(8,128)}, f32[2,32,16,8]{3,2,1,0:T(8,128)S(1)}, u32[]{:S(2)}) copy-start(f32[2,32,16,8]{3,2,1,0:T(8,128)S(1)} %collective-permute-done) | copy-start | bytes 98308
  20.6 0.9 copy-start.3
  25.1 29.1 %collective-permute-start.2 = (f32[2,264,512]{2,1,0:T(8,128)}, f32[2,264,512]{2,1,0:T(8,128)}, u32[]{:S(2)}, u32[]{:S(2)}) collective-permute-start(f32[2,264,512]{2,1,0:T(8,128)} %pad_maximum_fusion), channel_id=1, source_target_pairs={{8,0},{16,8},{24,16},{32,24},{40,32},{48,40},{56,48},{64,56},{72,6... | collective-permute-start | bytes 3244040 | tf_op jit(solution)/shard_map/ppermute | solution.py:21
  28.0 27.0 %collective-permute-start.3 = (f32[2,264,512]{2,1,0:T(8,128)}, f32[2,264,512]{2,1,0:T(8,128)}, u32[]{:S(2)}, u32[]{:S(2)}) collective-permute-start(f32[2,264,512]{2,1,0:T(8,128)} %pad_maximum_fusion.1), channel_id=1, source_target_pairs={{248,0},{0,8},{8,16},{16,24},{24,32},{32,40},{40,48},{48,56},{56,6... | collective-permute-start | bytes 3244040 | tf_op jit(solution)/shard_map/ppermute | solution.py:21

commit v8 on v6

--- a/solution.py
+++ b/solution.py
@@ -58,13 +58,7 @@
             field[z, pl.ds(0, own_rows), pl.ds(own_cols, width - own_cols)] = tail_ref[part, z]
             field[z, pl.ds(own_rows, halo)] = below_ref[part, z]
             field[z, pl.ds(own_rows + halo, halo)] = above_ref[part, z]
-        noisy = noisy_ref[z]
-        primal[z] = noisy
-        extrapolated[z] = noisy
-        pulled[z] = primal_step * fidelity * noisy
-        dual_x[z] = jnp.zeros_like(noisy)
-        dual_y[z] = jnp.zeros_like(noisy)
-        dual_z[z] = jnp.zeros_like(noisy)
+        pulled[z] = primal_step * fidelity * noisy_ref[z]
         return carry
 
     lax.fori_loop(0, planes, setup, 0)
@@ -72,20 +66,26 @@
     last_lane = lane == LANES - 1
     first_lane = lane == 0
 
-    def plane(z, carry):
+    def plane(z, carry, first=False):
+        start = noisy_ref if first else extrapolated
+        begun = noisy_ref if first else primal
+
+        def dual(ref, index, cols):
+            return jnp.zeros((rows, LANES), jnp.float32) if first else ref[index, :, cols]
+
         after = jnp.minimum(z + 1, planes - 1)
         before = jnp.maximum(z - 1, 0)
         step_z = jnp.where(z < planes - 1, dual_step, 0.0)
-        turned = [pltpu.roll(extrapolated[z, :, pl.ds(block * LANES, LANES)], LANES - 1, 1) for block in range(blocks)]
+        turned = [pltpu.roll(start[z, :, pl.ds(block * LANES, LANES)], LANES - 1, 1) for block in range(blocks)]
         for block in range(blocks):
             cols = pl.ds(block * LANES, LANES)
-            here = extrapolated[z, :, cols]
+            here = start[z, :, cols]
             next_y = jnp.where(last_lane, turned[(block + 1) % blocks], turned[block])
             next_x = pltpu.roll(here, rows - 1, 0)
             new_x, new_y, new_z = project(
-                dual_x[z, :, cols] + step_x_ref[:, cols] * (next_x - here),
-                dual_y[z, :, cols] + step_y_ref[:, cols] * (next_y - here),
-                dual_z[z, :, cols] + step_z * (extrapolated[after, :, cols] - here),
+                dual(dual_x, z, cols) + step_x_ref[:, cols] * (next_x - here),
+                dual(dual_y, z, cols) + step_y_ref[:, cols] * (next_y - here),
+                dual(dual_z, z, cols) + step_z * (start[after, :, cols] - here),
                 weight_ref[z, :, cols],
             )
             dual_x[z, :, cols] = new_x
@@ -99,13 +99,14 @@
             prev_y = jnp.where(first_lane, turned[(block - 1) % blocks], turned[block])
             prev_z = jnp.where(z > 0, dual_z[before, :, cols], 0.0)
             divergence = (new_x - pltpu.roll(new_x, 1, 0)) + (new_y - prev_y) + (dual_z[z, :, cols] - prev_z)
-            old = primal[z, :, cols]
+            old = begun[z, :, cols]
             updated = (old + primal_step * divergence + pulled[z, :, cols]) * shrink
             extrapolated[z, :, cols] = 2.0 * updated - old
             primal[z, :, cols] = updated
         return carry
 
-    for iteration in range(ITERS):
+    lax.fori_loop(0, planes, functools.partial(plane, first=True), 0)
+    for iteration in range(1, ITERS):
         lax.fori_loop(0, planes, plane, 0)
     out_ref[...] = primal[:, :own_rows, :own_cols]
 

time: 114 us -> 113 us (level)
  no operation moved by 1% of the time
where the time goes in v8:
time: 113 us
  Pallas kernels  56.7 us (50%)
  waiting for transfers between devices  43 us (38%)
  starting transfers between devices  8.71 us (8%)
  other arithmetic  4.32 us (4%)
    pallas_call x1, Pallas kernels, per_device(): pl.pallas_call(iterate_kernel, out_shape=jax.ShapeDtypeStruct(noisy.shape...  56.7 us
    ppermute x4, waiting for transfers between devices, from_offset(): lax.ppermute(value, axis, [((dest + offset) % count, dest) for dest in ra...  43 us
    ppermute x4, starting transfers between devices, from_offset(): lax.ppermute(value, axis, [((dest + offset) % count, dest) for dest in ra...  8.71 us
  transfers between devices with their start and end apart: 4, of which 3 were waited for; matrix products, arithmetic and copies ran while one was open for 1% of the time, Pallas kernels for 0%

profile of v8, /device:TPU:1, one launch (start us, length us, event | category | flops | bytes accessed | tf_op | source)
XLA Modules:
  0.0 112.9 jit_solution(3052047585039851625)
XLA Ops:
  0.0 0.0 copy-start
  0.0 0.0 copy-start.1
  0.0 1.6 %fusion.2 = (f32[2,32,16,8]{3,2,1,0:T(8,128)S(1)}, f32[2,32,16,8]{3,2,1,0:T(8,128)S(1)}) fusion(f32[1,32,16,512]{3,2,1,0:T(8,128)} %bitcast.2, f32[1,32,16,512]{3,2,1,0:T(8,128)} %bitcast.5), kind=kLoop, calls=%fused_computation.10 | loop fusion | flops 16384 | bytes 2162688 | tf_op jit(solution)/shard_map/stack | solution.py:27
  1.6 4.4 %collective-permute-start = (f32[2,32,16,8]{3,2,1,0:T(8,128)S(1)}, f32[2,32,16,8]{3,2,1,0:T(8,128)S(1)}, u32[]{:S(2)}, u32[]{:S(2)}) collective-permute-start(f32[2,32,16,8]{3,2,1,0:T(8,128)S(1)} %get-tuple-element.5), channel_id=1, source_target_pairs={{1,0},{2,1},{3,2},{4,3},{5,4},{6,5},{7,6},{0,7},{9,8},{10,9},{11,1... | collective-permute-start | bytes 98312 | tf_op jit(solution)/shard_map/ppermute | solution.py:21
  5.9 0.0 collective-permute-start.1
  5.9 0.0 copy-done
  6.0 0.0 copy-done.1
  6.0 0.1 fusion.1
  6.1 10.5 %collective-permute-done = f32[2,32,16,8]{3,2,1,0:T(8,128)S(1)} collective-permute-done((f32[2,32,16,8]{3,2,1,0:T(8,128)S(1)}, f32[2,32,16,8]{3,2,1,0:T(8,128)S(1)}, u32[]{:S(2)}, u32[]{:S(2)}) %collective-permute-start) | collective-permute-done | bytes 32800 | tf_op jit(solution)/shard_map/ppermute | solution.py:21
  16.6 4.0 %collective-permute-done.1 = f32[2,32,16,8]{3,2,1,0:T(8,128)S(1)} collective-permute-done((f32[2,32,16,8]{3,2,1,0:T(8,128)S(1)}, f32[2,32,16,8]{3,2,1,0:T(8,128)S(1)}, u32[]{:S(2)}, u32[]{:S(2)}) %collective-permute-start.1) | collective-permute-done | bytes 32800 | tf_op jit(solution)/shard_map/ppermute | solution.py:21
  20.6 0.3 pad_maximum_fusion.2.tail_ref
  21.0 1.2 %pad_maximum_fusion.1 = f32[2,32,8,640]{3,2,1,0:T(8,128)} fusion(f32[2,32,8,128]{3,2,1,0:T(8,128)S(1)} %get-tuple-element.8, f32[2,32,8,512]{3,2,1,0:T(8,128)S(1)} %fusion.1), kind=kLoop, calls=%fused_computation.8 | loop fusion | flops 327680 | bytes 2621440 | tf_op jit(solution)/shard_map/concatenate | solution.py:35
  22.2 1.8 %collective-permute-start.2 = (f32[2,32,8,640]{3,2,1,0:T(8,128)}, f32[2,32,8,640]{3,2,1,0:T(8,128)}, u32[]{:S(2)}, u32[]{:S(2)}) collective-permute-start(f32[2,32,8,640]{3,2,1,0:T(8,128)} %pad_maximum_fusion.1), channel_id=1, source_target_pairs={{8,0},{16,8},{24,16},{32,24},{40,32},{48,40},{56,48},{64,56},{72,6... | collective-permute-start | bytes 3932168 | tf_op jit(solution)/shard_map/ppermute | solution.py:21
  24.0 1.2 %fusion = f32[2,32,8,640]{3,2,1,0:T(8,128)} fusion(f32[1,32,16,512]{3,2,1,0:T(8,128)S(1)} %bitcast.7, f32[1,32,16,512]{3,2,1,0:T(8,128)S(1)} %bitcast.4, f32[2,32,8,128]{3,2,1,0:T(8,128)S(1)} %get-tuple-element.7), kind=kLoop, calls=%fused_computation.7 | loop fusion | flops 655360 | bytes 3670016 | tf_op jit(solution)/shard_map/concatenate | solution.py:36
  25.1 2.5 %collective-permute-start.3 = (f32[2,32,8,640]{3,2,1,0:T(8,128)}, f32[2,32,8,640]{3,2,1,0:T(8,128)}, u32[]{:S(2)}, u32[]{:S(2)}) collective-permute-start(f32[2,32,8,640]{3,2,1,0:T(8,128)} %fusion), channel_id=1, source_target_pairs={{248,0},{0,8},{8,16},{16,24},{24,32},{32,40},{40,48},{48,56},{56,6... | collective-permute-start | bytes 3932168 | tf_op jit(solution)/shard_map/ppermute | solution.py:21
  27.7 28.5 %collective-permute-done.2.below_ref = f32[2,32,8,640]{3,2,1,0:T(8,128)} collective-permute-done((f32[2,32,8,640]{3,2,1,0:T(8,128)}, f32[2,32,8,640]{3,2,1,0:T(8,128)}, u32[]{:S(2)}, u32[]{:S(2)}) %collective-permute-start.2) | collective-permute-done | bytes 1310752 | tf_op jit(solution)/shard_map/ppermute | solution.py:21
  56.1 0.0 collective-permute-done.3.above_ref
  56.2 0.1 broadcast_in_dim.32.step_x_ref
  56.2 56.7 %shard_map.28 = f32[32,16,512]{2,1,0:T(8,128)} custom-call(f32[32,16,512]{2,1,0:T(8,128)S(1)} %copy-done, f32[32,16,512]{2,1,0:T(8,128)S(1)} %copy-done.1, f32[2,32,16,128]{3,2,1,0:T(8,128)S(1)} %pad_maximum_fusion.2.tail_ref, f32[2,32,8,640]{3,2,1,0:T(8,128)} %collective-permute-done.2.below_ref, f32[2,32,8,640]{3,2,1,0:T(8,128)} %collective-permute-done.3.above_ref, ...), custom_call_target="tpu_custom_call" | custom-call | tf_op jit(solution)/shard_map/pallas_call | solution.py:140
  (5 shorter events, 0.1 us)
Async XLA Ops:
  0.0 6.0 %copy-start = (f32[32,16,512]{2,1,0:T(8,128)S(1)}, f32[32,16,512]{2,1,0:T(8,128)}, u32[]{:S(2)}) copy-start(f32[32,16,512]{2,1,0:T(8,128)} %own_noisy_ref.1) | copy-start | bytes 3145732
  0.0 6.0 %copy-start.1 = (f32[32,16,512]{2,1,0:T(8,128)S(1)}, f32[32,16,512]{2,1,0:T(8,128)}, u32[]{:S(2)}) copy-start(f32[32,16,512]{2,1,0:T(8,128)} %own_weight_ref.1) | copy-start | bytes 3145732
  1.6 15.0 %collective-permute-start = (f32[2,32,16,8]{3,2,1,0:T(8,128)S(1)}, f32[2,32,16,8]{3,2,1,0:T(8,128)S(1)}, u32[]{:S(2)}, u32[]{:S(2)}) collective-permute-start(f32[2,32,16,8]{3,2,1,0:T(8,128)S(1)} %get-tuple-element.5), channel_id=1, source_target_pairs={{1,0},{2,1},{3,2},{4,3},{5,4},{6,5},{7,6},{0,7},{9,8},{10,9},{11,1... | collective-permute-start | bytes 98312 | tf_op jit(solution)/shard_map/ppermute | solution.py:21
  5.9 14.6 %collective-permute-start.1 = (f32[2,32,16,8]{3,2,1,0:T(8,128)S(1)}, f32[2,32,16,8]{3,2,1,0:T(8,128)S(1)}, u32[]{:S(2)}, u32[]{:S(2)}) collective-permute-start(f32[2,32,16,8]{3,2,1,0:T(8,128)S(1)} %get-tuple-element.6), channel_id=1, source_target_pairs={{7,0},{0,1},{1,2},{2,3},{3,4},{4,5},{5,6},{6,7},{15,8},{8,9},{9,10... | collective-permute-start | bytes 98312 | tf_op jit(solution)/shard_map/ppermute | solution.py:21
  22.2 34.0 %collective-permute-start.2 = (f32[2,32,8,640]{3,2,1,0:T(8,128)}, f32[2,32,8,640]{3,2,1,0:T(8,128)}, u32[]{:S(2)}, u32[]{:S(2)}) collective-permute-start(f32[2,32,8,640]{3,2,1,0:T(8,128)} %pad_maximum_fusion.1), channel_id=1, source_target_pairs={{8,0},{16,8},{24,16},{32,24},{40,32},{48,40},{56,48},{64,56},{72,6... | collective-permute-start | bytes 3932168 | tf_op jit(solution)/shard_map/ppermute | solution.py:21
  25.1 31.0 %collective-permute-start.3 = (f32[2,32,8,640]{3,2,1,0:T(8,128)}, f32[2,32,8,640]{3,2,1,0:T(8,128)}, u32[]{:S(2)}, u32[]{:S(2)}) collective-permute-start(f32[2,32,8,640]{3,2,1,0:T(8,128)} %fusion), channel_id=1, source_target_pairs={{248,0},{0,8},{8,16},{16,24},{24,32},{32,40},{40,48},{48,56},{56,6... | collective-permute-start | bytes 3932168 | tf_op jit(solution)/shard_map/ppermute | solution.py:21

commit v9 on v8

--- a/solution.py
+++ b/solution.py
@@ -66,7 +66,7 @@
     last_lane = lane == LANES - 1
     first_lane = lane == 0
 
-    def plane(z, carry, first=False):
+    def plane(z, carry, first=False, last=False):
         start = noisy_ref if first else extrapolated
         begun = noisy_ref if first else primal
 
@@ -92,7 +92,7 @@
             dual_y[z, :, cols] = new_y
             dual_z[z, :, cols] = new_z
         turned = [pltpu.roll(dual_y[z, :, pl.ds(block * LANES, LANES)], 1, 1) for block in range(blocks)]
-        for block in range(blocks):
+        for block in range(own_cols // LANES if last else blocks):
             cols = pl.ds(block * LANES, LANES)
             new_x = dual_x[z, :, cols]
             new_y = dual_y[z, :, cols]
@@ -101,14 +101,17 @@
             divergence = (new_x - pltpu.roll(new_x, 1, 0)) + (new_y - prev_y) + (dual_z[z, :, cols] - prev_z)
             old = begun[z, :, cols]
             updated = (old + primal_step * divergence + pulled[z, :, cols]) * shrink
+            if last:
+                out_ref[z, :, cols] = updated[:own_rows]
+                continue
             extrapolated[z, :, cols] = 2.0 * updated - old
             primal[z, :, cols] = updated
         return carry
 
     lax.fori_loop(0, planes, functools.partial(plane, first=True), 0)
-    for iteration in range(1, ITERS):
+    for iteration in range(1, ITERS - 1):
         lax.fori_loop(0, planes, plane, 0)
-    out_ref[...] = primal[:, :own_rows, :own_cols]
+    lax.fori_loop(0, planes, functools.partial(plane, last=True), 0)
 
 
 def project(dual_x, dual_y, dual_z, weight):

time: 113 us -> 112 us (level)
  no operation moved by 1% of the time
where the time goes in v9:
time: 112 us
  Pallas kernels  56.1 us (50%)
  waiting for transfers between devices  43 us (38%)
  starting transfers between devices  8.71 us (8%)
  other arithmetic  4.32 us (4%)
    pallas_call x1, Pallas kernels, per_device(): pl.pallas_call(iterate_kernel, out_shape=jax.ShapeDtypeStruct(noisy.shape...  56.1 us
    ppermute x4, waiting for transfers between devices, from_offset(): lax.ppermute(value, axis, [((dest + offset) % count, dest) for dest in ra...  43 us
    ppermute x4, starting transfers between devices, from_offset(): lax.ppermute(value, axis, [((dest + offset) % count, dest) for dest in ra...  8.71 us
  transfers between devices with their start and end apart: 4, of which 3 were waited for; matrix products, arithmetic and copies ran while one was open for 1% of the time, Pallas kernels for 0%

profile of v9, /device:TPU:1, one launch (start us, length us, event | category | flops | bytes accessed | tf_op | source)
XLA Modules:
  0.0 112.3 jit_solution(14027700008768118801)
XLA Ops:
  0.0 0.0 copy-start
  0.0 0.0 copy-start.1
  0.0 1.6 %fusion.2 = (f32[2,32,16,8]{3,2,1,0:T(8,128)S(1)}, f32[2,32,16,8]{3,2,1,0:T(8,128)S(1)}) fusion(f32[1,32,16,512]{3,2,1,0:T(8,128)} %bitcast.2, f32[1,32,16,512]{3,2,1,0:T(8,128)} %bitcast.5), kind=kLoop, calls=%fused_computation.10 | loop fusion | flops 16384 | bytes 2162688 | tf_op jit(solution)/shard_map/stack | solution.py:27
  1.6 4.4 %collective-permute-start = (f32[2,32,16,8]{3,2,1,0:T(8,128)S(1)}, f32[2,32,16,8]{3,2,1,0:T(8,128)S(1)}, u32[]{:S(2)}, u32[]{:S(2)}) collective-permute-start(f32[2,32,16,8]{3,2,1,0:T(8,128)S(1)} %get-tuple-element.5), channel_id=1, source_target_pairs={{1,0},{2,1},{3,2},{4,3},{5,4},{6,5},{7,6},{0,7},{9,8},{10,9},{11,1... | collective-permute-start | bytes 98312 | tf_op jit(solution)/shard_map/ppermute | solution.py:21
  5.9 0.0 collective-permute-start.1
  5.9 0.0 copy-done
  6.0 0.0 copy-done.1
  6.0 0.1 fusion.1
  6.1 10.5 %collective-permute-done = f32[2,32,16,8]{3,2,1,0:T(8,128)S(1)} collective-permute-done((f32[2,32,16,8]{3,2,1,0:T(8,128)S(1)}, f32[2,32,16,8]{3,2,1,0:T(8,128)S(1)}, u32[]{:S(2)}, u32[]{:S(2)}) %collective-permute-start) | collective-permute-done | bytes 32800 | tf_op jit(solution)/shard_map/ppermute | solution.py:21
  16.6 4.0 %collective-permute-done.1 = f32[2,32,16,8]{3,2,1,0:T(8,128)S(1)} collective-permute-done((f32[2,32,16,8]{3,2,1,0:T(8,128)S(1)}, f32[2,32,16,8]{3,2,1,0:T(8,128)S(1)}, u32[]{:S(2)}, u32[]{:S(2)}) %collective-permute-start.1) | collective-permute-done | bytes 32800 | tf_op jit(solution)/shard_map/ppermute | solution.py:21
  20.6 0.3 pad_maximum_fusion.2.tail_ref
  21.0 1.2 %pad_maximum_fusion.1 = f32[2,32,8,640]{3,2,1,0:T(8,128)} fusion(f32[2,32,8,128]{3,2,1,0:T(8,128)S(1)} %get-tuple-element.8, f32[2,32,8,512]{3,2,1,0:T(8,128)S(1)} %fusion.1), kind=kLoop, calls=%fused_computation.8 | loop fusion | flops 327680 | bytes 2621440 | tf_op jit(solution)/shard_map/concatenate | solution.py:35
  22.2 1.8 %collective-permute-start.2 = (f32[2,32,8,640]{3,2,1,0:T(8,128)}, f32[2,32,8,640]{3,2,1,0:T(8,128)}, u32[]{:S(2)}, u32[]{:S(2)}) collective-permute-start(f32[2,32,8,640]{3,2,1,0:T(8,128)} %pad_maximum_fusion.1), channel_id=1, source_target_pairs={{8,0},{16,8},{24,16},{32,24},{40,32},{48,40},{56,48},{64,56},{72,6... | collective-permute-start | bytes 3932168 | tf_op jit(solution)/shard_map/ppermute | solution.py:21
  24.0 1.2 %fusion = f32[2,32,8,640]{3,2,1,0:T(8,128)} fusion(f32[1,32,16,512]{3,2,1,0:T(8,128)S(1)} %bitcast.7, f32[1,32,16,512]{3,2,1,0:T(8,128)S(1)} %bitcast.4, f32[2,32,8,128]{3,2,1,0:T(8,128)S(1)} %get-tuple-element.7), kind=kLoop, calls=%fused_computation.7 | loop fusion | flops 655360 | bytes 3670016 | tf_op jit(solution)/shard_map/concatenate | solution.py:36
  25.1 2.5 %collective-permute-start.3 = (f32[2,32,8,640]{3,2,1,0:T(8,128)}, f32[2,32,8,640]{3,2,1,0:T(8,128)}, u32[]{:S(2)}, u32[]{:S(2)}) collective-permute-start(f32[2,32,8,640]{3,2,1,0:T(8,128)} %fusion), channel_id=1, source_target_pairs={{248,0},{0,8},{8,16},{16,24},{24,32},{32,40},{40,48},{48,56},{56,6... | collective-permute-start | bytes 3932168 | tf_op jit(solution)/shard_map/ppermute | solution.py:21
  27.7 28.5 %collective-permute-done.2.below_ref = f32[2,32,8,640]{3,2,1,0:T(8,128)} collective-permute-done((f32[2,32,8,640]{3,2,1,0:T(8,128)}, f32[2,32,8,640]{3,2,1,0:T(8,128)}, u32[]{:S(2)}, u32[]{:S(2)}) %collective-permute-start.2) | collective-permute-done | bytes 1310752 | tf_op jit(solution)/shard_map/ppermute | solution.py:21
  56.1 0.0 collective-permute-done.3.above_ref
  56.2 0.1 broadcast_in_dim.32.step_x_ref
  56.2 56.1 %shard_map.28 = f32[32,16,512]{2,1,0:T(8,128)} custom-call(f32[32,16,512]{2,1,0:T(8,128)S(1)} %copy-done, f32[32,16,512]{2,1,0:T(8,128)S(1)} %copy-done.1, f32[2,32,16,128]{3,2,1,0:T(8,128)S(1)} %pad_maximum_fusion.2.tail_ref, f32[2,32,8,640]{3,2,1,0:T(8,128)} %collective-permute-done.2.below_ref, f32[2,32,8,640]{3,2,1,0:T(8,128)} %collective-permute-done.3.above_ref, ...), custom_call_target="tpu_custom_call" | custom-call | tf_op jit(solution)/shard_map/pallas_call | solution.py:143
  (5 shorter events, 0.1 us)
Async XLA Ops:
  0.0 6.0 %copy-start = (f32[32,16,512]{2,1,0:T(8,128)S(1)}, f32[32,16,512]{2,1,0:T(8,128)}, u32[]{:S(2)}) copy-start(f32[32,16,512]{2,1,0:T(8,128)} %own_noisy_ref.1) | copy-start | bytes 3145732
  0.0 6.0 %copy-start.1 = (f32[32,16,512]{2,1,0:T(8,128)S(1)}, f32[32,16,512]{2,1,0:T(8,128)}, u32[]{:S(2)}) copy-start(f32[32,16,512]{2,1,0:T(8,128)} %own_weight_ref.1) | copy-start | bytes 3145732
  1.6 15.0 %collective-permute-start = (f32[2,32,16,8]{3,2,1,0:T(8,128)S(1)}, f32[2,32,16,8]{3,2,1,0:T(8,128)S(1)}, u32[]{:S(2)}, u32[]{:S(2)}) collective-permute-start(f32[2,32,16,8]{3,2,1,0:T(8,128)S(1)} %get-tuple-element.5), channel_id=1, source_target_pairs={{1,0},{2,1},{3,2},{4,3},{5,4},{6,5},{7,6},{0,7},{9,8},{10,9},{11,1... | collective-permute-start | bytes 98312 | tf_op jit(solution)/shard_map/ppermute | solution.py:21
  5.9 14.6 %collective-permute-start.1 = (f32[2,32,16,8]{3,2,1,0:T(8,128)S(1)}, f32[2,32,16,8]{3,2,1,0:T(8,128)S(1)}, u32[]{:S(2)}, u32[]{:S(2)}) collective-permute-start(f32[2,32,16,8]{3,2,1,0:T(8,128)S(1)} %get-tuple-element.6), channel_id=1, source_target_pairs={{7,0},{0,1},{1,2},{2,3},{3,4},{4,5},{5,6},{6,7},{15,8},{8,9},{9,10... | collective-permute-start | bytes 98312 | tf_op jit(solution)/shard_map/ppermute | solution.py:21
  22.2 34.0 %collective-permute-start.2 = (f32[2,32,8,640]{3,2,1,0:T(8,128)}, f32[2,32,8,640]{3,2,1,0:T(8,128)}, u32[]{:S(2)}, u32[]{:S(2)}) collective-permute-start(f32[2,32,8,640]{3,2,1,0:T(8,128)} %pad_maximum_fusion.1), channel_id=1, source_target_pairs={{8,0},{16,8},{24,16},{32,24},{40,32},{48,40},{56,48},{64,56},{72,6... | collective-permute-start | bytes 3932168 | tf_op jit(solution)/shard_map/ppermute | solution.py:21
  25.1 31.0 %collective-permute-start.3 = (f32[2,32,8,640]{3,2,1,0:T(8,128)}, f32[2,32,8,640]{3,2,1,0:T(8,128)}, u32[]{:S(2)}, u32[]{:S(2)}) collective-permute-start(f32[2,32,8,640]{3,2,1,0:T(8,128)} %fusion), channel_id=1, source_target_pairs={{248,0},{0,8},{8,16},{16,24},{24,32},{32,40},{40,48},{48,56},{56,6... | collective-permute-start | bytes 3932168 | tf_op jit(solution)/shard_map/ppermute | solution.py:21
